TPU v7x, 128 devices: a whole 4x4x4 slice. The times are simulated.
128 devices in a mesh: dp: 16 (over x, y), fsdp: 8 (over z, core).
Axes of the slice: x: 4, y: 4, z: 4, core: 2. Of those that a mesh axis runs over, the one named last changes fastest.
Arguments:
- page_embed: bfloat16 [81920, 2048], P(('dp', 'fsdp')), may hold values from -6 to 6
- page_slot: int32 [81920], P(('dp', 'fsdp')), may hold values from 0 to 10239, as said below
- doc_ids: int32 [128, 640], P(('dp', 'fsdp')), may hold values from 0 to 9, never falling along the last dimension, each value on 1 to 128 neighbouring positions
- qkv_weight: bfloat16 [3, 2048, 1024], P(None, 'fsdp'), may hold values from -0.125 to 0.125
- out_weight: bfloat16 [1024, 2048], P(None, 'fsdp'), may hold values from -0.1875 to 0.1875
- fig_slot: int32 [2048], P(('dp', 'fsdp')), may hold values from 0 to 639
- cap_slot: int32 [2048], P(('dp', 'fsdp')), may hold values from 0 to 639
- logit_scale: float32 [1], replicated, may hold values from 10 to 30
- loss_cotangent: float32 [2048], P(('dp', 'fsdp')), may hold values from 8 to 64
Outputs:
- page_grad: bfloat16 [81920, 2048], P(('dp', 'fsdp'))
- pair_loss: float32 [2048], P(('dp', 'fsdp'))
Inputs may be any that keep to these rules, and one draw needn't show every extreme that they name: page_slot // 640 is the dp index of the owner and page_slot % 640 the slot there; within each group every slot is named by exactly one page; one device sends at most 50 pages to one owner, and every device sends exactly 50 to some owners. `doc_ids`: along a device's slots the document number never falls; each of the 10 documents has 1 to 128 slots, one exactly 128. `fig_slot`: a slot of the pair's own device. `cap_slot`: a slot of the pair's own device.
All inputs are finite; a program needn't handle non-finite values.
Results may differ from a plain program's by a relative error of at most 0.017.
Values may be sent and summed in bfloat16 or wider, within the bound.
No kernel may reach another device: no remote copies, remote signals or barrier semaphores. Data moves between devices by JAX's collectives and lax.ppermute only.
A program may use at most 192 MiB of HBM per device.

v0:
```python
import math

import jax
import jax.numpy as jnp
from jax import lax
from jax.sharding import PartitionSpec as P

HD = 64


EPSILON = 1e-06


def log_total(values, axis):
    return jnp.log(jnp.sum(jnp.exp(values), axis=axis))


def attend(slot_row_block, qkv_mat, out_mat, doc_row):
    row_count = slot_row_block.shape[0]
    query_h = (
        jnp.dot(slot_row_block, qkv_mat[0], preferred_element_type=jnp.float32)
        .astype(jnp.bfloat16)
        .reshape(row_count, -1, HD)
    )
    key_h = (
        jnp.dot(slot_row_block, qkv_mat[1], preferred_element_type=jnp.float32)
        .astype(jnp.bfloat16)
        .reshape(row_count, -1, HD)
    )
    value_h = (
        jnp.dot(slot_row_block, qkv_mat[2], preferred_element_type=jnp.float32)
        .astype(jnp.bfloat16)
        .reshape(row_count, -1, HD)
    )
    scores = jnp.einsum("qhd,khd->hqk", query_h, key_h, preferred_element_type=jnp.float32) * (
        1.0 / math.sqrt(HD)
    )
    same_doc = doc_row[:, None] == doc_row[None, :]
    scores = jnp.where(same_doc[None], scores, -1e30)
    weights = jnp.exp(scores)
    attn_prob = (weights / jnp.sum(weights, axis=2, keepdims=True)).astype(jnp.bfloat16)
    mixed = jnp.einsum("hqk,khd->qhd", attn_prob, value_h, preferred_element_type=jnp.float32)
    mixed = mixed.astype(jnp.bfloat16).reshape(row_count, -1)
    return jnp.dot(mixed, out_mat, preferred_element_type=jnp.float32)


def body(
    page_embed,
    page_slot,
    doc_ids,
    qkv_weight,
    out_weight,
    fig_slot,
    cap_slot,
    logit_scale,
    loss_cotangent,
):
    dp_count = lax.axis_size("dp")
    row_count = page_embed.shape[0]
    feature_width = page_embed.shape[1]
    capacity = 5 * row_count // (4 * dp_count)
    owner_idx = page_slot // row_count
    slot_idx = page_slot % row_count
    onehot = (owner_idx[:, None] == jnp.arange(dp_count)[None, :]).astype(jnp.int32)
    rank_idx = jnp.sum((jnp.cumsum(onehot, axis=0) - onehot) * onehot, axis=1)
    send_rows = (
        jnp.zeros((dp_count, capacity, feature_width), jnp.bfloat16)
        .at[owner_idx, rank_idx]
        .set(page_embed)
    )
    send_ids = (
        jnp.full((dp_count, capacity), row_count, jnp.int32).at[owner_idx, rank_idx].set(slot_idx)
    )
    recv_rows, recv_ids = (
        lax.all_to_all(send_rows, "dp", split_axis=0, concat_axis=0, tiled=True),
        lax.all_to_all(send_ids, "dp", split_axis=0, concat_axis=0, tiled=True),
    )
    flat_ids = recv_ids.reshape(-1)
    slot_row_block = (
        jnp.zeros((row_count, feature_width), jnp.bfloat16)
        .at[flat_ids]
        .set(recv_rows.reshape(-1, feature_width), mode="drop")
    )
    qkv_full, out_full = (
        lax.all_gather(qkv_weight, "fsdp", axis=1, tiled=True),
        lax.all_gather(out_weight, "fsdp", axis=1, tiled=True),
    )
    doc_row = doc_ids[0]

    def branch(inputs):
        return attend(inputs, qkv_full, out_full, doc_row)

    attn_out, pullback = jax.vjp(branch, slot_row_block)
    slot_output = slot_row_block.astype(jnp.float32) + attn_out
    fig_vec = slot_output[fig_slot]
    cap_vec = slot_output[cap_slot]
    fig_inv = lax.rsqrt(jnp.sum(fig_vec * fig_vec, axis=1, keepdims=True) + EPSILON)
    cap_inv = lax.rsqrt(jnp.sum(cap_vec * cap_vec, axis=1, keepdims=True) + EPSILON)
    fig_unit = fig_vec * fig_inv
    cap_unit = cap_vec * cap_inv
    fig_emb = fig_unit.astype(jnp.bfloat16)
    cap_emb = cap_unit.astype(jnp.bfloat16)
    all_fig, all_cap = (
        lax.all_gather(fig_emb, "dp", axis=0, tiled=True),
        lax.all_gather(cap_emb, "dp", axis=0, tiled=True),
    )
    logit_mult = logit_scale[0]
    pair_count = fig_slot.shape[0]
    pair_total = all_fig.shape[0]
    first_pair = lax.axis_index("dp") * pair_count
    row_logits = logit_mult * jnp.dot(fig_emb, all_cap.T, preferred_element_type=jnp.float32)
    col_logits = logit_mult * jnp.dot(all_fig, cap_emb.T, preferred_element_type=jnp.float32)
    row_lse = log_total(row_logits, 1)
    col_lse = log_total(col_logits, 0)
    own_mask = jnp.arange(pair_total)[None, :] == (first_pair + jnp.arange(pair_count))[:, None]
    eye_rows = own_mask.astype(jnp.float32)
    diag_logit = jnp.sum(jnp.where(own_mask, row_logits, 0.0), axis=1)
    pair_loss = 0.5 * (row_lse - diag_logit) + 0.5 * (col_lse - diag_logit)
    prob_rows = jnp.exp(row_logits - row_lse[:, None])
    prob_cols = jnp.exp(col_logits - col_lse[None, :])
    cap_wide = all_cap.astype(jnp.float32)
    fig_wide = all_fig.astype(jnp.float32)
    row_grad = 0.5 * loss_cotangent[:, None] * (prob_rows - eye_rows)
    col_grad = 0.5 * (prob_cols - eye_rows.T) * loss_cotangent[None, :]
    fig_grad = logit_mult * jnp.dot(row_grad, cap_wide, precision=lax.Precision.HIGHEST)
    cap_grad = logit_mult * jnp.dot(col_grad.T, fig_wide, precision=lax.Precision.HIGHEST)
    fig_part = logit_mult * jnp.dot(
        col_grad, cap_emb.astype(jnp.float32), precision=lax.Precision.HIGHEST
    )
    cap_part = logit_mult * jnp.dot(
        row_grad.T, fig_emb.astype(jnp.float32), precision=lax.Precision.HIGHEST
    )
    fig_more, cap_more = (
        lax.psum_scatter(
            fig_part.astype(jnp.bfloat16), "dp", scatter_dimension=0, tiled=True
        ).astype(jnp.float32),
        lax.psum_scatter(
            cap_part.astype(jnp.bfloat16), "dp", scatter_dimension=0, tiled=True
        ).astype(jnp.float32),
    )
    fig_grad = fig_grad + fig_more
    cap_grad = cap_grad + cap_more
    figure_direction = fig_inv * (
        fig_grad - fig_unit * jnp.sum(fig_unit * fig_grad, axis=1, keepdims=True)
    )
    caption_direction = cap_inv * (
        cap_grad - cap_unit * jnp.sum(cap_unit * cap_grad, axis=1, keepdims=True)
    )
    slot_ct = (
        jnp.zeros((row_count, feature_width), jnp.float32)
        .at[fig_slot]
        .add(figure_direction)
        .at[cap_slot]
        .add(caption_direction)
    )
    branch_ct = pullback(slot_ct)[0]
    slot_gradient = (slot_ct + branch_ct.astype(jnp.float32)).astype(jnp.bfloat16)
    safe_ids = jnp.minimum(recv_ids, row_count - 1)
    live_mask = (recv_ids < row_count)[:, :, None]
    back_rows = jnp.where(live_mask, slot_gradient[safe_ids], jnp.zeros((), jnp.bfloat16))
    home_rows = lax.all_to_all(back_rows, "dp", split_axis=0, concat_axis=0, tiled=True)
    page_grad = home_rows[owner_idx, rank_idx]
    return (page_grad, pair_loss)


def solution(mesh):
    return jax.shard_map(
        body,
        mesh=mesh,
        in_specs=(
            P(("dp", "fsdp"), None),
            P(("dp", "fsdp")),
            P(("dp", "fsdp"), None),
            P(None, "fsdp", None),
            P(None, "fsdp"),
            P(("dp", "fsdp")),
            P(("dp", "fsdp")),
            P(),
            P(("dp", "fsdp")),
        ),
        out_specs=(P(("dp", "fsdp"), None), P(("dp", "fsdp"))),
        check_vma=False,
    )
```

profile of v0, /device:TPU:0, one launch (start us, length us, event | category | flops | bytes accessed | tf_op | source)
XLA Modules:
  0.0 762.2 jit_solution(8278584684030657163)
XLA Ops:
  11.6 89.8 %scatter_fusion = s32[16,50]{1,0:T(8,128)} fusion(s32[16,50]{1,0:T(8,128)} %broadcast.152, s32[640]{0:T(1024)S(1)} %get-tuple-element.5, s32[640]{0:T(1024)S(1)} %get-tuple-element.8), kind=kCustom, calls=%fused_computation.4 | custom fusion | bytes 12800 | tf_op jit(solution)/shard_map/scatter | solution.py:72
  101.4 6.8 all-to-all-start
  108.6 86.5 %scatter_fusion.1 = bf16[16,50,2048]{2,0,1:T(8,128)(2,1)S(1)} fusion(bf16[16,50,2048]{2,0,1:T(8,128)(2,1)S(1)} %broadcast_in_dim.51, s32[640]{0:T(1024)S(1)} %get-tuple-element.5, bf16[640,2048]{1,0:T(8,128)(2,1)} %param.9), kind=kCustom, calls=%fused_computation.5 | custom fusion | bytes 7869440 | tf_op jit(solution)/shard_map/scatter | solution.py:69
  198.8 7.4 all-to-all-start.1
  209.4 45.6 %all-to-all-done.1 = bf16[16,50,2048]{2,1,0:T(8,128)(2,1)} async-done(((bf16[16,50,2048]{2,1,0:T(8,128)(2,1)}), bf16[16,50,2048]{2,1,0:T(8,128)(2,1)}, u32[]{:S(2)}, u32[]{:S(2)}) %all-to-all-start.1) | async-done | bytes 3276832 | tf_op jit(solution)/shard_map/all_to_all | solution.py:75
  259.6 8.6 %scatter_custom_fusion.2 = bf16[640,2048]{1,0:T(8,128)(2,1)S(1)} fusion(s32[800]{0:T(1024)S(1)} %fusion.56, bf16[800,2048]{1,0:T(8,128)(2,1)} %reshape.247, bf16[]{:T(256)} %constant.23.clone.1), kind=kCustom, calls=%fused_computation.53 | custom fusion | bytes 2621952 | tf_op jit(solution)/shard_map/scatter | solution.py:82
  268.3 7.0 fusion.21
  277.9 6.1 fusion.22
  286.5 6.1 fusion.23
  294.3 16.7 %fusion.63 = (f32[16,640]{1,0:T(8,128)S(1)}, f32[16,640,640]{1,2,0:T(8,128)}) fusion(bf16[640,16,64]{0,2,1:T(8,128)(2,1)} %bitcast.119, bf16[640,16,64]{0,2,1:T(8,128)(2,1)} %bitcast.117, pred[640,640]{0,1:T(8,128)(4,1)S(1)} %broadcast_compare_fusion), kind=kOutput, calls=%fused_computation.135 | convolution fusion | flops 858511360 | bytes 29286400 | tf_op jit(solution)/shard_map/jvp(qhd,khd->hqk)/dot_general | solution.py:35
  310.9 10.0 %divide_convert_fusion = bf16[16,640,640]{1,2,0:T(8,128)(2,1)S(1)} fusion(f32[16,640,640]{1,2,0:T(8,128)} %get-tuple-element.16, f32[16,640]{1,0:T(8,128)S(1)} %get-tuple-element.15), kind=kLoop, calls=%fused_computation.17 | loop fusion | flops 13107200 | bytes 39362560 | tf_op jit(solution)/shard_map/jvp()/convert_element_type | solution.py:41
  328.0 8.2 %convert_add_fusion = f32[640,2048]{1,0:T(8,128)} fusion(bf16[640,2048]{1,0:T(8,128)(2,1)} %copy-done.2, bf16[640,1024]{0,1:T(8,128)(2,1)S(1)} %bitcast.114, bf16[1024,2048]{1,0:T(8,128)(2,1)} %all-gather.7.cloned.1.call-done), kind=kOutput, calls=%fused_computation.21 | convolution fusion | flops 2686976000 | bytes 13369344 | tf_op jit(solution)/shard_map/jvp()/dot_general | solution.py:44
  346.3 37.6 %all-gather.11.cloned.1.call-done = bf16[256,2048]{1,0:T(8,128)(2,1)} async-done(((bf16[16,2048]{1,0:T(8,128)(2,1)}), bf16[256,2048]{1,0:T(8,128)(2,1)}) %all-gather.11.cloned.1.call-update) | async-done | bytes 1048592 | tf_op jit(solution)/shard_map/all_gather | solution.py:104
  385.6 42.1 %all-gather.9.cloned.1.call-done = bf16[256,2048]{1,0:T(8,128)(2,1)} async-done(((bf16[16,2048]{1,0:T(8,128)(2,1)}), bf16[256,2048]{1,0:T(8,128)(2,1)}) %all-gather.9.cloned.1.call-update) | async-done | bytes 1048592 | tf_op jit(solution)/shard_map/all_gather | solution.py:105
  437.4 67.8 %reduce-scatter.3.cloned.1.call-done = bf16[16,2048]{1,0:T(8,128)(2,1)} async-done(((bf16[256,2048]{1,0:T(8,128)(2,1)}), bf16[16,2048]{1,0:T(8,128)(2,1)}) %reduce-scatter.3.cloned.1.call-update) | async-done | bytes 65552 | tf_op jit(solution)/shard_map/reduce_scatter | solution.py:134
  512.1 68.7 %reduce-scatter.5.cloned.1.call-done = bf16[16,2048]{1,0:T(8,128)(2,1)} async-done(((bf16[256,2048]{1,0:T(8,128)(2,1)}), bf16[16,2048]{1,0:T(8,128)(2,1)}) %reduce-scatter.5.cloned.1.call-update) | async-done | bytes 65552 | tf_op jit(solution)/shard_map/reduce_scatter | solution.py:137
  588.0 7.7 %fusion.64 = bf16[640,1024]{1,0:T(8,128)(2,1)} fusion(f32[640,2048]{1,0:T(8,128)} %scatter_custom_fusion.4, bf16[1024,2048]{1,0:T(8,128)(2,1)} %all-gather.7.cloned.1.call-done), kind=kOutput, calls=%fused_computation.136 | convolution fusion | flops 2684354560 | bytes 10747904 | tf_op jit(solution)/shard_map/transpose(jvp())/dot_general | solution.py:44
  597.8 10.1 %convolution_convert_fusion.3 = bf16[16,64,640]{2,1,0:T(8,128)(2,1)} fusion(bf16[16,64,640]{2,1,0:T(8,128)(2,1)S(1)} %bitcast.112, bf16[16,640,640]{1,2,0:T(8,128)(2,1)} %copy-done), kind=kOutput, calls=%fused_computation.50 | convolution fusion | flops 839516160 | bytes 15728640 | tf_op jit(solution)/shard_map/transpose(jvp(hqk,khd->qhd))/dot_general | solution.py:42
  607.9 15.0 %fusion.5 = (f32[16,640]{1,0:T(8,128)S(1)}, bf16[16,640,640]{1,2,0:T(8,128)(2,1)}) fusion(f32[16,640,640]{1,2,0:T(8,128)} %get-tuple-element.16, f32[16,640]{1,0:T(8,128)S(1)} %copy-done.14, bf16[16,64,640]{2,1,0:T(8,128)(2,1)S(1)} %bitcast.113, bf16[640,16,64]{0,2,1:T(8,128)(2,1)S(1)} %bitcast.111), kind=kOutput, calls=%fused_computation.16 | convolution fusion | flops 871618560 | bytes 42024960 | tf_op jit(solution)/shard_map/transpose(jvp(hqk,khd->qhd))/dot_general | solution.py:42
  622.9 16.5 %convolution_convert_fusion.2 = bf16[16,640,64]{1,2,0:T(8,128)(2,1)S(1)} fusion(bf16[640,16,64]{0,2,1:T(8,128)(2,1)} %bitcast.120, f32[16,640,640]{1,2,0:T(8,128)} %get-tuple-element.16, bf16[16,640,640]{1,2,0:T(8,128)(2,1)} %get-tuple-element.25, f32[16,640]{1,0:T(8,128)S(1)} %neg.6, f32[16,640]{1,0:T(8,128)S(1)} %copy-done.13, ...), kind=kOutput, calls=%fused_computation.49 | convolution fusion | flops 878837760 | bytes 42434560 | tf_op jit(solution)/shard_map/transpose(jvp(qhd,khd->hqk))/dot_general | solution.py:35
  639.4 17.1 %convolution_convert_fusion.1 = bf16[16,640,64]{1,2,0:T(8,128)(2,1)} fusion(bf16[640,16,64]{0,2,1:T(8,128)(2,1)S(1)} %bitcast.118, f32[16,640,640]{1,2,0:T(8,128)} %get-tuple-element.16, bf16[16,640,640]{1,2,0:T(8,128)(2,1)} %get-tuple-element.25, f32[16,640]{1,0:T(8,128)S(1)} %neg.6, f32[16,640]{1,0:T(8,128)S(1)} %copy-done.13, ...), kind=kOutput, calls=%fused_computation.48 | convolution fusion | flops 878837760 | bytes 42434560 | tf_op jit(solution)/shard_map/transpose(jvp(qhd,khd->hqk))/dot_general | solution.py:35
  682.6 5.9 copy_select_fusion
  690.3 48.3 %all_to_all.19 = bf16[16,50,2048]{2,1,0:T(8,128)(2,1)S(1)} all-to-all(bf16[16,50,2048]{2,1,0:T(8,128)(2,1)S(1)} %copy.65), channel_id=1, replica_groups=mesh['dp'=16,'fsdp'=8] {'dp'}, dimensions={0} | all-to-all | bytes 6553600 | tf_op jit(solution)/shard_map/all_to_all | solution.py:161
  740.4 14.7 %gather_fusion.3 = bf16[640,2048]{1,0:T(8,128)(2,1)} fusion(bf16[16,50,2048]{2,0,1:T(8,128)(2,1)S(1)} %copy.66, s32[640]{0:T(1024)S(1)} %copy-done.1), kind=kCustom, calls=%fused_computation.3 | custom fusion | bytes 5248000 | tf_op jit(solution)/shard_map/gather | solution.py:162
  (155 shorter events, 96.5 us)
Async XLA Ops:
  7.2 261.1 %all-gather.5.cloned.1.call-start = ((), (), s32[]{:S(2)}) async-start(), calls=%async_computation.5 | async-start | bytes 14155776 | tf_op jit(solution)/shard_map/all_gather | solution.py:85
  101.4 97.4 %all-to-all-start = ((s32[16,1,50]{2,1,0:T(1,128)}), s32[16,1,50]{2,1,0:T(1,128)S(1)}, u32[]{:S(2)}, u32[]{:S(2)}) async-start(s32[16,1,50]{2,1,0:T(1,128)} %bitcast.3), calls=%async_computation | async-start | bytes 16384 | tf_op jit(solution)/shard_map/all_to_all | solution.py:76
  198.8 56.2 %all-to-all-start.1 = ((bf16[16,50,2048]{2,1,0:T(8,128)(2,1)}), bf16[16,50,2048]{2,1,0:T(8,128)(2,1)}, u32[]{:S(2)}, u32[]{:S(2)}) async-start(bf16[16,50,2048]{2,1,0:T(8,128)(2,1)} %copy.55), calls=%async_computation.1 | async-start | bytes 7340032 | tf_op jit(solution)/shard_map/all_to_all | solution.py:75
  206.2 121.8 %all-gather.7.cloned.1.call-start = ((), (), s32[]{:S(2)}) async-start(), calls=%async_computation.6 | async-start | bytes 4718592 | tf_op jit(solution)/shard_map/all_gather | solution.py:86
  206.9 176.9 %all-gather.11.cloned.1.call-start = ((), (), s32[]{:S(2)}) async-start(), calls=%async_computation.8 | async-start | bytes 1114112 | tf_op jit(solution)/shard_map/all_gather | solution.py:104
  207.5 86.8 %copy-start.9 = (pred[640,640]{0,1:T(8,128)(4,1)}, pred[640,640]{0,1:T(8,128)(4,1)S(1)}, u32[]{:S(2)}) copy-start(pred[640,640]{0,1:T(8,128)(4,1)S(1)} %broadcast_compare_fusion) | copy-start | bytes 1228804
  339.4 95.9 %copy-start.5 = (f32[16,2048]{1,0:T(8,128)}, f32[16,2048]{1,0:T(8,128)S(1)}, u32[]{:S(2)}) copy-start(f32[16,2048]{1,0:T(8,128)S(1)} %gather_fusion) | copy-start | bytes 393220
  340.8 92.3 %copy-start.8 = (bf16[16,2048]{1,0:T(8,128)(2,1)S(1)}, bf16[16,2048]{1,0:T(8,128)(2,1)}, u32[]{:S(2)}) copy-start(bf16[16,2048]{1,0:T(8,128)(2,1)} %multiply_convert_fusion.1) | copy-start | bytes 196612
  340.8 86.9 %all-gather.9.cloned.1.call-start = ((), (), s32[]{:S(2)}) async-start(), calls=%async_computation.7 | async-start | bytes 1114112 | tf_op jit(solution)/shard_map/all_gather | solution.py:105
  345.5 159.7 %reduce-scatter.3.cloned.1.call-start = ((), (), s32[]{:S(2)}) async-start(), calls=%async_computation.9 | async-start | bytes 1114112 | tf_op jit(solution)/shard_map/reduce_scatter | solution.py:134
  346.2 89.1 %copy-start.21 = (s32[16]{0:T(128)}, s32[16]{0:T(128)S(1)}, u32[]{:S(2)}) copy-start(s32[16]{0:T(128)S(1)} %iota_add_fusion) | copy-start | bytes 196
  346.3 89.1 %copy-start.23 = (f32[16]{0:T(128)}, f32[16]{0:T(128)S(1)}, u32[]{:S(2)}) copy-start(f32[16]{0:T(128)S(1)} %broadcast_multiply_fusion) | copy-start | bytes 196
  383.9 51.6 %copy-start.17 = (s32[16,1,50]{2,1,0:T(1,128)S(1)}, s32[16,1,50]{2,1,0:T(1,128)}, u32[]{:S(2)}) copy-start(s32[16,1,50]{2,1,0:T(1,128)} %copy-done.16) | copy-start | bytes 9604
  383.9 52.9 %copy-start.12 = (f32[16,640]{1,0:T(8,128)S(1)}, f32[16,640]{1,0:T(8,128)}, u32[]{:S(2)}) copy-start(f32[16,640]{1,0:T(8,128)} %copy-done.11) | copy-start | bytes 122884
  427.7 77.5 %copy-start.4 = (bf16[256,2048]{1,0:T(8,128)(2,1)S(1)}, bf16[256,2048]{1,0:T(8,128)(2,1)}, u32[]{:S(2)}) copy-start(bf16[256,2048]{1,0:T(8,128)(2,1)} %all-gather.9.cloned.1.call-done) | copy-start | bytes 3145732
  429.6 75.6 %copy-start.15 = (f32[16,256]{1,0:T(8,128)}, f32[16,256]{1,0:T(8,128)S(1)}, u32[]{:S(2)}) copy-start(f32[16,256]{1,0:T(8,128)S(1)} %get-tuple-element.17) | copy-start | bytes 49156
  430.1 75.1 %copy-start.28 = (f32[16]{0:T(128)}, f32[16]{0:T(128)S(1)}, u32[]{:S(2)}) copy-start(f32[16]{0:T(128)S(1)} %get-tuple-element.14) | copy-start | bytes 196
  430.1 75.1 %copy-start.30 = (f32[16]{0:T(128)}, f32[16]{0:T(128)S(1)}, u32[]{:S(2)}) copy-start(f32[16]{0:T(128)S(1)} %get-tuple-element.13) | copy-start | bytes 196
  433.1 147.6 %reduce-scatter.5.cloned.1.call-start = ((), (), s32[]{:S(2)}) async-start(), calls=%async_computation.10 | async-start | bytes 1114112 | tf_op jit(solution)/shard_map/reduce_scatter | solution.py:137
  505.2 75.5 %copy-start.3 = (bf16[256,2048]{1,0:T(8,128)(2,1)S(1)}, bf16[256,2048]{1,0:T(8,128)(2,1)}, u32[]{:S(2)}) copy-start(bf16[256,2048]{1,0:T(8,128)(2,1)} %all-gather.11.cloned.1.call-done) | copy-start | bytes 3145732
  508.2 72.5 %copy-start.22 = (s32[16]{0:T(128)S(1)}, s32[16]{0:T(128)}, u32[]{:S(2)}) copy-start(s32[16]{0:T(128)} %copy-done.21) | copy-start | bytes 196
  508.2 72.5 %copy-start.24 = (f32[16]{0:T(128)S(1)}, f32[16]{0:T(128)}, u32[]{:S(2)}) copy-start(f32[16]{0:T(128)} %copy-done.23) | copy-start | bytes 196
  508.2 72.5 %copy-start.26 = (f32[16]{0:T(128)S(1)}, f32[16]{0:T(128)}, u32[]{:S(2)}) copy-start(f32[16]{0:T(128)} %copy-done.25) | copy-start | bytes 196
  508.2 72.5 %copy-start.29 = (f32[16]{0:T(128)S(1)}, f32[16]{0:T(128)}, u32[]{:S(2)}) copy-start(f32[16]{0:T(128)} %copy-done.28) | copy-start | bytes 196
  (24 other events, 277.5 us)
Sparse Core Ops, SparseCore 0:
  9.7 69.9 all-gather.4
  208.7 38.8 all-gather.6
  340.9 42.8 all-gather.10
  385.9 41.8 all-gather.8
  433.2 71.9 reduce-scatter.2
  508.6 72.0 reduce-scatter.4
where the time goes:
time: 776 us; the launch traced here: 762 us
  waiting for transfers between devices  263 us (34%)
  local copies, waits for them, and re-layouts  245 us (32%)
  matrix products  142 us (18%)
  blocking collectives  48.3 us (6%)
  other arithmetic  33.3 us (4%)
  between operations  15.7 us (2%)
  starting transfers between devices  14.4 us (2%)
    scatter x2, local copies, waits for them, and re-layouts, body(): send_rows = jnp.zeros((dp_count, capacity, feature_width), jnp.bfloat16)....  90.2 us
    scatter x1, local copies, waits for them, and re-layouts, body(): jnp.full((dp_count, capacity), row_count, jnp.int32).at[owner_idx, rank_idx]  89.8 us
    reduce_scatter x1, waiting for transfers between devices, body(): lax.psum_scatter(cap_part.astype(jnp.bfloat16), 'dp', scatter_dimension=0...  68.7 us
    reduce_scatter x1, waiting for transfers between devices, body(): lax.psum_scatter(fig_part.astype(jnp.bfloat16), 'dp', scatter_dimension=0...  67.8 us
    dot_general x3, matrix products, attend(): jnp.einsum('qhd,khd->hqk', query_h, key_h, preferred_element_type=jnp.flo...  50.2 us
    all_to_all x1, blocking collectives, body(): lax.all_to_all(back_rows, 'dp', split_axis=0, concat_axis=0, tiled=True)  48.3 us
    all_to_all x1, waiting for transfers between devices, body(): lax.all_to_all(send_rows, 'dp', split_axis=0, concat_axis=0, tiled=True)  45.6 us
    all_gather x1, waiting for transfers between devices, body(): lax.all_gather(cap_emb, 'dp', axis=0, tiled=True)  42.1 us
  transfers between devices with their start and end apart: 8, of which 5 were waited for; matrix products, arithmetic and copies ran while one was open for 36% of the time, Pallas kernels for 0%

commit v1 on v0

v1 whole, which is shorter than its diff:
```python
import math

import jax
import jax.numpy as jnp
from jax import lax
from jax.sharding import PartitionSpec as P

HD = 64


EPSILON = 1e-06


def log_total(values, axis):
    return jnp.log(jnp.sum(jnp.exp(values), axis=axis))


def attend(slot_row_block, qkv_mat, out_mat, doc_row):
    row_count = slot_row_block.shape[0]
    query_h = (
        jnp.dot(slot_row_block, qkv_mat[0], preferred_element_type=jnp.float32)
        .astype(jnp.bfloat16)
        .reshape(row_count, -1, HD)
    )
    key_h = (
        jnp.dot(slot_row_block, qkv_mat[1], preferred_element_type=jnp.float32)
        .astype(jnp.bfloat16)
        .reshape(row_count, -1, HD)
    )
    value_h = (
        jnp.dot(slot_row_block, qkv_mat[2], preferred_element_type=jnp.float32)
        .astype(jnp.bfloat16)
        .reshape(row_count, -1, HD)
    )
    scores = jnp.einsum("qhd,khd->hqk", query_h, key_h, preferred_element_type=jnp.float32) * (
        1.0 / math.sqrt(HD)
    )
    same_doc = doc_row[:, None] == doc_row[None, :]
    scores = jnp.where(same_doc[None], scores, -1e30)
    weights = jnp.exp(scores)
    attn_prob = (weights / jnp.sum(weights, axis=2, keepdims=True)).astype(jnp.bfloat16)
    mixed = jnp.einsum("hqk,khd->qhd", attn_prob, value_h, preferred_element_type=jnp.float32)
    mixed = mixed.astype(jnp.bfloat16).reshape(row_count, -1)
    return jnp.dot(mixed, out_mat, preferred_element_type=jnp.float32)


def select_rows(onehot, rows):
    picked = jnp.dot(onehot, rows, preferred_element_type=jnp.float32)
    return picked.astype(rows.dtype)


def select_rows_t(onehot, rows):
    picked = lax.dot_general(
        onehot, rows, (((0,), (0,)), ((), ())), preferred_element_type=jnp.float32
    )
    return picked.astype(rows.dtype)


def body(
    page_embed,
    page_slot,
    doc_ids,
    qkv_weight,
    out_weight,
    fig_slot,
    cap_slot,
    logit_scale,
    loss_cotangent,
):
    dp_count = lax.axis_size("dp")
    row_count = page_embed.shape[0]
    feature_width = page_embed.shape[1]
    capacity = 5 * row_count // (4 * dp_count)
    buffer_rows = dp_count * capacity
    owner_idx = page_slot // row_count
    slot_idx = page_slot % row_count
    onehot = (owner_idx[:, None] == jnp.arange(dp_count)[None, :]).astype(jnp.int32)
    rank_idx = jnp.sum((jnp.cumsum(onehot, axis=0) - onehot) * onehot, axis=1)
    dest = owner_idx * capacity + rank_idx
    send_match = dest[None, :] == jnp.arange(buffer_rows)[:, None]
    send_onehot = send_match.astype(jnp.bfloat16)
    send_rows = select_rows(send_onehot, page_embed)
    send_ids = jnp.where(
        jnp.any(send_match, axis=1),
        jnp.sum(jnp.where(send_match, slot_idx[None, :], 0), axis=1),
        row_count,
    ).reshape(dp_count, capacity)
    recv_rows, recv_ids = (
        lax.all_to_all(
            send_rows.reshape(dp_count, capacity, feature_width),
            "dp",
            split_axis=0,
            concat_axis=0,
            tiled=True,
        ),
        lax.all_to_all(send_ids, "dp", split_axis=0, concat_axis=0, tiled=True),
    )
    flat_ids = recv_ids.reshape(-1)
    recv_onehot = (jnp.arange(row_count)[:, None] == flat_ids[None, :]).astype(jnp.bfloat16)
    slot_row_block = select_rows(recv_onehot, recv_rows.reshape(-1, feature_width))
    qkv_full, out_full = (
        lax.all_gather(qkv_weight, "fsdp", axis=1, tiled=True),
        lax.all_gather(out_weight, "fsdp", axis=1, tiled=True),
    )
    doc_row = doc_ids[0]

    def branch(inputs):
        return attend(inputs, qkv_full, out_full, doc_row)

    attn_out, pullback = jax.vjp(branch, slot_row_block)
    slot_output = slot_row_block.astype(jnp.float32) + attn_out
    fig_vec = slot_output[fig_slot]
    cap_vec = slot_output[cap_slot]
    fig_inv = lax.rsqrt(jnp.sum(fig_vec * fig_vec, axis=1, keepdims=True) + EPSILON)
    cap_inv = lax.rsqrt(jnp.sum(cap_vec * cap_vec, axis=1, keepdims=True) + EPSILON)
    fig_unit = fig_vec * fig_inv
    cap_unit = cap_vec * cap_inv
    fig_emb = fig_unit.astype(jnp.bfloat16)
    cap_emb = cap_unit.astype(jnp.bfloat16)
    pair_count = fig_slot.shape[0]
    both_emb = jnp.concatenate([fig_emb, cap_emb], axis=0)
    all_both = lax.all_gather(both_emb, "dp", axis=0, tiled=False)
    all_weight = lax.all_gather(loss_cotangent, "dp", axis=0, tiled=True)
    all_fig = all_both[:, :pair_count].reshape(-1, feature_width)
    all_cap = all_both[:, pair_count:].reshape(-1, feature_width)
    logit_mult = logit_scale[0]
    pair_total = all_fig.shape[0]
    first_pair = lax.axis_index("dp") * pair_count
    logits = logit_mult * jnp.dot(all_fig, all_cap.T, preferred_element_type=jnp.float32)
    row_lse = log_total(logits, 1)
    col_lse = log_total(logits, 0)
    eye_mat = jnp.eye(pair_total, dtype=jnp.float32)
    diag_logit = jnp.sum(logits * eye_mat, axis=1)
    own_rows = first_pair + jnp.arange(pair_count)
    own_mask = (jnp.arange(pair_total)[None, :] == own_rows[:, None]).astype(jnp.float32)
    loss_all = 0.5 * (row_lse - diag_logit) + 0.5 * (col_lse - diag_logit)
    pair_loss = jnp.dot(own_mask, loss_all, precision=lax.Precision.HIGHEST)
    prob_rows = jnp.exp(logits - row_lse[:, None])
    prob_cols = jnp.exp(logits - col_lse[None, :])
    coef = 0.5 * all_weight[:, None] * (prob_rows - eye_mat) + 0.5 * (
        prob_cols - eye_mat
    ) * all_weight[None, :]
    coef_rows = jnp.dot(own_mask, coef, precision=lax.Precision.HIGHEST)
    coef_cols = jnp.dot(own_mask, coef.T, precision=lax.Precision.HIGHEST)
    fig_grad = logit_mult * jnp.dot(
        coef_rows, all_cap.astype(jnp.float32), precision=lax.Precision.HIGHEST
    )
    cap_grad = logit_mult * jnp.dot(
        coef_cols, all_fig.astype(jnp.float32), precision=lax.Precision.HIGHEST
    )
    figure_direction = fig_inv * (
        fig_grad - fig_unit * jnp.sum(fig_unit * fig_grad, axis=1, keepdims=True)
    )
    caption_direction = cap_inv * (
        cap_grad - cap_unit * jnp.sum(cap_unit * cap_grad, axis=1, keepdims=True)
    )
    slot_ct = (
        jnp.zeros((row_count, feature_width), jnp.float32)
        .at[fig_slot]
        .add(figure_direction)
        .at[cap_slot]
        .add(caption_direction)
    )
    branch_ct = pullback(slot_ct)[0]
    slot_gradient = (slot_ct + branch_ct.astype(jnp.float32)).astype(jnp.bfloat16)
    back_rows = select_rows_t(recv_onehot, slot_gradient)
    home_rows = lax.all_to_all(
        back_rows.reshape(dp_count, capacity, feature_width),
        "dp",
        split_axis=0,
        concat_axis=0,
        tiled=True,
    )
    page_grad = select_rows_t(send_onehot, home_rows.reshape(-1, feature_width))
    return (page_grad, pair_loss)


def solution(mesh):
    return jax.shard_map(
        body,
        mesh=mesh,
        in_specs=(
            P(("dp", "fsdp"), None),
            P(("dp", "fsdp")),
            P(("dp", "fsdp"), None),
            P(None, "fsdp", None),
            P(None, "fsdp"),
            P(("dp", "fsdp")),
            P(("dp", "fsdp")),
            P(),
            P(("dp", "fsdp")),
        ),
        out_specs=(P(("dp", "fsdp"), None), P(("dp", "fsdp"))),
        check_vma=False,
    )
```

time: 776 us -> 404 us (0.52); the launches traced: 762 us -> 400 us
  local copies, waits for them, and re-layouts: 245 us -> 42.7 us
  waiting for transfers between devices: 263 us -> 104 us
  matrix products: 142 us -> 156 us
  blocking collectives: 48.3 us -> 36.5 us
  other arithmetic: 33.3 us -> 24.6 us
    scatter x4 -> x0, local copies, waits for them, and re-layouts: 189 us -> none  [the longest x2 90.2 us: body(): send_rows = jnp.zeros((dp_count, capacity, feature_width), jnp.bfloat16)....]
    reduce_scatter x2 -> x0, waiting for transfers between devices: 136 us -> none  [the longest x1 68.7 us: body(): lax.psum_scatter(cap_part.astype(jnp.bfloat16), 'dp', scatter_dimension=0...]
    all_gather x2 -> x1, waiting for transfers between devices: 79.7 us -> 8.79 us  [body(): all_both = lax.all_gather(both_emb, 'dp', axis=0, tiled=False)]
    all_to_all x1 -> x2, waiting for transfers between devices: 45.6 us -> 94.1 us  [the longest x1 48 us: body(): lax.all_to_all(back_rows.reshape(dp_count, capacity, feature_width), 'dp'...]
    all_to_all x1 -> x0, blocking collectives: 48.3 us -> none  [body(): lax.all_to_all(back_rows, 'dp', split_axis=0, concat_axis=0, tiled=True)]
    unnamed x0 -> x1, blocking collectives: none -> 36.5 us
    gather x3 -> x0, local copies, waits for them, and re-layouts: 24.5 us -> none  [the longest x1 14.7 us: body(): page_grad = home_rows[owner_idx, rank_idx]]
    dot_general x6 -> x10, matrix products: 13.2 us -> 29.5 us  [the longest x2 17.2 us: select_rows_t(): lax.dot_general(onehot, rows, (((0,), (0,)), ((), ())), preferred_element...]
  transfers between devices with their start and end apart: 8 -> 6, of which waited for: 5 -> 3; matrix products, arithmetic and copies ran while one was open for 36% -> 20% of each run, Pallas kernels for 0% -> 0%
where the time goes in v1:
time: 404 us; the launch traced here: 400 us
  matrix products  156 us (39%)
  waiting for transfers between devices  104 us (26%)
  local copies, waits for them, and re-layouts  42.7 us (11%)
  blocking collectives  36.5 us (9%)
  other arithmetic  24.6 us (6%)
  starting transfers between devices  20.2 us (5%)
  between operations  15.7 us (4%)
    dot_general x3, matrix products, attend(): jnp.einsum('qhd,khd->hqk', query_h, key_h, preferred_element_type=jnp.flo...  50.3 us
    all_to_all x1, waiting for transfers between devices, body(): lax.all_to_all(back_rows.reshape(dp_count, capacity, feature_width), 'dp'...  48 us
    all_to_all x1, waiting for transfers between devices, body(): lax.all_to_all(send_rows.reshape(dp_count, capacity, feature_width), 'dp'...  46.1 us
    unnamed x1, blocking collectives  36.5 us
    dot_general x3, matrix products, attend(): jnp.einsum('hqk,khd->qhd', attn_prob, value_h, preferred_element_type=jnp...  27.2 us
    dot_general x2, matrix products, select_rows_t(): lax.dot_general(onehot, rows, (((0,), (0,)), ((), ())), preferred_element...  17.2 us
    dot_general x2, matrix products, attend(): return jnp.dot(mixed, out_mat, preferred_element_type=jnp.float32)  16 us
    dot_general x2, matrix products, attend(): jnp.dot(slot_row_block, qkv_mat[0], preferred_element_type=jnp.float32)  13.8 us
  transfers between devices with their start and end apart: 6, of which 3 were waited for; matrix products, arithmetic and copies ran while one was open for 20% of the time, Pallas kernels for 0%

profile of v1, /device:TPU:0, one launch (start us, length us, event | category | flops | bytes accessed | tf_op | source)
XLA Modules:
  0.0 399.8 jit_solution(7606666642404240071)
XLA Ops:
  12.5 7.1 %all-to-all-start = ((s32[16,1,50]{2,1,0:T(1,128)}), s32[16,1,50]{2,1,0:T(1,128)S(1)}, u32[]{:S(2)}, u32[]{:S(2)}) async-start(s32[16,1,50]{2,1,0:T(1,128)} %select_n.51), calls=%async_computation | async-start | bytes 16384 | tf_op jit(solution)/shard_map/all_to_all | solution.py:96
  28.5 7.6 %all-to-all-start.1 = ((bf16[16,50,2048]{2,1,0:T(8,128)(2,1)}), bf16[16,50,2048]{2,1,0:T(8,128)(2,1)}, u32[]{:S(2)}, u32[]{:S(2)}) async-start(bf16[16,50,2048]{2,1,0:T(8,128)(2,1)} %reshape.159), calls=%async_computation.1 | async-start | bytes 7340032 | tf_op jit(solution)/shard_map/all_to_all | solution.py:89
  38.8 46.1 %all-to-all-done.1 = bf16[16,50,2048]{2,1,0:T(8,128)(2,1)} async-done(((bf16[16,50,2048]{2,1,0:T(8,128)(2,1)}), bf16[16,50,2048]{2,1,0:T(8,128)(2,1)}, u32[]{:S(2)}, u32[]{:S(2)}) %all-to-all-start.1) | async-done | bytes 3276832 | tf_op jit(solution)/shard_map/all_to_all | solution.py:89
  89.6 5.2 %convolution_convert_fusion.3 = bf16[640,2048]{1,0:T(8,128)(2,1)S(1)} fusion(bf16[800,2048]{1,0:T(8,128)(2,1)} %reshape.160, s32[800]{0:T(1024)S(1)} %eq.103), kind=kOutput, calls=%fused_computation.28 | convolution fusion | flops 2098974720 | bytes 5901440 | tf_op jit(solution)/shard_map/dot_general | solution.py:48
  94.9 7.0 %fusion.21 = bf16[640,1024]{1,0:T(8,128)(2,1)} fusion(bf16[640,2048]{1,0:T(8,128)(2,1)S(1)} %convolution_convert_fusion.3, bf16[3,2048,1024]{2,1,0:T(8,128)(2,1)} %all-gather.5.cloned.1.call-done), kind=kOutput, calls=%fused_computation.44 | convolution fusion | flops 2685009920 | bytes 8126464 | tf_op jit(solution)/shard_map/jvp()/dot_general | solution.py:21
  104.4 6.1 %fusion.20 = bf16[640,1024]{1,0:T(8,128)(2,1)} fusion(bf16[640,2048]{1,0:T(8,128)(2,1)S(1)} %convolution_convert_fusion.3, bf16[3,2048,1024]{2,1,0:T(8,128)(2,1)} %all-gather.5.cloned.1.call-done), kind=kOutput, calls=%fused_computation.43 | convolution fusion | flops 2685009920 | bytes 8126464 | tf_op jit(solution)/shard_map/jvp()/dot_general | solution.py:26
  112.9 6.1 %fusion.22 = bf16[640,1024]{1,0:T(8,128)(2,1)} fusion(bf16[640,2048]{1,0:T(8,128)(2,1)S(1)} %convolution_convert_fusion.3, bf16[3,2048,1024]{2,1,0:T(8,128)(2,1)} %all-gather.5.cloned.1.call-done), kind=kOutput, calls=%fused_computation.45 | convolution fusion | flops 2685009920 | bytes 8126464 | tf_op jit(solution)/shard_map/jvp()/dot_general | solution.py:31
  121.1 16.7 %fusion.57 = (f32[16,640]{1,0:T(8,128)S(1)}, f32[16,640,640]{1,2,0:T(8,128)}) fusion(bf16[640,16,64]{0,2,1:T(8,128)(2,1)} %bitcast.121, bf16[640,16,64]{0,2,1:T(8,128)(2,1)} %bitcast.123, pred[640,640]{0,1:T(8,128)(4,1)S(1)} %broadcast_compare_fusion), kind=kOutput, calls=%fused_computation.121 | convolution fusion | flops 858511360 | bytes 29286400 | tf_op jit(solution)/shard_map/jvp(qhd,khd->hqk)/dot_general | solution.py:35
  137.8 9.7 %divide_convert_fusion = bf16[16,640,640]{1,2,0:T(8,128)(2,1)S(1)} fusion(f32[16,640,640]{1,2,0:T(8,128)} %get-tuple-element.15, f32[16,640]{1,0:T(8,128)S(1)} %get-tuple-element.14), kind=kLoop, calls=%fused_computation.12 | loop fusion | flops 13107200 | bytes 39362560 | tf_op jit(solution)/shard_map/jvp()/convert_element_type | solution.py:41
  154.6 8.2 %convert_add_fusion = f32[640,2048]{1,0:T(8,128)} fusion(bf16[640,2048]{1,0:T(8,128)(2,1)} %copy-done.3, bf16[640,1024]{0,1:T(8,128)(2,1)S(1)} %bitcast.115, bf16[1024,2048]{1,0:T(8,128)(2,1)} %all-gather.7.cloned.1.call-done), kind=kOutput, calls=%fused_computation.16 | convolution fusion | flops 2686976000 | bytes 13369344 | tf_op jit(solution)/shard_map/jvp()/dot_general | solution.py:44
  172.4 36.5 %all-reduce = f32[256]{0:T(256)S(1)} all-reduce(f32[256]{0:T(256)S(1)} %dynamic-update-slice), channel_id=1, replica_groups=mesh['dp'=16,'fsdp'=8] {'dp'}, use_global_device_ids=true, to_apply=%add | all-reduce | flops 256 | bytes 2048
  208.8 8.8 %all-gather.9.cloned.1.call-done = bf16[512,2048]{1,0:T(8,128)(2,1)} async-done(((bf16[32,2048]{1,0:T(8,128)(2,1)}), bf16[512,2048]{1,0:T(8,128)(2,1)}) %all-gather.9.cloned.1.call-update) | async-done | bytes 2097168 | tf_op jit(solution)/shard_map/all_gather | solution.py:122
  225.3 5.6 %scatter_custom_fusion.1 = f32[640,2048]{1,0:T(8,128)} fusion(f32[640,2048]{1,0:T(8,128)} %scatter_custom_fusion, s32[16]{0:T(128)S(1)} %compare_select_fusion, f32[16,2048]{1,0:T(8,128)S(1)} %get-tuple-element.20, f32[16,2048]{1,0:T(8,128)S(1)} %gather_fusion.1, f32[16]{0:T(128)S(1)} %get-tuple-element.19, f32[16]{0:T(128)S(1)} %add_rsqrt_fusion), kind=kCustom, calls=%fused_computation.68 | custom fusion | flops 163840 | bytes 5506048 | tf_op jit(solution)/shard_map/scatter-add | solution.py:162
  230.9 7.7 %fusion.58 = bf16[640,1024]{1,0:T(8,128)(2,1)} fusion(f32[640,2048]{1,0:T(8,128)} %scatter_custom_fusion.1, bf16[1024,2048]{1,0:T(8,128)(2,1)} %all-gather.7.cloned.1.call-done), kind=kOutput, calls=%fused_computation.122 | convolution fusion | flops 2684354560 | bytes 10747904 | tf_op jit(solution)/shard_map/transpose(jvp())/dot_general | solution.py:44
  240.4 10.0 %convolution_convert_fusion.7 = bf16[16,64,640]{2,1,0:T(8,128)(2,1)} fusion(bf16[16,64,640]{2,1,0:T(8,128)(2,1)S(1)} %bitcast.113, bf16[16,640,640]{1,2,0:T(8,128)(2,1)} %copy-done.2), kind=kOutput, calls=%fused_computation.48 | convolution fusion | flops 839516160 | bytes 15728640 | tf_op jit(solution)/shard_map/transpose(jvp(hqk,khd->qhd))/dot_general | solution.py:42
  250.4 14.9 %fusion.5 = (f32[16,640]{1,0:T(8,128)S(1)}, bf16[16,640,640]{1,2,0:T(8,128)(2,1)}) fusion(f32[16,640,640]{1,2,0:T(8,128)} %get-tuple-element.15, f32[16,640]{1,0:T(8,128)S(1)} %multiply_divide_fusion, bf16[16,64,640]{2,1,0:T(8,128)(2,1)S(1)} %bitcast.114, bf16[640,16,64]{0,2,1:T(8,128)(2,1)S(1)} %bitcast.112), kind=kOutput, calls=%fused_computation.11 | convolution fusion | flops 871618560 | bytes 42024960 | tf_op jit(solution)/shard_map/transpose(jvp(hqk,khd->qhd))/dot_general | solution.py:42
  265.3 16.5 %convolution_convert_fusion.6 = bf16[16,640,64]{1,2,0:T(8,128)(2,1)S(1)} fusion(bf16[640,16,64]{0,2,1:T(8,128)(2,1)} %bitcast.122, f32[16,640,640]{1,2,0:T(8,128)} %get-tuple-element.15, bf16[16,640,640]{1,2,0:T(8,128)(2,1)} %get-tuple-element.22, f32[16,640]{1,0:T(8,128)S(1)} %neg.6, f32[16,640]{1,0:T(8,128)S(1)} %get-tuple-element.14, ...), kind=kOutput, calls=%fused_computation.47 | convolution fusion | flops 878837760 | bytes 42434560 | tf_op jit(solution)/shard_map/transpose(jvp(qhd,khd->hqk))/dot_general | solution.py:35
  281.8 17.1 %convolution_convert_fusion.5 = bf16[16,640,64]{1,2,0:T(8,128)(2,1)} fusion(bf16[640,16,64]{0,2,1:T(8,128)(2,1)S(1)} %bitcast.124, f32[16,640,640]{1,2,0:T(8,128)} %get-tuple-element.15, bf16[16,640,640]{1,2,0:T(8,128)(2,1)} %get-tuple-element.22, f32[16,640]{1,0:T(8,128)S(1)} %neg.6, f32[16,640]{1,0:T(8,128)S(1)} %get-tuple-element.14, ...), kind=kOutput, calls=%fused_computation.46 | convolution fusion | flops 878837760 | bytes 42434560 | tf_op jit(solution)/shard_map/transpose(jvp(qhd,khd->hqk))/dot_general | solution.py:35
  299.0 6.8 %fusion.12 = bf16[640,2048]{1,0:T(8,128)(2,1)} fusion(bf16[640,1024]{0,1:T(8,128)(2,1)S(1)} %bitcast.128, bf16[3,2048,1024]{2,1,0:T(8,128)(2,1)} %all-gather.5.cloned.1.call-done), kind=kOutput, calls=%fused_computation.29 | convolution fusion | flops 2685665280 | bytes 8126464 | tf_op jit(solution)/shard_map/transpose(jvp())/dot_general | solution.py:26
  305.7 6.8 %fusion.13 = bf16[640,2048]{1,0:T(8,128)(2,1)} fusion(bf16[640,1024]{0,1:T(8,128)(2,1)S(1)} %bitcast.129, bf16[3,2048,1024]{2,1,0:T(8,128)(2,1)} %all-gather.5.cloned.1.call-done), kind=kOutput, calls=%fused_computation.30 | convolution fusion | flops 2685665280 | bytes 8126464 | tf_op jit(solution)/shard_map/transpose(jvp())/dot_general | solution.py:21
  312.5 10.7 %convolution_convert_fusion.2 = bf16[800,2048]{1,0:T(8,128)(2,1)} fusion(f32[640,2048]{1,0:T(8,128)} %scatter_custom_fusion.1, bf16[640,2048]{1,0:T(8,128)(2,1)} %fusion.13, bf16[640,2048]{1,0:T(8,128)(2,1)} %fusion.12, s32[800]{0:T(1024)S(1)} %copy-done.9, bf16[640,1024]{0,1:T(8,128)(2,1)S(1)} %bitcast.125, ...), kind=kOutput, calls=%fused_computation.27 | convolution fusion | flops 4791521280 | bytes 19270784 | tf_op jit(solution)/shard_map/dot_general | solution.py:53
  327.9 5.2 %all-to-all-start.2 = ((bf16[16,50,2048]{2,1,0:T(8,128)(2,1)}), bf16[16,50,2048]{2,1,0:T(8,128)(2,1)}, u32[]{:S(2)}, u32[]{:S(2)}) async-start(bf16[16,50,2048]{2,1,0:T(8,128)(2,1)} %reshape.171), calls=%async_computation.2 | async-start | bytes 7340032 | tf_op jit(solution)/shard_map/all_to_all | solution.py:167
  333.8 48.0 %all-to-all-done.2 = bf16[16,50,2048]{2,1,0:T(8,128)(2,1)} async-done(((bf16[16,50,2048]{2,1,0:T(8,128)(2,1)}), bf16[16,50,2048]{2,1,0:T(8,128)(2,1)}, u32[]{:S(2)}, u32[]{:S(2)}) %all-to-all-start.2) | async-done | bytes 3276832 | tf_op jit(solution)/shard_map/all_to_all | solution.py:167
  386.5 6.5 %convolution_convert_fusion.4 = bf16[640,2048]{1,0:T(8,128)(2,1)} fusion(bf16[800,2048]{1,0:T(8,128)(2,1)} %reshape.172, s32[640]{0:T(1024)S(1)} %copy-done.7), kind=kOutput, calls=%fused_computation.32 | convolution fusion | flops 2098974720 | bytes 5900800 | tf_op jit(solution)/shard_map/dot_general | solution.py:53
  (96 shorter events, 63.2 us)
Async XLA Ops:
  7.2 12.5 %copy-start = (bf16[640,2048]{1,0:T(8,128)(2,1)S(1)}, bf16[640,2048]{1,0:T(8,128)(2,1)}, u32[]{:S(2)}) copy-start(bf16[640,2048]{1,0:T(8,128)(2,1)} %param.9) | copy-start | bytes 7864324
  7.2 87.7 %all-gather.5.cloned.1.call-start = ((), (), s32[]{:S(2)}) async-start(), calls=%async_computation.3 | async-start | bytes 14155776 | tf_op jit(solution)/shard_map/all_gather | solution.py:102
  11.2 12.6 %copy-start.6 = (s32[640]{0:T(1024)}, s32[640]{0:T(1024)S(1)}, u32[]{:S(2)}) copy-start(s32[640]{0:T(1024)S(1)} %get-tuple-element.8) | copy-start | bytes 7684
  12.5 16.0 %all-to-all-start = ((s32[16,1,50]{2,1,0:T(1,128)}), s32[16,1,50]{2,1,0:T(1,128)S(1)}, u32[]{:S(2)}, u32[]{:S(2)}) async-start(s32[16,1,50]{2,1,0:T(1,128)} %select_n.51), calls=%async_computation | async-start | bytes 16384 | tf_op jit(solution)/shard_map/all_to_all | solution.py:96
  28.5 8.6 %copy-start.10 = (s32[1,640]{1,0:T(1,128)S(1)}, s32[1,640]{1,0:T(1,128)}, u32[]{:S(2)}) copy-start(s32[1,640]{1,0:T(1,128)} %param.11) | copy-start | bytes 7684
  28.5 8.6 %copy-start.11 = (s32[16]{0:T(128)S(1)}, s32[16]{0:T(128)}, u32[]{:S(2)}) copy-start(s32[16]{0:T(128)} %param.15) | copy-start | bytes 196
  28.5 8.7 %copy-start.12 = (s32[16]{0:T(128)S(1)}, s32[16]{0:T(128)}, u32[]{:S(2)}) copy-start(s32[16]{0:T(128)} %param.14) | copy-start | bytes 196
  28.5 56.4 %all-to-all-start.1 = ((bf16[16,50,2048]{2,1,0:T(8,128)(2,1)}), bf16[16,50,2048]{2,1,0:T(8,128)(2,1)}, u32[]{:S(2)}, u32[]{:S(2)}) async-start(bf16[16,50,2048]{2,1,0:T(8,128)(2,1)} %reshape.159), calls=%async_computation.1 | async-start | bytes 7340032 | tf_op jit(solution)/shard_map/all_to_all | solution.py:89
  36.1 118.4 %all-gather.7.cloned.1.call-start = ((), (), s32[]{:S(2)}) async-start(), calls=%async_computation.4 | async-start | bytes 4718592 | tf_op jit(solution)/shard_map/all_gather | solution.py:103
  36.9 180.7 %all-gather.9.cloned.1.call-start = ((), (), s32[]{:S(2)}) async-start(), calls=%async_computation.5 | async-start | bytes 2228224 | tf_op jit(solution)/shard_map/all_gather | solution.py:122
  38.8 56.0 %copy-start.8 = (s32[800]{0:T(1024)}, s32[800]{0:T(1024)S(1)}, u32[]{:S(2)}) copy-start(s32[800]{0:T(1024)S(1)} %eq.103) | copy-start | bytes 9604
  94.8 18.1 %copy-start.3 = (bf16[640,2048]{1,0:T(8,128)(2,1)}, bf16[640,2048]{1,0:T(8,128)(2,1)S(1)}, u32[]{:S(2)}) copy-start(bf16[640,2048]{1,0:T(8,128)(2,1)S(1)} %convolution_convert_fusion.3) | copy-start | bytes 7864324
  147.5 4.7 %copy-start.2 = (bf16[16,640,640]{1,2,0:T(8,128)(2,1)}, bf16[16,640,640]{1,2,0:T(8,128)(2,1)S(1)}, u32[]{:S(2)}) copy-start(bf16[16,640,640]{1,2,0:T(8,128)(2,1)S(1)} %divide_convert_fusion) | copy-start | bytes 39321604
  154.6 16.3 %copy-start.15 = (u32[128]{0:T(128)S(1)}, u32[128]{0:T(128)}, u32[]{:S(2)}) copy-start(u32[128]{0:T(128)} %constant.63) | copy-start | bytes 1540
  154.6 17.5 %copy-start.13 = (f32[16]{0:T(128)S(1)}, f32[16]{0:T(128)}, u32[]{:S(2)}) copy-start(f32[16]{0:T(128)} %param.17) | copy-start | bytes 196
  265.3 16.5 %copy-start.4 = (bf16[640,1024]{0,1:T(8,128)(2,1)S(1)}, bf16[640,1024]{0,1:T(8,128)(2,1)}, u32[]{:S(2)}) copy-start(bf16[640,1024]{0,1:T(8,128)(2,1)} %copy.34) | copy-start | bytes 3932164
  299.0 6.8 %copy-start.14 = (bf16[16,640,64]{1,2,0:T(8,128)(2,1)S(1)}, bf16[16,640,64]{1,2,0:T(8,128)(2,1)}, u32[]{:S(2)}) copy-start(bf16[16,640,64]{1,2,0:T(8,128)(2,1)} %convolution_convert_fusion.5) | copy-start | bytes 3932164
  305.7 6.8 %copy-start.5 = (bf16[16,64,640]{2,1,0:T(8,128)(2,1)S(1)}, bf16[16,64,640]{2,1,0:T(8,128)(2,1)}, u32[]{:S(2)}) copy-start(bf16[16,64,640]{2,1,0:T(8,128)(2,1)} %convolution_convert_fusion.7) | copy-start | bytes 3932164
  305.7 6.8 %copy-start.9 = (s32[800]{0:T(1024)S(1)}, s32[800]{0:T(1024)}, u32[]{:S(2)}) copy-start(s32[800]{0:T(1024)} %copy-done.8) | copy-start | bytes 9604
  327.9 54.0 %all-to-all-start.2 = ((bf16[16,50,2048]{2,1,0:T(8,128)(2,1)}), bf16[16,50,2048]{2,1,0:T(8,128)(2,1)}, u32[]{:S(2)}, u32[]{:S(2)}) async-start(bf16[16,50,2048]{2,1,0:T(8,128)(2,1)} %reshape.171), calls=%async_computation.2 | async-start | bytes 7340032 | tf_op jit(solution)/shard_map/all_to_all | solution.py:167
  333.1 53.4 %copy-start.7 = (s32[640]{0:T(1024)S(1)}, s32[640]{0:T(1024)}, u32[]{:S(2)}) copy-start(s32[640]{0:T(1024)} %copy-done.6) | copy-start | bytes 7684
  386.5 6.5 %copy-start.1 = (bf16[640,2048]{1,0:T(8,128)(2,1)S(1)}, bf16[640,2048]{1,0:T(8,128)(2,1)}, u32[]{:S(2)}) copy-start(bf16[640,2048]{1,0:T(8,128)(2,1)} %param.9) | copy-start | bytes 7864324
Sparse Core Ops, SparseCore 0:
  9.7 69.9 all-gather.4
  81.4 36.5 all-gather.6
  170.3 47.2 all-gather.8

commit v2 on v1

--- a/solution.py
+++ b/solution.py
@@ -118,11 +118,18 @@
     fig_emb = fig_unit.astype(jnp.bfloat16)
     cap_emb = cap_unit.astype(jnp.bfloat16)
     pair_count = fig_slot.shape[0]
-    both_emb = jnp.concatenate([fig_emb, cap_emb], axis=0)
+    weight_hi = loss_cotangent.astype(jnp.bfloat16)
+    weight_lo = (loss_cotangent - weight_hi.astype(jnp.float32)).astype(jnp.bfloat16)
+    weight_rows = jnp.zeros((2, feature_width), jnp.bfloat16)
+    weight_rows = weight_rows.at[0, :pair_count].set(weight_hi).at[1, :pair_count].set(weight_lo)
+    both_emb = jnp.concatenate([fig_emb, cap_emb, weight_rows], axis=0)
     all_both = lax.all_gather(both_emb, "dp", axis=0, tiled=False)
-    all_weight = lax.all_gather(loss_cotangent, "dp", axis=0, tiled=True)
     all_fig = all_both[:, :pair_count].reshape(-1, feature_width)
-    all_cap = all_both[:, pair_count:].reshape(-1, feature_width)
+    all_cap = all_both[:, pair_count : 2 * pair_count].reshape(-1, feature_width)
+    all_weight = (
+        all_both[:, 2 * pair_count, :pair_count].astype(jnp.float32)
+        + all_both[:, 2 * pair_count + 1, :pair_count].astype(jnp.float32)
+    ).reshape(-1)
     logit_mult = logit_scale[0]
     pair_total = all_fig.shape[0]
     first_pair = lax.axis_index("dp") * pair_count

time: 404 us -> 407 us (level)
  waiting for transfers between devices: 104 us -> 144 us
  blocking collectives: 36.5 us -> 0 us
    all_gather x1, waiting for transfers between devices: 8.79 us -> 48.1 us  [body(): all_both = lax.all_gather(both_emb, 'dp', axis=0, tiled=False)]
    unnamed x1 -> x0, blocking collectives: 36.5 us -> none
where the time goes in v2:
time: 407 us; the launch traced here: 403 us
  matrix products  156 us (38%)
  waiting for transfers between devices  144 us (35%)
  local copies, waits for them, and re-layouts  42.1 us (10%)
  other arithmetic  25.9 us (6%)
  starting transfers between devices  20.2 us (5%)
  between operations  15 us (4%)
    dot_general x3, matrix products, attend(): jnp.einsum('qhd,khd->hqk', query_h, key_h, preferred_element_type=jnp.flo...  50.3 us
    all_to_all x1, waiting for transfers between devices, body(): lax.all_to_all(back_rows.reshape(dp_count, capacity, feature_width), 'dp'...  48.3 us
    all_gather x1, waiting for transfers between devices, body(): all_both = lax.all_gather(both_emb, 'dp', axis=0, tiled=False)  48.1 us
    all_to_all x1, waiting for transfers between devices, body(): lax.all_to_all(send_rows.reshape(dp_count, capacity, feature_width), 'dp'...  45.9 us
    dot_general x3, matrix products, attend(): jnp.einsum('hqk,khd->qhd', attn_prob, value_h, preferred_element_type=jnp...  27.3 us
    dot_general x2, matrix products, select_rows_t(): lax.dot_general(onehot, rows, (((0,), (0,)), ((), ())), preferred_element...  17.2 us
    dot_general x2, matrix products, attend(): return jnp.dot(mixed, out_mat, preferred_element_type=jnp.float32)  16 us
    dot_general x2, matrix products, attend(): jnp.dot(slot_row_block, qkv_mat[0], preferred_element_type=jnp.float32)  13.8 us
  transfers between devices with their start and end apart: 6, of which 3 were waited for; matrix products, arithmetic and copies ran while one was open for 20% of the time, Pallas kernels for 0%

profile of v2, /device:TPU:0, one launch (start us, length us, event | category | flops | bytes accessed | tf_op | source)
XLA Modules:
  0.0 402.8 jit_solution(541539569761171642)
XLA Ops:
  12.5 7.1 %all-to-all-start = ((s32[16,1,50]{2,1,0:T(1,128)}), s32[16,1,50]{2,1,0:T(1,128)S(1)}, u32[]{:S(2)}, u32[]{:S(2)}) async-start(s32[16,1,50]{2,1,0:T(1,128)} %select_n.51), calls=%async_computation | async-start | bytes 16384 | tf_op jit(solution)/shard_map/all_to_all | solution.py:96
  23.8 4.7 %reshape.247 = bf16[16,50,2048]{2,1,0:T(8,128)(2,1)} reshape(bf16[800,2048]{1,0:T(8,128)(2,1)} %convolution_convert_fusion.1) | data formatting | bytes 6553600 | tf_op jit(solution)/shard_map/reshape | solution.py:90
  28.6 7.6 %all-to-all-start.1 = ((bf16[16,50,2048]{2,1,0:T(8,128)(2,1)}), bf16[16,50,2048]{2,1,0:T(8,128)(2,1)}, u32[]{:S(2)}, u32[]{:S(2)}) async-start(bf16[16,50,2048]{2,1,0:T(8,128)(2,1)} %reshape.247), calls=%async_computation.1 | async-start | bytes 7340032 | tf_op jit(solution)/shard_map/all_to_all | solution.py:89
  39.0 45.9 %all-to-all-done.1 = bf16[16,50,2048]{2,1,0:T(8,128)(2,1)} async-done(((bf16[16,50,2048]{2,1,0:T(8,128)(2,1)}), bf16[16,50,2048]{2,1,0:T(8,128)(2,1)}, u32[]{:S(2)}, u32[]{:S(2)}) %all-to-all-start.1) | async-done | bytes 3276832 | tf_op jit(solution)/shard_map/all_to_all | solution.py:89
  89.6 5.2 %convolution_convert_fusion.3 = bf16[640,2048]{1,0:T(8,128)(2,1)S(1)} fusion(bf16[800,2048]{1,0:T(8,128)(2,1)} %reshape.248, s32[800]{0:T(1024)S(1)} %eq.103), kind=kOutput, calls=%fused_computation.28 | convolution fusion | flops 2098974720 | bytes 5901440 | tf_op jit(solution)/shard_map/dot_general | solution.py:48
  94.9 7.0 %fusion.21 = bf16[640,1024]{1,0:T(8,128)(2,1)} fusion(bf16[640,2048]{1,0:T(8,128)(2,1)S(1)} %convolution_convert_fusion.3, bf16[3,2048,1024]{2,1,0:T(8,128)(2,1)} %all-gather.6.cloned.1.call-done), kind=kOutput, calls=%fused_computation.44 | convolution fusion | flops 2685009920 | bytes 8126464 | tf_op jit(solution)/shard_map/jvp()/dot_general | solution.py:21
  104.4 6.1 %fusion.20 = bf16[640,1024]{1,0:T(8,128)(2,1)} fusion(bf16[640,2048]{1,0:T(8,128)(2,1)S(1)} %convolution_convert_fusion.3, bf16[3,2048,1024]{2,1,0:T(8,128)(2,1)} %all-gather.6.cloned.1.call-done), kind=kOutput, calls=%fused_computation.43 | convolution fusion | flops 2685009920 | bytes 8126464 | tf_op jit(solution)/shard_map/jvp()/dot_general | solution.py:26
  112.9 6.1 %fusion.22 = bf16[640,1024]{1,0:T(8,128)(2,1)} fusion(bf16[640,2048]{1,0:T(8,128)(2,1)S(1)} %convolution_convert_fusion.3, bf16[3,2048,1024]{2,1,0:T(8,128)(2,1)} %all-gather.6.cloned.1.call-done), kind=kOutput, calls=%fused_computation.45 | convolution fusion | flops 2685009920 | bytes 8126464 | tf_op jit(solution)/shard_map/jvp()/dot_general | solution.py:31
  120.9 16.6 %fusion.60 = (f32[16,640]{1,0:T(8,128)S(1)}, f32[16,640,640]{1,2,0:T(8,128)}) fusion(bf16[640,16,64]{0,2,1:T(8,128)(2,1)} %bitcast.124, bf16[640,16,64]{0,2,1:T(8,128)(2,1)} %bitcast.126, pred[640,640]{0,1:T(8,128)(4,1)S(1)} %broadcast_compare_fusion), kind=kOutput, calls=%fused_computation.127 | convolution fusion | flops 858511360 | bytes 29286400 | tf_op jit(solution)/shard_map/jvp(qhd,khd->hqk)/dot_general | solution.py:35
  137.6 10.1 %divide_convert_fusion = bf16[16,640,640]{1,2,0:T(8,128)(2,1)S(1)} fusion(f32[16,640,640]{1,2,0:T(8,128)} %get-tuple-element.41, f32[16,640]{1,0:T(8,128)S(1)} %get-tuple-element.40), kind=kLoop, calls=%fused_computation.12 | loop fusion | flops 13107200 | bytes 39362560 | tf_op jit(solution)/shard_map/jvp()/convert_element_type | solution.py:41
  154.8 8.2 %convert_add_fusion = f32[640,2048]{1,0:T(8,128)} fusion(bf16[640,2048]{1,0:T(8,128)(2,1)} %copy-done.3, bf16[640,1024]{0,1:T(8,128)(2,1)S(1)} %bitcast.119, bf16[1024,2048]{1,0:T(8,128)(2,1)} %all-gather.8.cloned.1.call-done), kind=kOutput, calls=%fused_computation.16 | convolution fusion | flops 2686976000 | bytes 13369344 | tf_op jit(solution)/shard_map/jvp()/dot_general | solution.py:44
  171.1 48.1 %all-gather.10.cloned.1.call-done = bf16[16,34,2048]{2,1,0:T(8,128)(2,1)} async-done(((bf16[1,34,2048]{2,1,0:T(8,128)(2,1)}), bf16[16,34,2048]{2,1,0:T(8,128)(2,1)}) %all-gather.10.cloned.1.call-update) | async-done | bytes 2228240 | tf_op jit(solution)/shard_map/all_gather | solution.py:126
  227.8 5.6 %scatter_custom_fusion.1 = f32[640,2048]{1,0:T(8,128)} fusion(f32[640,2048]{1,0:T(8,128)} %scatter_custom_fusion, s32[16]{0:T(128)S(1)} %compare_select_fusion, f32[16,2048]{1,0:T(8,128)S(1)} %get-tuple-element.46, f32[16,2048]{1,0:T(8,128)S(1)} %gather_fusion.1, f32[16]{0:T(128)S(1)} %get-tuple-element.45, f32[16]{0:T(128)S(1)} %add_rsqrt_fusion), kind=kCustom, calls=%fused_computation.68 | custom fusion | flops 163840 | bytes 5506048 | tf_op jit(solution)/shard_map/scatter-add | solution.py:169
  233.4 7.7 %fusion.61 = bf16[640,1024]{1,0:T(8,128)(2,1)} fusion(f32[640,2048]{1,0:T(8,128)} %scatter_custom_fusion.1, bf16[1024,2048]{1,0:T(8,128)(2,1)} %all-gather.8.cloned.1.call-done), kind=kOutput, calls=%fused_computation.128 | convolution fusion | flops 2684354560 | bytes 10747904 | tf_op jit(solution)/shard_map/transpose(jvp())/dot_general | solution.py:44
  243.0 10.0 %convolution_convert_fusion.7 = bf16[16,64,640]{2,1,0:T(8,128)(2,1)} fusion(bf16[16,64,640]{2,1,0:T(8,128)(2,1)S(1)} %bitcast.117, bf16[16,640,640]{1,2,0:T(8,128)(2,1)} %copy-done.2), kind=kOutput, calls=%fused_computation.48 | convolution fusion | flops 839516160 | bytes 15728640 | tf_op jit(solution)/shard_map/transpose(jvp(hqk,khd->qhd))/dot_general | solution.py:42
  253.1 15.0 %fusion.5 = (f32[16,640]{1,0:T(8,128)S(1)}, bf16[16,640,640]{1,2,0:T(8,128)(2,1)}) fusion(f32[16,640,640]{1,2,0:T(8,128)} %get-tuple-element.41, f32[16,640]{1,0:T(8,128)S(1)} %multiply_divide_fusion, bf16[16,64,640]{2,1,0:T(8,128)(2,1)S(1)} %bitcast.118, bf16[640,16,64]{0,2,1:T(8,128)(2,1)S(1)} %bitcast.116), kind=kOutput, calls=%fused_computation.11 | convolution fusion | flops 871618560 | bytes 42024960 | tf_op jit(solution)/shard_map/transpose(jvp(hqk,khd->qhd))/dot_general | solution.py:42
  268.0 16.5 %convolution_convert_fusion.6 = bf16[16,640,64]{1,2,0:T(8,128)(2,1)S(1)} fusion(bf16[640,16,64]{0,2,1:T(8,128)(2,1)} %bitcast.125, f32[16,640,640]{1,2,0:T(8,128)} %get-tuple-element.41, bf16[16,640,640]{1,2,0:T(8,128)(2,1)} %get-tuple-element.48, f32[16,640]{1,0:T(8,128)S(1)} %neg.6, f32[16,640]{1,0:T(8,128)S(1)} %get-tuple-element.40, ...), kind=kOutput, calls=%fused_computation.47 | convolution fusion | flops 878837760 | bytes 42434560 | tf_op jit(solution)/shard_map/transpose(jvp(qhd,khd->hqk))/dot_general | solution.py:35
  284.5 17.1 %convolution_convert_fusion.5 = bf16[16,640,64]{1,2,0:T(8,128)(2,1)} fusion(bf16[640,16,64]{0,2,1:T(8,128)(2,1)S(1)} %bitcast.127, f32[16,640,640]{1,2,0:T(8,128)} %get-tuple-element.41, bf16[16,640,640]{1,2,0:T(8,128)(2,1)} %get-tuple-element.48, f32[16,640]{1,0:T(8,128)S(1)} %neg.6, f32[16,640]{1,0:T(8,128)S(1)} %get-tuple-element.40, ...), kind=kOutput, calls=%fused_computation.46 | convolution fusion | flops 878837760 | bytes 42434560 | tf_op jit(solution)/shard_map/transpose(jvp(qhd,khd->hqk))/dot_general | solution.py:35
  301.7 6.8 %fusion.12 = bf16[640,2048]{1,0:T(8,128)(2,1)} fusion(bf16[640,1024]{0,1:T(8,128)(2,1)S(1)} %bitcast.131, bf16[3,2048,1024]{2,1,0:T(8,128)(2,1)} %all-gather.6.cloned.1.call-done), kind=kOutput, calls=%fused_computation.29 | convolution fusion | flops 2685665280 | bytes 8126464 | tf_op jit(solution)/shard_map/transpose(jvp())/dot_general | solution.py:26
  308.5 6.8 %fusion.13 = bf16[640,2048]{1,0:T(8,128)(2,1)} fusion(bf16[640,1024]{0,1:T(8,128)(2,1)S(1)} %bitcast.132, bf16[3,2048,1024]{2,1,0:T(8,128)(2,1)} %all-gather.6.cloned.1.call-done), kind=kOutput, calls=%fused_computation.30 | convolution fusion | flops 2685665280 | bytes 8126464 | tf_op jit(solution)/shard_map/transpose(jvp())/dot_general | solution.py:21
  315.2 10.7 %convolution_convert_fusion.2 = bf16[800,2048]{1,0:T(8,128)(2,1)} fusion(f32[640,2048]{1,0:T(8,128)} %scatter_custom_fusion.1, bf16[640,2048]{1,0:T(8,128)(2,1)} %fusion.13, bf16[640,2048]{1,0:T(8,128)(2,1)} %fusion.12, s32[800]{0:T(1024)S(1)} %copy-done.9, bf16[640,1024]{0,1:T(8,128)(2,1)S(1)} %bitcast.128, ...), kind=kOutput, calls=%fused_computation.27 | convolution fusion | flops 4791521280 | bytes 19270784 | tf_op jit(solution)/shard_map/dot_general | solution.py:53
  330.6 5.2 %all-to-all-start.2 = ((bf16[16,50,2048]{2,1,0:T(8,128)(2,1)}), bf16[16,50,2048]{2,1,0:T(8,128)(2,1)}, u32[]{:S(2)}, u32[]{:S(2)}) async-start(bf16[16,50,2048]{2,1,0:T(8,128)(2,1)} %reshape.261), calls=%async_computation.2 | async-start | bytes 7340032 | tf_op jit(solution)/shard_map/all_to_all | solution.py:174
  336.5 48.3 %all-to-all-done.2 = bf16[16,50,2048]{2,1,0:T(8,128)(2,1)} async-done(((bf16[16,50,2048]{2,1,0:T(8,128)(2,1)}), bf16[16,50,2048]{2,1,0:T(8,128)(2,1)}, u32[]{:S(2)}, u32[]{:S(2)}) %all-to-all-start.2) | async-done | bytes 3276832 | tf_op jit(solution)/shard_map/all_to_all | solution.py:174
  389.5 6.5 %convolution_convert_fusion.4 = bf16[640,2048]{1,0:T(8,128)(2,1)} fusion(bf16[800,2048]{1,0:T(8,128)(2,1)} %reshape.262, s32[640]{0:T(1024)S(1)} %copy-done.7), kind=kOutput, calls=%fused_computation.32 | convolution fusion | flops 2098974720 | bytes 5900800 | tf_op jit(solution)/shard_map/dot_general | solution.py:53
  (94 shorter events, 58.7 us)
Async XLA Ops:
  7.2 12.5 %copy-start = (bf16[640,2048]{1,0:T(8,128)(2,1)S(1)}, bf16[640,2048]{1,0:T(8,128)(2,1)}, u32[]{:S(2)}) copy-start(bf16[640,2048]{1,0:T(8,128)(2,1)} %param.13) | copy-start | bytes 7864324
  7.2 87.7 %all-gather.6.cloned.1.call-start = ((), (), s32[]{:S(2)}) async-start(), calls=%async_computation.3 | async-start | bytes 14155776 | tf_op jit(solution)/shard_map/all_gather | solution.py:102
  11.2 12.6 %copy-start.6 = (s32[640]{0:T(1024)}, s32[640]{0:T(1024)S(1)}, u32[]{:S(2)}) copy-start(s32[640]{0:T(1024)S(1)} %get-tuple-element.32) | copy-start | bytes 7684
  12.5 16.0 %all-to-all-start = ((s32[16,1,50]{2,1,0:T(1,128)}), s32[16,1,50]{2,1,0:T(1,128)S(1)}, u32[]{:S(2)}, u32[]{:S(2)}) async-start(s32[16,1,50]{2,1,0:T(1,128)} %select_n.51), calls=%async_computation | async-start | bytes 16384 | tf_op jit(solution)/shard_map/all_to_all | solution.py:96
  28.5 8.6 %copy-start.10 = (s32[1,640]{1,0:T(1,128)S(1)}, s32[1,640]{1,0:T(1,128)}, u32[]{:S(2)}) copy-start(s32[1,640]{1,0:T(1,128)} %param.15) | copy-start | bytes 7684
  28.5 8.6 %copy-start.11 = (f32[16]{0:T(128)S(1)}, f32[16]{0:T(128)}, u32[]{:S(2)}) copy-start(f32[16]{0:T(128)} %param.21) | copy-start | bytes 196
  28.5 8.8 %copy-start.12 = (s32[16]{0:T(128)S(1)}, s32[16]{0:T(128)}, u32[]{:S(2)}) copy-start(s32[16]{0:T(128)} %param.19) | copy-start | bytes 196
  28.5 8.9 %copy-start.13 = (s32[16]{0:T(128)S(1)}, s32[16]{0:T(128)}, u32[]{:S(2)}) copy-start(s32[16]{0:T(128)} %param.18) | copy-start | bytes 196
  28.6 56.4 %all-to-all-start.1 = ((bf16[16,50,2048]{2,1,0:T(8,128)(2,1)}), bf16[16,50,2048]{2,1,0:T(8,128)(2,1)}, u32[]{:S(2)}, u32[]{:S(2)}) async-start(bf16[16,50,2048]{2,1,0:T(8,128)(2,1)} %reshape.247), calls=%async_computation.1 | async-start | bytes 7340032 | tf_op jit(solution)/shard_map/all_to_all | solution.py:89
  36.2 118.6 %all-gather.8.cloned.1.call-start = ((), (), s32[]{:S(2)}) async-start(), calls=%async_computation.4 | async-start | bytes 4718592 | tf_op jit(solution)/shard_map/all_gather | solution.py:103
  36.9 182.3 %all-gather.10.cloned.1.call-start = ((), (), s32[]{:S(2)}) async-start(), calls=%async_computation.5 | async-start | bytes 2785280 | tf_op jit(solution)/shard_map/all_gather | solution.py:126
  39.0 50.6 %copy-start.8 = (s32[800]{0:T(1024)}, s32[800]{0:T(1024)S(1)}, u32[]{:S(2)}) copy-start(s32[800]{0:T(1024)S(1)} %eq.103) | copy-start | bytes 9604
  94.8 18.1 %copy-start.3 = (bf16[640,2048]{1,0:T(8,128)(2,1)}, bf16[640,2048]{1,0:T(8,128)(2,1)S(1)}, u32[]{:S(2)}) copy-start(bf16[640,2048]{1,0:T(8,128)(2,1)S(1)} %convolution_convert_fusion.3) | copy-start | bytes 7864324
  147.7 4.7 %copy-start.2 = (bf16[16,640,640]{1,2,0:T(8,128)(2,1)}, bf16[16,640,640]{1,2,0:T(8,128)(2,1)S(1)}, u32[]{:S(2)}) copy-start(bf16[16,640,640]{1,2,0:T(8,128)(2,1)S(1)} %divide_convert_fusion) | copy-start | bytes 39321604
  268.0 16.5 %copy-start.4 = (bf16[640,1024]{0,1:T(8,128)(2,1)S(1)}, bf16[640,1024]{0,1:T(8,128)(2,1)}, u32[]{:S(2)}) copy-start(bf16[640,1024]{0,1:T(8,128)(2,1)} %copy.43) | copy-start | bytes 3932164
  301.7 6.8 %copy-start.14 = (bf16[16,640,64]{1,2,0:T(8,128)(2,1)S(1)}, bf16[16,640,64]{1,2,0:T(8,128)(2,1)}, u32[]{:S(2)}) copy-start(bf16[16,640,64]{1,2,0:T(8,128)(2,1)} %convolution_convert_fusion.5) | copy-start | bytes 3932164
  308.5 6.8 %copy-start.5 = (bf16[16,64,640]{2,1,0:T(8,128)(2,1)S(1)}, bf16[16,64,640]{2,1,0:T(8,128)(2,1)}, u32[]{:S(2)}) copy-start(bf16[16,64,640]{2,1,0:T(8,128)(2,1)} %convolution_convert_fusion.7) | copy-start | bytes 3932164
  308.5 6.8 %copy-start.9 = (s32[800]{0:T(1024)S(1)}, s32[800]{0:T(1024)}, u32[]{:S(2)}) copy-start(s32[800]{0:T(1024)} %copy-done.8) | copy-start | bytes 9604
  330.6 54.2 %all-to-all-start.2 = ((bf16[16,50,2048]{2,1,0:T(8,128)(2,1)}), bf16[16,50,2048]{2,1,0:T(8,128)(2,1)}, u32[]{:S(2)}, u32[]{:S(2)}) async-start(bf16[16,50,2048]{2,1,0:T(8,128)(2,1)} %reshape.261), calls=%async_computation.2 | async-start | bytes 7340032 | tf_op jit(solution)/shard_map/all_to_all | solution.py:174
  336.5 53.0 %copy-start.7 = (s32[640]{0:T(1024)S(1)}, s32[640]{0:T(1024)}, u32[]{:S(2)}) copy-start(s32[640]{0:T(1024)} %copy-done.6) | copy-start | bytes 7684
  389.5 6.5 %copy-start.1 = (bf16[640,2048]{1,0:T(8,128)(2,1)S(1)}, bf16[640,2048]{1,0:T(8,128)(2,1)}, u32[]{:S(2)}) copy-start(bf16[640,2048]{1,0:T(8,128)(2,1)} %param.13) | copy-start | bytes 7864324
Sparse Core Ops, SparseCore 0:
  9.7 69.9 all-gather.5
  81.4 36.5 all-gather.7
  170.5 48.6 all-gather.9

commit v3 on v2

--- a/solution.py
+++ b/solution.py
@@ -15,12 +15,13 @@
     return jnp.log(jnp.sum(jnp.exp(values), axis=axis))
 
 
-def attend(slot_row_block, qkv_mat, out_mat, doc_row):
+def attend(query_rows, slot_row_block, qkv_mat, out_mat, query_doc, doc_row):
+    query_count = query_rows.shape[0]
     row_count = slot_row_block.shape[0]
     query_h = (
-        jnp.dot(slot_row_block, qkv_mat[0], preferred_element_type=jnp.float32)
+        jnp.dot(query_rows, qkv_mat[0], preferred_element_type=jnp.float32)
         .astype(jnp.bfloat16)
-        .reshape(row_count, -1, HD)
+        .reshape(query_count, -1, HD)
     )
     key_h = (
         jnp.dot(slot_row_block, qkv_mat[1], preferred_element_type=jnp.float32)
@@ -35,12 +36,12 @@
     scores = jnp.einsum("qhd,khd->hqk", query_h, key_h, preferred_element_type=jnp.float32) * (
         1.0 / math.sqrt(HD)
     )
-    same_doc = doc_row[:, None] == doc_row[None, :]
+    same_doc = query_doc[:, None] == doc_row[None, :]
     scores = jnp.where(same_doc[None], scores, -1e30)
     weights = jnp.exp(scores)
     attn_prob = (weights / jnp.sum(weights, axis=2, keepdims=True)).astype(jnp.bfloat16)
     mixed = jnp.einsum("hqk,khd->qhd", attn_prob, value_h, preferred_element_type=jnp.float32)
-    mixed = mixed.astype(jnp.bfloat16).reshape(row_count, -1)
+    mixed = mixed.astype(jnp.bfloat16).reshape(query_count, -1)
     return jnp.dot(mixed, out_mat, preferred_element_type=jnp.float32)
 
 
@@ -103,21 +104,29 @@
         lax.all_gather(out_weight, "fsdp", axis=1, tiled=True),
     )
     doc_row = doc_ids[0]
+    pair_count = fig_slot.shape[0]
+    query_slots = jnp.concatenate([fig_slot, cap_slot], axis=0)
+    query_onehot = (query_slots[:, None] == jnp.arange(row_count)[None, :]).astype(jnp.bfloat16)
+    query_doc = jnp.sum(
+        jnp.where(query_slots[:, None] == jnp.arange(row_count)[None, :], doc_row[None, :], 0),
+        axis=1,
+    )
 
     def branch(inputs):
-        return attend(inputs, qkv_full, out_full, doc_row)
+        picked = select_rows(query_onehot, inputs)
+        return attend(picked, inputs, qkv_full, out_full, query_doc, doc_row)
 
     attn_out, pullback = jax.vjp(branch, slot_row_block)
-    slot_output = slot_row_block.astype(jnp.float32) + attn_out
-    fig_vec = slot_output[fig_slot]
-    cap_vec = slot_output[cap_slot]
+    query_rows = select_rows(query_onehot, slot_row_block)
+    query_output = query_rows.astype(jnp.float32) + attn_out
+    fig_vec = query_output[:pair_count]
+    cap_vec = query_output[pair_count:]
     fig_inv = lax.rsqrt(jnp.sum(fig_vec * fig_vec, axis=1, keepdims=True) + EPSILON)
     cap_inv = lax.rsqrt(jnp.sum(cap_vec * cap_vec, axis=1, keepdims=True) + EPSILON)
     fig_unit = fig_vec * fig_inv
     cap_unit = cap_vec * cap_inv
     fig_emb = fig_unit.astype(jnp.bfloat16)
     cap_emb = cap_unit.astype(jnp.bfloat16)
-    pair_count = fig_slot.shape[0]
     weight_hi = loss_cotangent.astype(jnp.bfloat16)
     weight_lo = (loss_cotangent - weight_hi.astype(jnp.float32)).astype(jnp.bfloat16)
     weight_rows = jnp.zeros((2, feature_width), jnp.bfloat16)
@@ -161,14 +170,14 @@
     caption_direction = cap_inv * (
         cap_grad - cap_unit * jnp.sum(cap_unit * cap_grad, axis=1, keepdims=True)
     )
-    slot_ct = (
-        jnp.zeros((row_count, feature_width), jnp.float32)
-        .at[fig_slot]
-        .add(figure_direction)
-        .at[cap_slot]
-        .add(caption_direction)
-    )
-    branch_ct = pullback(slot_ct)[0]
+    query_ct = jnp.concatenate([figure_direction, caption_direction], axis=0)
+    slot_ct = lax.dot_general(
+        query_onehot.astype(jnp.float32),
+        query_ct,
+        (((0,), (0,)), ((), ())),
+        precision=lax.Precision.HIGHEST,
+    )
+    branch_ct = pullback(query_ct)[0]
     slot_gradient = (slot_ct + branch_ct.astype(jnp.float32)).astype(jnp.bfloat16)
     back_rows = select_rows_t(recv_onehot, slot_gradient)
     home_rows = lax.all_to_all(

time: 407 us -> 287 us (0.71)
  matrix products: 156 us -> 70.9 us
  other arithmetic: 25.9 us -> 6.69 us
  local copies, waits for them, and re-layouts: 42.1 us -> 29.2 us
    dot_general x3, matrix products: 50.3 us -> 1.74 us  [attend(): jnp.einsum('qhd,khd->hqk', query_h, key_h, preferred_element_type=jnp.flo...]
    dot_general x3, matrix products: 27.3 us -> 4.07 us  [attend(): jnp.einsum('hqk,khd->qhd', attn_prob, value_h, preferred_element_type=jnp...]
    dot_general x2, matrix products: 16 us -> 4.34 us  [attend(): return jnp.dot(mixed, out_mat, preferred_element_type=jnp.float32)]
    convert_element_type x2 -> x1, other arithmetic: 10.2 us -> 0.09 us  [body(): fig_emb = fig_unit.astype(jnp.bfloat16)]
    scatter-add x2 -> x0, other arithmetic: 9.06 us -> none  [body(): slot_ct = jnp.zeros((row_count, feature_width), jnp.float32).at[fig_slot]...]
    dot_general x2, matrix products: 13.8 us -> 5.46 us  [the longest x1 3.01 us: attend(): jnp.dot(query_rows, qkv_mat[0], preferred_element_type=jnp.float32)]
    dot_general x1 -> x2, matrix products: 6.11 us -> 13 us  [attend(): jnp.dot(slot_row_block, qkv_mat[2], preferred_element_type=jnp.float32)]
    dot_general x2, matrix products: 17.2 us -> 10.7 us  [select_rows_t(): lax.dot_general(onehot, rows, (((0,), (0,)), ((), ())), preferred_element...]
  transfers between devices with their start and end apart: 6 -> 6, of which waited for: 3 -> 3; matrix products, arithmetic and copies ran while one was open for 20% -> 17% of each run, Pallas kernels for 0% -> 0%
where the time goes in v3:
time: 287 us; the launch traced here: 285 us
  waiting for transfers between devices  144 us (50%)
  matrix products  70.9 us (25%)
  local copies, waits for them, and re-layouts  29.2 us (10%)
  starting transfers between devices  19.4 us (7%)
  between operations  14.8 us (5%)
  other arithmetic  6.69 us (2%)
    all_to_all x1, waiting for transfers between devices, body(): lax.all_to_all(back_rows.reshape(dp_count, capacity, feature_width), 'dp'...  48.4 us
    all_gather x1, waiting for transfers between devices, body(): all_both = lax.all_gather(both_emb, 'dp', axis=0, tiled=False)  47.7 us
    all_to_all x1, waiting for transfers between devices, body(): lax.all_to_all(send_rows.reshape(dp_count, capacity, feature_width), 'dp'...  47 us
    dot_general x4, matrix products, select_rows(): picked = jnp.dot(onehot, rows, preferred_element_type=jnp.float32)  15.7 us
    dot_general x2, matrix products, attend(): jnp.dot(slot_row_block, qkv_mat[2], preferred_element_type=jnp.float32)  13 us
    dot_general x2, matrix products, attend(): jnp.dot(slot_row_block, qkv_mat[1], preferred_element_type=jnp.float32)  12.9 us
    dot_general x2, matrix products, select_rows_t(): lax.dot_general(onehot, rows, (((0,), (0,)), ((), ())), preferred_element...  10.7 us
    all_to_all x1, starting transfers between devices, body(): lax.all_to_all(send_rows.reshape(dp_count, capacity, feature_width), 'dp'...  7.28 us
  transfers between devices with their start and end apart: 6, of which 3 were waited for; matrix products, arithmetic and copies ran while one was open for 17% of the time, Pallas kernels for 0%

profile of v3, /device:TPU:0, one launch (start us, length us, event | category | flops | bytes accessed | tf_op | source)
XLA Modules:
  0.0 285.4 jit_solution(14935274900330503738)
XLA Ops:
  13.2 7.1 %all-to-all-start = ((s32[16,1,50]{2,1,0:T(1,128)}), s32[16,1,50]{2,1,0:T(1,128)S(1)}, u32[]{:S(2)}, u32[]{:S(2)}) async-start(s32[16,1,50]{2,1,0:T(1,128)} %select_n.47), calls=%async_computation | async-start | bytes 16384 | tf_op jit(solution)/shard_map/all_to_all | solution.py:97
  20.4 4.1 %convolution_convert_fusion = bf16[800,2048]{1,0:T(8,128)(2,1)} fusion(bf16[640,2048]{1,0:T(8,128)(2,1)S(1)} %copy-done, s32[640]{0:T(1024)S(1)} %get-tuple-element.40), kind=kOutput, calls=%fused_computation.10 | convolution fusion | flops 2099302400 | bytes 5900800 | tf_op jit(solution)/shard_map/dot_general | solution.py:49
  24.4 4.9 %reshape.246 = bf16[16,50,2048]{2,1,0:T(8,128)(2,1)} reshape(bf16[800,2048]{1,0:T(8,128)(2,1)} %convolution_convert_fusion) | data formatting | bytes 6553600 | tf_op jit(solution)/shard_map/reshape | solution.py:91
  29.4 7.3 %all-to-all-start.1 = ((bf16[16,50,2048]{2,1,0:T(8,128)(2,1)}), bf16[16,50,2048]{2,1,0:T(8,128)(2,1)}, u32[]{:S(2)}, u32[]{:S(2)}) async-start(bf16[16,50,2048]{2,1,0:T(8,128)(2,1)} %reshape.246), calls=%async_computation.1 | async-start | bytes 7340032 | tf_op jit(solution)/shard_map/all_to_all | solution.py:90
  38.6 47.0 %all-to-all-done.1 = bf16[16,50,2048]{2,1,0:T(8,128)(2,1)} async-done(((bf16[16,50,2048]{2,1,0:T(8,128)(2,1)}), bf16[16,50,2048]{2,1,0:T(8,128)(2,1)}, u32[]{:S(2)}, u32[]{:S(2)}) %all-to-all-start.1) | async-done | bytes 3276832 | tf_op jit(solution)/shard_map/all_to_all | solution.py:90
  85.6 4.7 %reshape.247 = bf16[800,2048]{1,0:T(8,128)(2,1)} reshape(bf16[16,50,2048]{2,1,0:T(8,128)(2,1)} %all-to-all-done.1) | data formatting | bytes 6553600 | tf_op jit(solution)/shard_map/reshape | solution.py:101
  90.3 5.2 %convolution_convert_fusion.2 = bf16[640,2048]{1,0:T(8,128)(2,1)S(1)} fusion(bf16[800,2048]{1,0:T(8,128)(2,1)} %reshape.247, s32[800]{0:T(1024)S(1)} %eq.119), kind=kOutput, calls=%fused_computation.12 | convolution fusion | flops 2098974720 | bytes 5901440 | tf_op jit(solution)/shard_map/dot_general | solution.py:49
  96.1 3.0 %fusion.25 = bf16[32,1024]{1,0:T(8,128)(2,1)S(1)} fusion(bf16[32,2048]{1,0:T(8,128)(2,1)S(1)} %convolution_convert_fusion.5, bf16[3,2048,1024]{2,1,0:T(8,128)(2,1)} %all-gather.6.cloned.1.call-done), kind=kOutput, calls=%fused_computation.51 | convolution fusion | flops 134250496 | bytes 4390912 | tf_op jit(solution)/shard_map/jvp()/dot_general | solution.py:22
  99.3 6.1 %fusion.12 = bf16[640,1024]{1,0:T(8,128)(2,1)} fusion(bf16[640,2048]{1,0:T(8,128)(2,1)S(1)} %convolution_convert_fusion.2, bf16[3,2048,1024]{2,1,0:T(8,128)(2,1)} %all-gather.6.cloned.1.call-done), kind=kOutput, calls=%fused_computation.30 | convolution fusion | flops 2685009920 | bytes 8126464 | tf_op jit(solution)/shard_map/jvp()/dot_general | solution.py:32
  105.4 2.4 copy.35
  107.8 6.2 %fusion.11 = bf16[640,1024]{1,0:T(8,128)(2,1)} fusion(bf16[640,2048]{1,0:T(8,128)(2,1)S(1)} %convolution_convert_fusion.2, bf16[3,2048,1024]{2,1,0:T(8,128)(2,1)} %all-gather.6.cloned.1.call-done), kind=kOutput, calls=%fused_computation.29 | convolution fusion | flops 2685009920 | bytes 8126464 | tf_op jit(solution)/shard_map/jvp()/dot_general | solution.py:27
  114.1 1.9 copy.36
  118.7 3.0 %convolution_add_fusion = f32[32,2048]{1,0:T(8,128)S(1)} fusion(bf16[32,1024]{1,0:T(8,128)(2,1)S(1)} %reshape.251, bf16[1024,2048]{1,0:T(8,128)(2,1)} %all-gather.8.cloned.1.call-done, bf16[32,2048]{1,0:T(8,128)(2,1)S(1)} %convolution_convert_fusion.5), kind=kOutput, calls=%fused_computation.19 | convolution fusion | flops 134348800 | bytes 4653056 | tf_op jit(solution)/shard_map/jvp()/dot_general | solution.py:45
  123.3 47.7 %all-gather.10.cloned.1.call-done = bf16[16,34,2048]{2,1,0:T(8,128)(2,1)} async-done(((bf16[1,34,2048]{2,1,0:T(8,128)(2,1)}), bf16[16,34,2048]{2,1,0:T(8,128)(2,1)}) %all-gather.10.cloned.1.call-update) | async-done | bytes 2228240 | tf_op jit(solution)/shard_map/all_gather | solution.py:135
  182.9 6.7 %fusion.6 = bf16[640,2048]{1,0:T(8,128)(2,1)} fusion(bf16[640,1024]{0,1:T(8,128)(2,1)S(1)} %bitcast.119, bf16[3,2048,1024]{2,1,0:T(8,128)(2,1)} %all-gather.6.cloned.1.call-done), kind=kOutput, calls=%fused_computation.14 | convolution fusion | flops 2685665280 | bytes 8126464 | tf_op jit(solution)/shard_map/transpose(jvp())/dot_general | solution.py:27
  189.7 6.8 %fusion.7 = bf16[640,2048]{1,0:T(8,128)(2,1)} fusion(bf16[640,1024]{0,1:T(8,128)(2,1)S(1)} %bitcast.120, bf16[3,2048,1024]{2,1,0:T(8,128)(2,1)} %all-gather.6.cloned.1.call-done), kind=kOutput, calls=%fused_computation.15 | convolution fusion | flops 2685665280 | bytes 8126464 | tf_op jit(solution)/shard_map/transpose(jvp())/dot_general | solution.py:32
  196.5 5.8 %fusion.8 = bf16[640,2048]{1,0:T(8,128)(2,1)S(1)} fusion(bf16[640,2048]{1,0:T(8,128)(2,1)} %fusion.7, bf16[640,2048]{1,0:T(8,128)(2,1)} %fusion.6, bf16[32,1024]{1,0:T(8,128)(2,1)S(1)} %reshape.259, bf16[3,2048,1024]{2,1,0:T(8,128)(2,1)} %all-gather.6.cloned.1.call-done, s32[32]{0:T(128)S(1)} %pad_add_fusion), kind=kOutput, calls=%fused_computation.17 | convolution fusion | flops 227364864 | bytes 12124288 | tf_op jit(solution)/shard_map/transpose(jvp())/dot_general | solution.py:49
  202.3 2.5 add_convert_fusion
  204.8 4.2 %convolution_convert_fusion.1 = bf16[800,2048]{1,0:T(8,128)(2,1)} fusion(bf16[640,2048]{1,0:T(8,128)(2,1)S(1)} %add_convert_fusion, s32[800]{0:T(1024)S(1)} %eq.119), kind=kOutput, calls=%fused_computation.11 | convolution fusion | flops 2099302400 | bytes 5901440 | tf_op jit(solution)/shard_map/dot_general | solution.py:54
  209.0 4.7 %reshape.260 = bf16[16,50,2048]{2,1,0:T(8,128)(2,1)} reshape(bf16[800,2048]{1,0:T(8,128)(2,1)} %convolution_convert_fusion.1) | data formatting | bytes 6553600 | tf_op jit(solution)/shard_map/reshape | solution.py:184
  213.7 4.9 %all-to-all-start.2 = ((bf16[16,50,2048]{2,1,0:T(8,128)(2,1)}), bf16[16,50,2048]{2,1,0:T(8,128)(2,1)}, u32[]{:S(2)}, u32[]{:S(2)}) async-start(bf16[16,50,2048]{2,1,0:T(8,128)(2,1)} %reshape.260), calls=%async_computation.2 | async-start | bytes 7340032 | tf_op jit(solution)/shard_map/all_to_all | solution.py:183
  219.3 48.4 %all-to-all-done.2 = bf16[16,50,2048]{2,1,0:T(8,128)(2,1)} async-done(((bf16[16,50,2048]{2,1,0:T(8,128)(2,1)}), bf16[16,50,2048]{2,1,0:T(8,128)(2,1)}, u32[]{:S(2)}, u32[]{:S(2)}) %all-to-all-start.2) | async-done | bytes 3276832 | tf_op jit(solution)/shard_map/all_to_all | solution.py:183
  267.7 4.7 %reshape.261 = bf16[800,2048]{1,0:T(8,128)(2,1)} reshape(bf16[16,50,2048]{2,1,0:T(8,128)(2,1)} %all-to-all-done.2) | data formatting | bytes 6553600 | tf_op jit(solution)/shard_map/reshape | solution.py:190
  272.4 6.5 %convolution_convert_fusion.4 = bf16[640,2048]{1,0:T(8,128)(2,1)} fusion(bf16[800,2048]{1,0:T(8,128)(2,1)} %reshape.261, s32[640]{0:T(1024)S(1)} %get-tuple-element.40), kind=kOutput, calls=%fused_computation.16 | convolution fusion | flops 2098974720 | bytes 5900800 | tf_op jit(solution)/shard_map/dot_general | solution.py:54
  (85 shorter events, 24.8 us)
Async XLA Ops:
  7.2 13.2 %copy-start = (bf16[640,2048]{1,0:T(8,128)(2,1)S(1)}, bf16[640,2048]{1,0:T(8,128)(2,1)}, u32[]{:S(2)}) copy-start(bf16[640,2048]{1,0:T(8,128)(2,1)} %param.13) | copy-start | bytes 7864324
  7.2 88.9 %all-gather.6.cloned.1.call-start = ((), (), s32[]{:S(2)}) async-start(), calls=%async_computation.3 | async-start | bytes 14155776 | tf_op jit(solution)/shard_map/all_gather | solution.py:103
  7.9 110.8 %all-gather.8.cloned.1.call-start = ((), (), s32[]{:S(2)}) async-start(), calls=%async_computation.4 | async-start | bytes 4718592 | tf_op jit(solution)/shard_map/all_gather | solution.py:104
  13.2 16.2 %all-to-all-start = ((s32[16,1,50]{2,1,0:T(1,128)}), s32[16,1,50]{2,1,0:T(1,128)S(1)}, u32[]{:S(2)}, u32[]{:S(2)}) async-start(s32[16,1,50]{2,1,0:T(1,128)} %select_n.47), calls=%async_computation | async-start | bytes 16384 | tf_op jit(solution)/shard_map/all_to_all | solution.py:97
  29.4 7.4 %copy-start.6 = (s32[1,640]{1,0:T(1,128)S(1)}, s32[1,640]{1,0:T(1,128)}, u32[]{:S(2)}) copy-start(s32[1,640]{1,0:T(1,128)} %param.15) | copy-start | bytes 7684
  29.4 7.4 %copy-start.7 = (f32[16]{0:T(128)S(1)}, f32[16]{0:T(128)}, u32[]{:S(2)}) copy-start(f32[16]{0:T(128)} %param.21) | copy-start | bytes 196
  29.4 7.6 %copy-start.8 = (s32[16]{0:T(128)S(1)}, s32[16]{0:T(128)}, u32[]{:S(2)}) copy-start(s32[16]{0:T(128)} %param.19) | copy-start | bytes 196
  29.4 7.6 %copy-start.9 = (s32[16]{0:T(128)S(1)}, s32[16]{0:T(128)}, u32[]{:S(2)}) copy-start(s32[16]{0:T(128)} %param.18) | copy-start | bytes 196
  29.4 56.2 %all-to-all-start.1 = ((bf16[16,50,2048]{2,1,0:T(8,128)(2,1)}), bf16[16,50,2048]{2,1,0:T(8,128)(2,1)}, u32[]{:S(2)}, u32[]{:S(2)}) async-start(bf16[16,50,2048]{2,1,0:T(8,128)(2,1)} %reshape.246), calls=%async_computation.1 | async-start | bytes 7340032 | tf_op jit(solution)/shard_map/all_to_all | solution.py:90
  36.7 134.3 %all-gather.10.cloned.1.call-start = ((), (), s32[]{:S(2)}) async-start(), calls=%async_computation.5 | async-start | bytes 2785280 | tf_op jit(solution)/shard_map/all_gather | solution.py:135
  116.0 2.5 copy-start.3
  116.0 1.9 copy-start.5
  174.3 2.2 copy-start.2
  177.8 2.0 copy-start.4
  182.9 6.7 %copy-start.10 = (bf16[16,64,640]{2,1,0:T(8,128)(2,1)S(1)}, bf16[16,64,640]{2,1,0:T(8,128)(2,1)}, u32[]{:S(2)}) copy-start(bf16[16,64,640]{2,1,0:T(8,128)(2,1)} %convolution_convert_fusion.7) | copy-start | bytes 3932164
  213.7 54.0 %all-to-all-start.2 = ((bf16[16,50,2048]{2,1,0:T(8,128)(2,1)}), bf16[16,50,2048]{2,1,0:T(8,128)(2,1)}, u32[]{:S(2)}, u32[]{:S(2)}) async-start(bf16[16,50,2048]{2,1,0:T(8,128)(2,1)} %reshape.260), calls=%async_computation.2 | async-start | bytes 7340032 | tf_op jit(solution)/shard_map/all_to_all | solution.py:183
  272.4 6.5 %copy-start.1 = (bf16[640,2048]{1,0:T(8,128)(2,1)S(1)}, bf16[640,2048]{1,0:T(8,128)(2,1)}, u32[]{:S(2)}) copy-start(bf16[640,2048]{1,0:T(8,128)(2,1)} %param.13) | copy-start | bytes 7864324
Sparse Core Ops, SparseCore 0:
  9.7 69.9 all-gather.5
  81.4 36.5 all-gather.7
  122.8 48.2 all-gather.9

commit v4 on v3

--- a/solution.py
+++ b/solution.py
@@ -79,8 +79,10 @@
     rank_idx = jnp.sum((jnp.cumsum(onehot, axis=0) - onehot) * onehot, axis=1)
     dest = owner_idx * capacity + rank_idx
     send_match = dest[None, :] == jnp.arange(buffer_rows)[:, None]
-    send_onehot = send_match.astype(jnp.bfloat16)
-    send_rows = select_rows(send_onehot, page_embed)
+    send_onehot = send_match.astype(jnp.bfloat16).reshape(dp_count, capacity, row_count)
+    send_rows = jnp.einsum(
+        "opk,kd->opd", send_onehot, page_embed, preferred_element_type=jnp.float32
+    ).astype(jnp.bfloat16)
     send_ids = jnp.where(
         jnp.any(send_match, axis=1),
         jnp.sum(jnp.where(send_match, slot_idx[None, :], 0), axis=1),
@@ -88,7 +90,7 @@
     ).reshape(dp_count, capacity)
     recv_rows, recv_ids = (
         lax.all_to_all(
-            send_rows.reshape(dp_count, capacity, feature_width),
+            send_rows,
             "dp",
             split_axis=0,
             concat_axis=0,
@@ -96,9 +98,12 @@
         ),
         lax.all_to_all(send_ids, "dp", split_axis=0, concat_axis=0, tiled=True),
     )
-    flat_ids = recv_ids.reshape(-1)
-    recv_onehot = (jnp.arange(row_count)[:, None] == flat_ids[None, :]).astype(jnp.bfloat16)
-    slot_row_block = select_rows(recv_onehot, recv_rows.reshape(-1, feature_width))
+    recv_onehot = (
+        jnp.arange(row_count)[:, None, None] == recv_ids[None, :, :]
+    ).astype(jnp.bfloat16)
+    slot_row_block = jnp.einsum(
+        "sop,opd->sd", recv_onehot, recv_rows, preferred_element_type=jnp.float32
+    ).astype(jnp.bfloat16)
     qkv_full, out_full = (
         lax.all_gather(qkv_weight, "fsdp", axis=1, tiled=True),
         lax.all_gather(out_weight, "fsdp", axis=1, tiled=True),
@@ -132,7 +137,14 @@
     weight_rows = jnp.zeros((2, feature_width), jnp.bfloat16)
     weight_rows = weight_rows.at[0, :pair_count].set(weight_hi).at[1, :pair_count].set(weight_lo)
     both_emb = jnp.concatenate([fig_emb, cap_emb, weight_rows], axis=0)
-    all_both = lax.all_gather(both_emb, "dp", axis=0, tiled=False)
+    gathered = [both_emb]
+    for shift in range(1, dp_count):
+        gathered.append(
+            lax.ppermute(
+                both_emb, "dp", perm=[(i, (i - shift) % dp_count) for i in range(dp_count)]
+            )
+        )
+    all_both = jnp.stack(gathered, axis=0)
     all_fig = all_both[:, :pair_count].reshape(-1, feature_width)
     all_cap = all_both[:, pair_count : 2 * pair_count].reshape(-1, feature_width)
     all_weight = (
@@ -141,7 +153,7 @@
     ).reshape(-1)
     logit_mult = logit_scale[0]
     pair_total = all_fig.shape[0]
-    first_pair = lax.axis_index("dp") * pair_count
+    first_pair = 0
     logits = logit_mult * jnp.dot(all_fig, all_cap.T, preferred_element_type=jnp.float32)
     row_lse = log_total(logits, 1)
     col_lse = log_total(logits, 0)
@@ -179,15 +191,13 @@
     )
     branch_ct = pullback(query_ct)[0]
     slot_gradient = (slot_ct + branch_ct.astype(jnp.float32)).astype(jnp.bfloat16)
-    back_rows = select_rows_t(recv_onehot, slot_gradient)
-    home_rows = lax.all_to_all(
-        back_rows.reshape(dp_count, capacity, feature_width),
-        "dp",
-        split_axis=0,
-        concat_axis=0,
-        tiled=True,
-    )
-    page_grad = select_rows_t(send_onehot, home_rows.reshape(-1, feature_width))
+    back_rows = jnp.einsum(
+        "sop,sd->opd", recv_onehot, slot_gradient, preferred_element_type=jnp.float32
+    ).astype(jnp.bfloat16)
+    home_rows = lax.all_to_all(back_rows, "dp", split_axis=0, concat_axis=0, tiled=True)
+    page_grad = jnp.einsum(
+        "opk,opd->kd", send_onehot, home_rows, preferred_element_type=jnp.float32
+    ).astype(jnp.bfloat16)
     return (page_grad, pair_loss)
 
 

time: 287 us -> 286 us (level)
  starting transfers between devices: 19.4 us -> 59 us
  waiting for transfers between devices: 144 us -> 122 us
  local copies, waits for them, and re-layouts: 29.2 us -> 7.5 us
  matrix products: 70.9 us -> 74.8 us
    all_gather x1 -> x0, waiting for transfers between devices: 47.7 us -> none  [body(): all_both = lax.all_gather(both_emb, 'dp', axis=0, tiled=False)]
    ppermute x0 -> x15, starting transfers between devices: none -> 41.5 us  [body(): lax.ppermute(both_emb, 'dp', perm=[(i, (i - shift) % dp_count) for i in r...]
    reshape x4 -> x0, local copies, waits for them, and re-layouts: 19 us -> none  [the longest x1 4.94 us: body(): send_rows.reshape(dp_count, capacity, feature_width)]
    ppermute x0 -> x15, waiting for transfers between devices: none -> 14.6 us  [body(): lax.ppermute(both_emb, 'dp', perm=[(i, (i - shift) % dp_count) for i in r...]
    dot_general x2 -> x4, matrix products: 10.7 us -> 21.1 us  [the longest x1 6.74 us: body(): jnp.einsum('opk,opd->kd', send_onehot, home_rows, preferred_element_type=...]
    all_gather x1, waiting for transfers between devices: 0.02 us -> 9.51 us  [body(): lax.all_gather(out_weight, 'fsdp', axis=1, tiled=True)]
    dot_general x4 -> x2, matrix products: 15.7 us -> 6.64 us  [select_rows(): picked = jnp.dot(onehot, rows, preferred_element_type=jnp.float32)]
  transfers between devices with their start and end apart: 6 -> 20, of which waited for: 3 -> 10; matrix products, arithmetic and copies ran while one was open for 17% -> 13% of each run, Pallas kernels for 0% -> 0%
where the time goes in v4:
time: 286 us; the launch traced here: 283 us
  waiting for transfers between devices  122 us (43%)
  matrix products  74.8 us (26%)
  starting transfers between devices  59 us (21%)
  between operations  15.5 us (5%)
  local copies, waits for them, and re-layouts  7.5 us (3%)
  other arithmetic  4.58 us (2%)
    all_to_all x1, waiting for transfers between devices, body(): lax.all_to_all(send_rows, 'dp', split_axis=0, concat_axis=0, tiled=True)  47.4 us
    all_to_all x1, waiting for transfers between devices, body(): lax.all_to_all(back_rows, 'dp', split_axis=0, concat_axis=0, tiled=True)  46.8 us
    ppermute x15, starting transfers between devices, body(): lax.ppermute(both_emb, 'dp', perm=[(i, (i - shift) % dp_count) for i in r...  41.5 us
    ppermute x15, waiting for transfers between devices, body(): lax.ppermute(both_emb, 'dp', perm=[(i, (i - shift) % dp_count) for i in r...  14.6 us
    dot_general x2, matrix products, attend(): jnp.dot(slot_row_block, qkv_mat[1], preferred_element_type=jnp.float32)  13.6 us
    dot_general x2, matrix products, attend(): jnp.dot(slot_row_block, qkv_mat[2], preferred_element_type=jnp.float32)  12.5 us
    all_gather x1, waiting for transfers between devices, body(): lax.all_gather(out_weight, 'fsdp', axis=1, tiled=True)  9.51 us
    all_to_all x1, starting transfers between devices, body(): lax.all_to_all(send_ids, 'dp', split_axis=0, concat_axis=0, tiled=True)  7.12 us
  transfers between devices with their start and end apart: 20, of which 10 were waited for; matrix products, arithmetic and copies ran while one was open for 13% of the time, Pallas kernels for 0%

profile of v4, /device:TPU:0, one launch (start us, length us, event | category | flops | bytes accessed | tf_op | source)
XLA Modules:
  0.0 283.2 jit_solution(17329135942031709958)
XLA Ops:
  12.5 7.1 %all-to-all-start = ((s32[16,1,50]{2,1,0:T(1,128)}), s32[16,1,50]{2,1,0:T(1,128)S(1)}, u32[]{:S(2)}, u32[]{:S(2)}) async-start(s32[16,1,50]{2,1,0:T(1,128)} %select_n.47), calls=%async_computation | async-start | bytes 16384 | tf_op jit(solution)/shard_map/all_to_all | solution.py:99
  20.4 4.6 %convolution_convert_fusion.1 = bf16[16,50,2048]{2,1,0:T(8,128)(2,1)} fusion(bf16[640,2048]{1,0:T(8,128)(2,1)S(1)} %copy-done, s32[16,50]{1,0:T(8,128)S(1)} %multiply_add_fusion, s32[640]{0:T(1024)S(1)} %get-tuple-element.40), kind=kOutput, calls=%fused_computation.13 | convolution fusion | flops 2099302400 | bytes 5904000 | tf_op jit(solution)/shard_map/opk,kd->opd/dot_general | solution.py:83
  27.1 5.8 %all-to-all-start.1 = ((bf16[16,50,2048]{2,1,0:T(8,128)(2,1)}), bf16[16,50,2048]{2,1,0:T(8,128)(2,1)}, u32[]{:S(2)}, u32[]{:S(2)}) async-start(bf16[16,50,2048]{2,1,0:T(8,128)(2,1)} %convolution_convert_fusion.1), calls=%async_computation.1 | async-start | bytes 7340032 | tf_op jit(solution)/shard_map/all_to_all | solution.py:92
  34.2 47.4 %all-to-all-done.1 = bf16[16,50,2048]{2,1,0:T(8,128)(2,1)} async-done(((bf16[16,50,2048]{2,1,0:T(8,128)(2,1)}), bf16[16,50,2048]{2,1,0:T(8,128)(2,1)}, u32[]{:S(2)}, u32[]{:S(2)}) %all-to-all-start.1) | async-done | bytes 3276832 | tf_op jit(solution)/shard_map/all_to_all | solution.py:92
  81.7 5.1 %bitcast_convert_fusion.1 = bf16[640,2048]{1,0:T(8,128)(2,1)S(1)} fusion(bf16[16,50,2048]{2,1,0:T(8,128)(2,1)} %all-to-all-done.1, s32[16,50]{1,0:T(8,128)S(1)} %bitcast.157), kind=kOutput, calls=%fused_computation.1 | convolution fusion | flops 2098974720 | bytes 5901440 | tf_op jit(solution)/shard_map/sop,opd->sd/dot_general | solution.py:104
  87.4 3.3 %fusion.33 = bf16[32,1024]{1,0:T(8,128)(2,1)S(1)} fusion(bf16[32,2048]{1,0:T(8,128)(2,1)S(1)} %convolution_convert_fusion.3, bf16[3,2048,1024]{2,1,0:T(8,128)(2,1)} %all-gather.3.cloned.1.call-done), kind=kOutput, calls=%fused_computation.59 | convolution fusion | flops 134250496 | bytes 4390912 | tf_op jit(solution)/shard_map/jvp()/dot_general | solution.py:22
  90.9 6.5 %fusion.15 = bf16[640,1024]{1,0:T(8,128)(2,1)} fusion(bf16[640,2048]{1,0:T(8,128)(2,1)S(1)} %bitcast_convert_fusion.1, bf16[3,2048,1024]{2,1,0:T(8,128)(2,1)} %all-gather.3.cloned.1.call-done), kind=kOutput, calls=%fused_computation.33 | convolution fusion | flops 2685009920 | bytes 8126464 | tf_op jit(solution)/shard_map/jvp()/dot_general | solution.py:27
  99.0 5.9 %fusion.16 = bf16[640,1024]{1,0:T(8,128)(2,1)S(1)} fusion(bf16[640,2048]{1,0:T(8,128)(2,1)} %copy-done.7, bf16[3,2048,1024]{2,1,0:T(8,128)(2,1)} %all-gather.3.cloned.1.call-done), kind=kOutput, calls=%fused_computation.34 | convolution fusion | flops 2685009920 | bytes 8126464 | tf_op jit(solution)/shard_map/jvp()/dot_general | solution.py:32
  108.5 9.5 %all-gather.5.cloned.1.call-done = bf16[1024,2048]{1,0:T(8,128)(2,1)} async-done(((bf16[1024,256]{1,0:T(8,128)(2,1)}), bf16[1024,2048]{1,0:T(8,128)(2,1)}) %all-gather.5.cloned.1.call-update) | async-done | bytes 4194320 | tf_op jit(solution)/shard_map/all_gather | solution.py:109
  118.0 3.0 %convolution_add_fusion = f32[32,2048]{1,0:T(8,128)S(1)} fusion(bf16[32,1024]{1,0:T(8,128)(2,1)S(1)} %reshape.248, bf16[1024,2048]{1,0:T(8,128)(2,1)} %all-gather.5.cloned.1.call-done, bf16[32,2048]{1,0:T(8,128)(2,1)S(1)} %convolution_convert_fusion.3), kind=kOutput, calls=%fused_computation.23 | convolution fusion | flops 134348800 | bytes 4653056 | tf_op jit(solution)/shard_map/jvp()/dot_general | solution.py:45
  121.3 4.9 %collective-permute-start = (bf16[34,2048]{1,0:T(8,128)(2,1)S(1)}, bf16[34,2048]{1,0:T(8,128)(2,1)S(1)}, u32[]{:S(2)}, u32[]{:S(2)}) collective-permute-start(bf16[34,2048]{1,0:T(8,128)(2,1)S(1)} %pad_maximum_fusion.3), channel_id=1, source_target_pairs={{0,120},{8,0},{16,8},{24,16},{32,24},{40,32},{48,40},{56,48},{64,5... | collective-permute-start | bytes 417800 | tf_op jit(solution)/shard_map/ppermute | solution.py:143
  131.3 4.0 %collective-permute-start.5 = (bf16[34,2048]{1,0:T(8,128)(2,1)S(1)}, bf16[34,2048]{1,0:T(8,128)(2,1)S(1)}, u32[]{:S(2)}, u32[]{:S(2)}) collective-permute-start(bf16[34,2048]{1,0:T(8,128)(2,1)S(1)} %pad_maximum_fusion.3), channel_id=1, source_target_pairs={{0,80},{8,88},{16,96},{24,104},{32,112},{40,120},{48,0},{56,8},{64... | collective-permute-start | bytes 417800 | tf_op jit(solution)/shard_map/ppermute | solution.py:143
  139.0 3.2 %collective-permute-start.7 = (bf16[34,2048]{1,0:T(8,128)(2,1)S(1)}, bf16[34,2048]{1,0:T(8,128)(2,1)S(1)}, u32[]{:S(2)}, u32[]{:S(2)}) collective-permute-start(bf16[34,2048]{1,0:T(8,128)(2,1)S(1)} %pad_maximum_fusion.3), channel_id=1, source_target_pairs={{0,64},{8,72},{16,80},{24,88},{32,96},{40,104},{48,112},{56,120},{... | collective-permute-start | bytes 417800 | tf_op jit(solution)/shard_map/ppermute | solution.py:143
  148.6 9.8 %collective-permute-start.11 = (bf16[34,2048]{1,0:T(8,128)(2,1)S(1)}, bf16[34,2048]{1,0:T(8,128)(2,1)S(1)}, u32[]{:S(2)}, u32[]{:S(2)}) collective-permute-start(bf16[34,2048]{1,0:T(8,128)(2,1)S(1)} %pad_maximum_fusion.3), channel_id=1, source_target_pairs={{0,32},{8,40},{16,48},{24,56},{32,64},{40,72},{48,80},{56,88},{64,... | collective-permute-start | bytes 417800 | tf_op jit(solution)/shard_map/ppermute | solution.py:143
  158.4 7.5 %collective-permute-start.12 = (bf16[34,2048]{1,0:T(8,128)(2,1)S(1)}, bf16[34,2048]{1,0:T(8,128)(2,1)S(1)}, u32[]{:S(2)}, u32[]{:S(2)}) collective-permute-start(bf16[34,2048]{1,0:T(8,128)(2,1)S(1)} %pad_maximum_fusion.3), channel_id=1, source_target_pairs={{0,24},{8,32},{16,40},{24,48},{32,56},{40,64},{48,72},{56,80},{64,... | collective-permute-start | bytes 417800 | tf_op jit(solution)/shard_map/ppermute | solution.py:143
  167.3 3.2 %collective-permute-done.12 = bf16[34,2048]{1,0:T(8,128)(2,1)S(1)} collective-permute-done((bf16[34,2048]{1,0:T(8,128)(2,1)S(1)}, bf16[34,2048]{1,0:T(8,128)(2,1)S(1)}, u32[]{:S(2)}, u32[]{:S(2)}) %collective-permute-start.12) | collective-permute-done | bytes 139296 | tf_op jit(solution)/shard_map/ppermute | solution.py:143
  170.5 5.4 %collective-permute-done.13 = bf16[34,2048]{1,0:T(8,128)(2,1)S(1)} collective-permute-done((bf16[34,2048]{1,0:T(8,128)(2,1)S(1)}, bf16[34,2048]{1,0:T(8,128)(2,1)S(1)}, u32[]{:S(2)}, u32[]{:S(2)}) %collective-permute-start.13) | collective-permute-done | bytes 139296 | tf_op jit(solution)/shard_map/ppermute | solution.py:143
  190.5 7.1 %fusion.6 = bf16[640,2048]{1,0:T(8,128)(2,1)} fusion(bf16[640,1024]{0,1:T(8,128)(2,1)} %bitcast.160, bf16[3,2048,1024]{2,1,0:T(8,128)(2,1)} %all-gather.3.cloned.1.call-done), kind=kOutput, calls=%fused_computation.15 | convolution fusion | flops 2685665280 | bytes 8126464 | tf_op jit(solution)/shard_map/transpose(jvp())/dot_general | solution.py:27
  197.6 6.6 %fusion.7 = bf16[640,2048]{1,0:T(8,128)(2,1)} fusion(bf16[640,1024]{0,1:T(8,128)(2,1)S(1)} %bitcast.161, bf16[3,2048,1024]{2,1,0:T(8,128)(2,1)} %all-gather.3.cloned.1.call-done), kind=kOutput, calls=%fused_computation.16 | convolution fusion | flops 2685665280 | bytes 8126464 | tf_op jit(solution)/shard_map/transpose(jvp())/dot_general | solution.py:32
  204.2 6.0 %fusion.10 = bf16[640,2048]{1,0:T(8,128)(2,1)S(1)} fusion(bf16[640,2048]{1,0:T(8,128)(2,1)} %fusion.7, bf16[640,2048]{1,0:T(8,128)(2,1)} %fusion.6, bf16[32,1024]{1,0:T(8,128)(2,1)S(1)} %reshape.256, bf16[3,2048,1024]{2,1,0:T(8,128)(2,1)} %all-gather.3.cloned.1.call-done, s32[32]{0:T(128)S(1)} %pad_add_fusion), kind=kOutput, calls=%fused_computation.19 | convolution fusion | flops 227364864 | bytes 12124288 | tf_op jit(solution)/shard_map/transpose(jvp())/dot_general | solution.py:49
  212.7 4.7 %convolution_convert_fusion = bf16[16,50,2048]{2,1,0:T(8,128)(2,1)} fusion(bf16[640,2048,1]{1,0,2:T(8,128)(2,1)S(1)} %fusion.11, s32[16,50]{1,0:T(8,128)S(1)} %bitcast.158), kind=kOutput, calls=%fused_computation.12 | convolution fusion | flops 2099302400 | bytes 5901440 | tf_op jit(solution)/shard_map/sop,sd->opd/dot_general | solution.py:194
  217.4 4.5 %all-to-all-start.2 = ((bf16[16,50,2048]{2,1,0:T(8,128)(2,1)}), bf16[16,50,2048]{2,1,0:T(8,128)(2,1)}, u32[]{:S(2)}, u32[]{:S(2)}) async-start(bf16[16,50,2048]{2,1,0:T(8,128)(2,1)} %convolution_convert_fusion), calls=%async_computation.2 | async-start | bytes 7340032 | tf_op jit(solution)/shard_map/all_to_all | solution.py:197
  222.5 46.8 %all-to-all-done.2 = bf16[16,50,2048]{2,1,0:T(8,128)(2,1)} async-done(((bf16[16,50,2048]{2,1,0:T(8,128)(2,1)}), bf16[16,50,2048]{2,1,0:T(8,128)(2,1)}, u32[]{:S(2)}, u32[]{:S(2)}) %all-to-all-start.2) | async-done | bytes 3276832 | tf_op jit(solution)/shard_map/all_to_all | solution.py:197
  269.4 6.7 %bitcast_convert_fusion = bf16[640,2048]{1,0:T(8,128)(2,1)} fusion(bf16[16,50,2048]{2,1,0:T(8,128)(2,1)} %all-to-all-done.2, s32[16,50]{1,0:T(8,128)S(1)} %multiply_add_fusion, s32[640]{0:T(1024)S(1)} %get-tuple-element.40), kind=kOutput, calls=%fused_computation | convolution fusion | flops 2098974720 | bytes 5904000 | tf_op jit(solution)/shard_map/opk,opd->kd/dot_general | solution.py:198
  (125 shorter events, 49.0 us)
Async XLA Ops:
  7.2 13.2 %copy-start = (bf16[640,2048]{1,0:T(8,128)(2,1)S(1)}, bf16[640,2048]{1,0:T(8,128)(2,1)}, u32[]{:S(2)}) copy-start(bf16[640,2048]{1,0:T(8,128)(2,1)} %param.13) | copy-start | bytes 7864324
  7.2 80.2 %all-gather.3.cloned.1.call-start = ((), (), s32[]{:S(2)}) async-start(), calls=%async_computation.3 | async-start | bytes 14155776 | tf_op jit(solution)/shard_map/all_gather | solution.py:108
  12.5 14.6 %all-to-all-start = ((s32[16,1,50]{2,1,0:T(1,128)}), s32[16,1,50]{2,1,0:T(1,128)S(1)}, u32[]{:S(2)}, u32[]{:S(2)}) async-start(s32[16,1,50]{2,1,0:T(1,128)} %select_n.47), calls=%async_computation | async-start | bytes 16384 | tf_op jit(solution)/shard_map/all_to_all | solution.py:99
  19.6 98.4 %all-gather.5.cloned.1.call-start = ((), (), s32[]{:S(2)}) async-start(), calls=%async_computation.4 | async-start | bytes 4718592 | tf_op jit(solution)/shard_map/all_gather | solution.py:109
  25.0 8.7 %copy-start.9 = (f32[16]{0:T(128)S(1)}, f32[16]{0:T(128)}, u32[]{:S(2)}) copy-start(f32[16]{0:T(128)} %param.21) | copy-start | bytes 196
  25.0 8.9 %copy-start.10 = (s32[16]{0:T(128)S(1)}, s32[16]{0:T(128)}, u32[]{:S(2)}) copy-start(s32[16]{0:T(128)} %param.19) | copy-start | bytes 196
  25.0 8.9 %copy-start.11 = (s32[16]{0:T(128)S(1)}, s32[16]{0:T(128)}, u32[]{:S(2)}) copy-start(s32[16]{0:T(128)} %param.18) | copy-start | bytes 196
  27.1 54.6 %all-to-all-start.1 = ((bf16[16,50,2048]{2,1,0:T(8,128)(2,1)}), bf16[16,50,2048]{2,1,0:T(8,128)(2,1)}, u32[]{:S(2)}, u32[]{:S(2)}) async-start(bf16[16,50,2048]{2,1,0:T(8,128)(2,1)} %convolution_convert_fusion.1), calls=%async_computation.1 | async-start | bytes 7340032 | tf_op jit(solution)/shard_map/all_to_all | solution.py:92
  121.3 10.0 %collective-permute-start = (bf16[34,2048]{1,0:T(8,128)(2,1)S(1)}, bf16[34,2048]{1,0:T(8,128)(2,1)S(1)}, u32[]{:S(2)}, u32[]{:S(2)}) collective-permute-start(bf16[34,2048]{1,0:T(8,128)(2,1)S(1)} %pad_maximum_fusion.3), channel_id=1, source_target_pairs={{0,120},{8,0},{16,8},{24,16},{32,24},{40,32},{48,40},{56,48},{64,5... | collective-permute-start | bytes 417800 | tf_op jit(solution)/shard_map/ppermute | solution.py:143
  126.2 10.0 %collective-permute-start.1 = (bf16[34,2048]{1,0:T(8,128)(2,1)S(1)}, bf16[34,2048]{1,0:T(8,128)(2,1)S(1)}, u32[]{:S(2)}, u32[]{:S(2)}) collective-permute-start(bf16[34,2048]{1,0:T(8,128)(2,1)S(1)} %pad_maximum_fusion.3), channel_id=1, source_target_pairs={{0,112},{8,120},{16,0},{24,8},{32,16},{40,24},{48,32},{56,40},{64,... | collective-permute-start | bytes 417800 | tf_op jit(solution)/shard_map/ppermute | solution.py:143
  127.1 12.0 %collective-permute-start.2 = (bf16[34,2048]{1,0:T(8,128)(2,1)S(1)}, bf16[34,2048]{1,0:T(8,128)(2,1)S(1)}, u32[]{:S(2)}, u32[]{:S(2)}) collective-permute-start(bf16[34,2048]{1,0:T(8,128)(2,1)S(1)} %pad_maximum_fusion.3), channel_id=1, source_target_pairs={{0,104},{8,112},{16,120},{24,0},{32,8},{40,16},{48,24},{56,32},{64... | collective-permute-start | bytes 417800 | tf_op jit(solution)/shard_map/ppermute | solution.py:143
  128.2 17.0 %collective-permute-start.3 = (bf16[34,2048]{1,0:T(8,128)(2,1)S(1)}, bf16[34,2048]{1,0:T(8,128)(2,1)S(1)}, u32[]{:S(2)}, u32[]{:S(2)}) collective-permute-start(bf16[34,2048]{1,0:T(8,128)(2,1)S(1)} %pad_maximum_fusion.3), channel_id=1, source_target_pairs={{0,96},{8,104},{16,112},{24,120},{32,0},{40,8},{48,16},{56,24},{64... | collective-permute-start | bytes 417800 | tf_op jit(solution)/shard_map/ppermute | solution.py:143
  128.9 16.6 %collective-permute-start.4 = (bf16[34,2048]{1,0:T(8,128)(2,1)S(1)}, bf16[34,2048]{1,0:T(8,128)(2,1)S(1)}, u32[]{:S(2)}, u32[]{:S(2)}) collective-permute-start(bf16[34,2048]{1,0:T(8,128)(2,1)S(1)} %pad_maximum_fusion.3), channel_id=1, source_target_pairs={{0,88},{8,96},{16,104},{24,112},{32,120},{40,0},{48,8},{56,16},{64... | collective-permute-start | bytes 417800 | tf_op jit(solution)/shard_map/ppermute | solution.py:143
  131.3 16.7 %collective-permute-start.5 = (bf16[34,2048]{1,0:T(8,128)(2,1)S(1)}, bf16[34,2048]{1,0:T(8,128)(2,1)S(1)}, u32[]{:S(2)}, u32[]{:S(2)}) collective-permute-start(bf16[34,2048]{1,0:T(8,128)(2,1)S(1)} %pad_maximum_fusion.3), channel_id=1, source_target_pairs={{0,80},{8,88},{16,96},{24,104},{32,112},{40,120},{48,0},{56,8},{64... | collective-permute-start | bytes 417800 | tf_op jit(solution)/shard_map/ppermute | solution.py:143
  136.2 12.4 %collective-permute-start.6 = (bf16[34,2048]{1,0:T(8,128)(2,1)S(1)}, bf16[34,2048]{1,0:T(8,128)(2,1)S(1)}, u32[]{:S(2)}, u32[]{:S(2)}) collective-permute-start(bf16[34,2048]{1,0:T(8,128)(2,1)S(1)} %pad_maximum_fusion.3), channel_id=1, source_target_pairs={{0,72},{8,80},{16,88},{24,96},{32,104},{40,112},{48,120},{56,0},{6... | collective-permute-start | bytes 417800 | tf_op jit(solution)/shard_map/ppermute | solution.py:143
  139.0 19.4 %collective-permute-start.7 = (bf16[34,2048]{1,0:T(8,128)(2,1)S(1)}, bf16[34,2048]{1,0:T(8,128)(2,1)S(1)}, u32[]{:S(2)}, u32[]{:S(2)}) collective-permute-start(bf16[34,2048]{1,0:T(8,128)(2,1)S(1)} %pad_maximum_fusion.3), channel_id=1, source_target_pairs={{0,64},{8,72},{16,80},{24,88},{32,96},{40,104},{48,112},{56,120},{... | collective-permute-start | bytes 417800 | tf_op jit(solution)/shard_map/ppermute | solution.py:143
  145.2 20.7 %collective-permute-start.8 = (bf16[34,2048]{1,0:T(8,128)(2,1)S(1)}, bf16[34,2048]{1,0:T(8,128)(2,1)S(1)}, u32[]{:S(2)}, u32[]{:S(2)}) collective-permute-start(bf16[34,2048]{1,0:T(8,128)(2,1)S(1)} %pad_maximum_fusion.3), channel_id=1, source_target_pairs={{0,56},{8,64},{16,72},{24,80},{32,88},{40,96},{48,104},{56,112},{6... | collective-permute-start | bytes 417800 | tf_op jit(solution)/shard_map/ppermute | solution.py:143
  145.6 20.5 %collective-permute-start.9 = (bf16[34,2048]{1,0:T(8,128)(2,1)S(1)}, bf16[34,2048]{1,0:T(8,128)(2,1)S(1)}, u32[]{:S(2)}, u32[]{:S(2)}) collective-permute-start(bf16[34,2048]{1,0:T(8,128)(2,1)S(1)} %pad_maximum_fusion.3), channel_id=1, source_target_pairs={{0,48},{8,56},{16,64},{24,72},{32,80},{40,88},{48,96},{56,104},{64... | collective-permute-start | bytes 417800 | tf_op jit(solution)/shard_map/ppermute | solution.py:143
  148.0 19.2 %collective-permute-start.10 = (bf16[34,2048]{1,0:T(8,128)(2,1)S(1)}, bf16[34,2048]{1,0:T(8,128)(2,1)S(1)}, u32[]{:S(2)}, u32[]{:S(2)}) collective-permute-start(bf16[34,2048]{1,0:T(8,128)(2,1)S(1)} %pad_maximum_fusion.3), channel_id=1, source_target_pairs={{0,40},{8,48},{16,56},{24,64},{32,72},{40,80},{48,88},{56,96},{64,... | collective-permute-start | bytes 417800 | tf_op jit(solution)/shard_map/ppermute | solution.py:143
  148.6 18.6 %collective-permute-start.11 = (bf16[34,2048]{1,0:T(8,128)(2,1)S(1)}, bf16[34,2048]{1,0:T(8,128)(2,1)S(1)}, u32[]{:S(2)}, u32[]{:S(2)}) collective-permute-start(bf16[34,2048]{1,0:T(8,128)(2,1)S(1)} %pad_maximum_fusion.3), channel_id=1, source_target_pairs={{0,32},{8,40},{16,48},{24,56},{32,64},{40,72},{48,80},{56,88},{64,... | collective-permute-start | bytes 417800 | tf_op jit(solution)/shard_map/ppermute | solution.py:143
  158.4 12.1 %collective-permute-start.12 = (bf16[34,2048]{1,0:T(8,128)(2,1)S(1)}, bf16[34,2048]{1,0:T(8,128)(2,1)S(1)}, u32[]{:S(2)}, u32[]{:S(2)}) collective-permute-start(bf16[34,2048]{1,0:T(8,128)(2,1)S(1)} %pad_maximum_fusion.3), channel_id=1, source_target_pairs={{0,24},{8,32},{16,40},{24,48},{32,56},{40,64},{48,72},{56,80},{64,... | collective-permute-start | bytes 417800 | tf_op jit(solution)/shard_map/ppermute | solution.py:143
  166.0 10.0 %collective-permute-start.13 = (bf16[34,2048]{1,0:T(8,128)(2,1)S(1)}, bf16[34,2048]{1,0:T(8,128)(2,1)S(1)}, u32[]{:S(2)}, u32[]{:S(2)}) collective-permute-start(bf16[34,2048]{1,0:T(8,128)(2,1)S(1)} %pad_maximum_fusion.3), channel_id=1, source_target_pairs={{0,16},{8,24},{16,32},{24,40},{32,48},{40,56},{48,64},{56,72},{64,... | collective-permute-start | bytes 417800 | tf_op jit(solution)/shard_map/ppermute | solution.py:143
  166.1 11.6 %collective-permute-start.14 = (bf16[34,2048]{1,0:T(8,128)(2,1)S(1)}, bf16[34,2048]{1,0:T(8,128)(2,1)S(1)}, u32[]{:S(2)}, u32[]{:S(2)}) collective-permute-start(bf16[34,2048]{1,0:T(8,128)(2,1)S(1)} %pad_maximum_fusion.3), channel_id=1, source_target_pairs={{0,8},{8,16},{16,24},{24,32},{32,40},{40,48},{48,56},{56,64},{64,7... | collective-permute-start | bytes 417800 | tf_op jit(solution)/shard_map/ppermute | solution.py:143
  217.4 52.0 %all-to-all-start.2 = ((bf16[16,50,2048]{2,1,0:T(8,128)(2,1)}), bf16[16,50,2048]{2,1,0:T(8,128)(2,1)}, u32[]{:S(2)}, u32[]{:S(2)}) async-start(bf16[16,50,2048]{2,1,0:T(8,128)(2,1)} %convolution_convert_fusion), calls=%async_computation.2 | async-start | bytes 7340032 | tf_op jit(solution)/shard_map/all_to_all | solution.py:197
  (9 other events, 35.1 us)
Sparse Core Ops, SparseCore 0:
  9.7 69.9 all-gather.2
  81.4 36.5 all-gather.4

commit v5 on v4

--- a/solution.py
+++ b/solution.py
@@ -137,14 +137,13 @@
     weight_rows = jnp.zeros((2, feature_width), jnp.bfloat16)
     weight_rows = weight_rows.at[0, :pair_count].set(weight_hi).at[1, :pair_count].set(weight_lo)
     both_emb = jnp.concatenate([fig_emb, cap_emb, weight_rows], axis=0)
-    gathered = [both_emb]
-    for shift in range(1, dp_count):
-        gathered.append(
-            lax.ppermute(
-                both_emb, "dp", perm=[(i, (i - shift) % dp_count) for i in range(dp_count)]
-            )
-        )
-    all_both = jnp.stack(gathered, axis=0)
+    all_both = lax.all_to_all(
+        jnp.broadcast_to(both_emb[None], (dp_count,) + both_emb.shape),
+        "dp",
+        split_axis=0,
+        concat_axis=0,
+        tiled=True,
+    )
     all_fig = all_both[:, :pair_count].reshape(-1, feature_width)
     all_cap = all_both[:, pair_count : 2 * pair_count].reshape(-1, feature_width)
     all_weight = (
@@ -153,7 +152,7 @@
     ).reshape(-1)
     logit_mult = logit_scale[0]
     pair_total = all_fig.shape[0]
-    first_pair = 0
+    first_pair = lax.axis_index("dp") * pair_count
     logits = logit_mult * jnp.dot(all_fig, all_cap.T, preferred_element_type=jnp.float32)
     row_lse = log_total(logits, 1)
     col_lse = log_total(logits, 0)

time: 286 us -> 272 us (0.951)
  starting transfers between devices: 59 us -> 26.1 us
  waiting for transfers between devices: 122 us -> 145 us
    ppermute x15 -> x0, starting transfers between devices: 41.5 us -> none  [body(): lax.ppermute(both_emb, 'dp', perm=[(i, (i - shift) % dp_count) for i in r...]
    all_to_all x0 -> x1, waiting for transfers between devices: none -> 35.6 us  [body(): lax.all_to_all(jnp.broadcast_to(both_emb[None], (dp_count,) + both_emb.sh...]
    ppermute x15 -> x0, waiting for transfers between devices: 14.6 us -> none  [body(): lax.ppermute(both_emb, 'dp', perm=[(i, (i - shift) % dp_count) for i in r...]
    all_to_all x0 -> x1, starting transfers between devices: none -> 7.03 us  [body(): lax.all_to_all(jnp.broadcast_to(both_emb[None], (dp_count,) + both_emb.sh...]
  transfers between devices with their start and end apart: 20 -> 6, of which waited for: 10 -> 5; matrix products, arithmetic and copies ran while one was open for 13% -> 14% of each run, Pallas kernels for 0% -> 0%
where the time goes in v5:
time: 272 us; the launch traced here: 271 us
  waiting for transfers between devices  145 us (53%)
  matrix products  72.6 us (27%)
  starting transfers between devices  26.1 us (10%)
  between operations  15.1 us (6%)
  local copies, waits for them, and re-layouts  8.12 us (3%)
  other arithmetic  4.57 us (2%)
    all_to_all x1, waiting for transfers between devices, body(): lax.all_to_all(back_rows, 'dp', split_axis=0, concat_axis=0, tiled=True)  48.1 us
    all_to_all x1, waiting for transfers between devices, body(): lax.all_to_all(send_rows, 'dp', split_axis=0, concat_axis=0, tiled=True)  48.1 us
    all_to_all x1, waiting for transfers between devices, body(): lax.all_to_all(jnp.broadcast_to(both_emb[None], (dp_count,) + both_emb.sh...  35.6 us
    dot_general x2, matrix products, attend(): jnp.dot(slot_row_block, qkv_mat[1], preferred_element_type=jnp.float32)  13.1 us
    dot_general x2, matrix products, attend(): jnp.dot(slot_row_block, qkv_mat[2], preferred_element_type=jnp.float32)  12.9 us
    all_gather x1, waiting for transfers between devices, body(): lax.all_gather(out_weight, 'fsdp', axis=1, tiled=True)  9.61 us
    all_to_all x1, starting transfers between devices, body(): lax.all_to_all(send_ids, 'dp', split_axis=0, concat_axis=0, tiled=True)  7.12 us
    all_to_all x1, starting transfers between devices, body(): lax.all_to_all(jnp.broadcast_to(both_emb[None], (dp_count,) + both_emb.sh...  7.03 us
  transfers between devices with their start and end apart: 6, of which 5 were waited for; matrix products, arithmetic and copies ran while one was open for 14% of the time, Pallas kernels for 0%

profile of v5, /device:TPU:0, one launch (start us, length us, event | category | flops | bytes accessed | tf_op | source)
XLA Modules:
  0.0 271.4 jit_solution(3355362005845137884)
XLA Ops:
  12.5 7.1 %all-to-all-start = ((s32[16,1,50]{2,1,0:T(1,128)}), s32[16,1,50]{2,1,0:T(1,128)S(1)}, u32[]{:S(2)}, u32[]{:S(2)}) async-start(s32[16,1,50]{2,1,0:T(1,128)} %select_n.47), calls=%async_computation | async-start | bytes 16384 | tf_op jit(solution)/shard_map/all_to_all | solution.py:99
  20.4 4.6 %convolution_convert_fusion.1 = bf16[16,50,2048]{2,1,0:T(8,128)(2,1)} fusion(bf16[640,2048]{1,0:T(8,128)(2,1)S(1)} %copy-done, s32[16,50]{1,0:T(8,128)S(1)} %multiply_add_fusion, s32[640]{0:T(1024)S(1)} %get-tuple-element.40), kind=kOutput, calls=%fused_computation.13 | convolution fusion | flops 2099302400 | bytes 5904000 | tf_op jit(solution)/shard_map/opk,kd->opd/dot_general | solution.py:83
  25.0 2.1 all-to-all-done
  27.1 5.3 %all-to-all-start.1 = ((bf16[16,50,2048]{2,1,0:T(8,128)(2,1)}), bf16[16,50,2048]{2,1,0:T(8,128)(2,1)}, u32[]{:S(2)}, u32[]{:S(2)}) async-start(bf16[16,50,2048]{2,1,0:T(8,128)(2,1)} %convolution_convert_fusion.1), calls=%async_computation.1 | async-start | bytes 7340032 | tf_op jit(solution)/shard_map/all_to_all | solution.py:92
  33.1 48.1 %all-to-all-done.1 = bf16[16,50,2048]{2,1,0:T(8,128)(2,1)} async-done(((bf16[16,50,2048]{2,1,0:T(8,128)(2,1)}), bf16[16,50,2048]{2,1,0:T(8,128)(2,1)}, u32[]{:S(2)}, u32[]{:S(2)}) %all-to-all-start.1) | async-done | bytes 3276832 | tf_op jit(solution)/shard_map/all_to_all | solution.py:92
  81.1 5.1 %bitcast_convert_fusion.1 = bf16[640,2048]{1,0:T(8,128)(2,1)S(1)} fusion(bf16[16,50,2048]{2,1,0:T(8,128)(2,1)} %all-to-all-done.1, s32[16,50]{1,0:T(8,128)S(1)} %bitcast.125), kind=kOutput, calls=%fused_computation.1 | convolution fusion | flops 2098974720 | bytes 5901440 | tf_op jit(solution)/shard_map/sop,opd->sd/dot_general | solution.py:104
  86.9 3.3 %fusion.33 = bf16[32,1024]{1,0:T(8,128)(2,1)S(1)} fusion(bf16[32,2048]{1,0:T(8,128)(2,1)S(1)} %convolution_convert_fusion.3, bf16[3,2048,1024]{2,1,0:T(8,128)(2,1)} %all-gather.3.cloned.1.call-done), kind=kOutput, calls=%fused_computation.59 | convolution fusion | flops 134250496 | bytes 4390912 | tf_op jit(solution)/shard_map/jvp()/dot_general | solution.py:22
  90.3 6.4 %fusion.15 = bf16[640,1024]{1,0:T(8,128)(2,1)} fusion(bf16[640,2048]{1,0:T(8,128)(2,1)S(1)} %bitcast_convert_fusion.1, bf16[3,2048,1024]{2,1,0:T(8,128)(2,1)} %all-gather.3.cloned.1.call-done), kind=kOutput, calls=%fused_computation.33 | convolution fusion | flops 2685009920 | bytes 8126464 | tf_op jit(solution)/shard_map/jvp()/dot_general | solution.py:27
  96.8 1.7 copy.36
  98.5 6.3 %fusion.16 = bf16[640,1024]{1,0:T(8,128)(2,1)S(1)} fusion(bf16[640,2048]{1,0:T(8,128)(2,1)} %copy-done.8, bf16[3,2048,1024]{2,1,0:T(8,128)(2,1)} %all-gather.3.cloned.1.call-done), kind=kOutput, calls=%fused_computation.34 | convolution fusion | flops 2685009920 | bytes 8126464 | tf_op jit(solution)/shard_map/jvp()/dot_general | solution.py:32
  108.4 9.6 %all-gather.5.cloned.1.call-done = bf16[1024,2048]{1,0:T(8,128)(2,1)} async-done(((bf16[1024,256]{1,0:T(8,128)(2,1)}), bf16[1024,2048]{1,0:T(8,128)(2,1)}) %all-gather.5.cloned.1.call-update) | async-done | bytes 4194320 | tf_op jit(solution)/shard_map/all_gather | solution.py:109
  118.0 3.0 %convolution_add_fusion = f32[32,2048]{1,0:T(8,128)S(1)} fusion(bf16[32,1024]{1,0:T(8,128)(2,1)S(1)} %reshape.253, bf16[1024,2048]{1,0:T(8,128)(2,1)} %all-gather.5.cloned.1.call-done, bf16[32,2048]{1,0:T(8,128)(2,1)S(1)} %convolution_convert_fusion.3), kind=kOutput, calls=%fused_computation.23 | convolution fusion | flops 134348800 | bytes 4653056 | tf_op jit(solution)/shard_map/jvp()/dot_general | solution.py:45
  121.3 1.8 broadcast_in_dim.89
  123.1 7.0 %all-to-all-start.2 = ((bf16[16,34,2048]{2,1,0:T(8,128)(2,1)}), bf16[16,34,2048]{2,1,0:T(8,128)(2,1)S(1)}, u32[]{:S(2)}, u32[]{:S(2)}) async-start(bf16[16,34,2048]{2,1,0:T(8,128)(2,1)} %broadcast_in_dim.89), calls=%async_computation.2 | async-start | bytes 5242880 | tf_op jit(solution)/shard_map/all_to_all | solution.py:140
  130.8 35.6 %all-to-all-done.2 = bf16[16,34,2048]{2,1,0:T(8,128)(2,1)S(1)} async-done(((bf16[16,34,2048]{2,1,0:T(8,128)(2,1)}), bf16[16,34,2048]{2,1,0:T(8,128)(2,1)S(1)}, u32[]{:S(2)}, u32[]{:S(2)}) %all-to-all-start.2) | async-done | bytes 2228256 | tf_op jit(solution)/shard_map/all_to_all | solution.py:140
  170.9 1.8 fusion.24
  175.9 6.7 %fusion.6 = bf16[640,2048]{1,0:T(8,128)(2,1)} fusion(bf16[640,1024]{0,1:T(8,128)(2,1)S(1)} %bitcast.128, bf16[3,2048,1024]{2,1,0:T(8,128)(2,1)} %all-gather.3.cloned.1.call-done), kind=kOutput, calls=%fused_computation.15 | convolution fusion | flops 2685665280 | bytes 8126464 | tf_op jit(solution)/shard_map/transpose(jvp())/dot_general | solution.py:27
  182.6 6.6 %fusion.7 = bf16[640,2048]{1,0:T(8,128)(2,1)} fusion(bf16[640,1024]{0,1:T(8,128)(2,1)S(1)} %bitcast.129, bf16[3,2048,1024]{2,1,0:T(8,128)(2,1)} %all-gather.3.cloned.1.call-done), kind=kOutput, calls=%fused_computation.16 | convolution fusion | flops 2685665280 | bytes 8126464 | tf_op jit(solution)/shard_map/transpose(jvp())/dot_general | solution.py:32
  189.2 6.1 %fusion.10 = bf16[640,2048]{1,0:T(8,128)(2,1)S(1)} fusion(bf16[640,2048]{1,0:T(8,128)(2,1)} %fusion.7, bf16[640,2048]{1,0:T(8,128)(2,1)} %fusion.6, bf16[32,1024]{1,0:T(8,128)(2,1)S(1)} %reshape.261, bf16[3,2048,1024]{2,1,0:T(8,128)(2,1)} %all-gather.3.cloned.1.call-done, s32[32]{0:T(128)S(1)} %pad_add_fusion), kind=kOutput, calls=%fused_computation.19 | convolution fusion | flops 227364864 | bytes 12124288 | tf_op jit(solution)/shard_map/transpose(jvp())/dot_general | solution.py:49
  195.3 2.5 fusion.11
  197.8 4.7 %convolution_convert_fusion = bf16[16,50,2048]{2,1,0:T(8,128)(2,1)} fusion(bf16[640,2048,1]{1,0,2:T(8,128)(2,1)S(1)} %fusion.11, s32[16,50]{1,0:T(8,128)S(1)} %bitcast.126), kind=kOutput, calls=%fused_computation.12 | convolution fusion | flops 2099302400 | bytes 5901440 | tf_op jit(solution)/shard_map/sop,sd->opd/dot_general | solution.py:193
  202.4 6.6 %all-to-all-start.3 = ((bf16[16,50,2048]{2,1,0:T(8,128)(2,1)}), bf16[16,50,2048]{2,1,0:T(8,128)(2,1)}, u32[]{:S(2)}, u32[]{:S(2)}) async-start(bf16[16,50,2048]{2,1,0:T(8,128)(2,1)} %convolution_convert_fusion), calls=%async_computation.3 | async-start | bytes 7340032 | tf_op jit(solution)/shard_map/all_to_all | solution.py:196
  209.7 48.1 %all-to-all-done.3 = bf16[16,50,2048]{2,1,0:T(8,128)(2,1)} async-done(((bf16[16,50,2048]{2,1,0:T(8,128)(2,1)}), bf16[16,50,2048]{2,1,0:T(8,128)(2,1)}, u32[]{:S(2)}, u32[]{:S(2)}) %all-to-all-start.3) | async-done | bytes 3276832 | tf_op jit(solution)/shard_map/all_to_all | solution.py:196
  257.8 6.7 %bitcast_convert_fusion = bf16[640,2048]{1,0:T(8,128)(2,1)} fusion(bf16[16,50,2048]{2,1,0:T(8,128)(2,1)} %all-to-all-done.3, s32[16,50]{1,0:T(8,128)S(1)} %multiply_add_fusion, s32[640]{0:T(1024)S(1)} %get-tuple-element.40), kind=kOutput, calls=%fused_computation | convolution fusion | flops 2098974720 | bytes 5904000 | tf_op jit(solution)/shard_map/opk,opd->kd/dot_general | solution.py:197
  (85 shorter events, 19.5 us)
Async XLA Ops:
  7.2 13.2 %copy-start = (bf16[640,2048]{1,0:T(8,128)(2,1)S(1)}, bf16[640,2048]{1,0:T(8,128)(2,1)}, u32[]{:S(2)}) copy-start(bf16[640,2048]{1,0:T(8,128)(2,1)} %param.13) | copy-start | bytes 7864324
  7.2 79.7 %all-gather.3.cloned.1.call-start = ((), (), s32[]{:S(2)}) async-start(), calls=%async_computation.4 | async-start | bytes 14155776 | tf_op jit(solution)/shard_map/all_gather | solution.py:108
  12.5 14.6 %all-to-all-start = ((s32[16,1,50]{2,1,0:T(1,128)}), s32[16,1,50]{2,1,0:T(1,128)S(1)}, u32[]{:S(2)}, u32[]{:S(2)}) async-start(s32[16,1,50]{2,1,0:T(1,128)} %select_n.47), calls=%async_computation | async-start | bytes 16384 | tf_op jit(solution)/shard_map/all_to_all | solution.py:99
  19.6 98.4 %all-gather.5.cloned.1.call-start = ((), (), s32[]{:S(2)}) async-start(), calls=%async_computation.5 | async-start | bytes 4718592 | tf_op jit(solution)/shard_map/all_gather | solution.py:109
  25.0 7.4 %copy-start.9 = (s32[1,640]{1,0:T(1,128)S(1)}, s32[1,640]{1,0:T(1,128)}, u32[]{:S(2)}) copy-start(s32[1,640]{1,0:T(1,128)} %param.15) | copy-start | bytes 7684
  25.0 7.5 %copy-start.10 = (f32[16]{0:T(128)S(1)}, f32[16]{0:T(128)}, u32[]{:S(2)}) copy-start(f32[16]{0:T(128)} %param.21) | copy-start | bytes 196
  25.0 7.7 %copy-start.11 = (s32[16]{0:T(128)S(1)}, s32[16]{0:T(128)}, u32[]{:S(2)}) copy-start(s32[16]{0:T(128)} %param.19) | copy-start | bytes 196
  25.0 7.7 %copy-start.12 = (s32[16]{0:T(128)S(1)}, s32[16]{0:T(128)}, u32[]{:S(2)}) copy-start(s32[16]{0:T(128)} %param.18) | copy-start | bytes 196
  27.1 54.0 %all-to-all-start.1 = ((bf16[16,50,2048]{2,1,0:T(8,128)(2,1)}), bf16[16,50,2048]{2,1,0:T(8,128)(2,1)}, u32[]{:S(2)}, u32[]{:S(2)}) async-start(bf16[16,50,2048]{2,1,0:T(8,128)(2,1)} %convolution_convert_fusion.1), calls=%async_computation.1 | async-start | bytes 7340032 | tf_op jit(solution)/shard_map/all_to_all | solution.py:92
  86.2 4.1 %copy-start.8 = (bf16[640,2048]{1,0:T(8,128)(2,1)}, bf16[640,2048]{1,0:T(8,128)(2,1)S(1)}, u32[]{:S(2)}) copy-start(bf16[640,2048]{1,0:T(8,128)(2,1)S(1)} %bitcast_convert_fusion.1) | copy-start | bytes 7864324
  98.5 7.8 %copy-start.3 = (bf16[640,1024]{0,1:T(8,128)(2,1)}, bf16[640,1024]{0,1:T(8,128)(2,1)S(1)}, u32[]{:S(2)}) copy-start(bf16[640,1024]{0,1:T(8,128)(2,1)S(1)} %copy.36) | copy-start | bytes 3932164
  106.2 1.3 copy-start.7
  106.7 1.4 copy-start.5
  123.1 43.3 %all-to-all-start.2 = ((bf16[16,34,2048]{2,1,0:T(8,128)(2,1)}), bf16[16,34,2048]{2,1,0:T(8,128)(2,1)S(1)}, u32[]{:S(2)}, u32[]{:S(2)}) async-start(bf16[16,34,2048]{2,1,0:T(8,128)(2,1)} %broadcast_in_dim.89), calls=%async_computation.2 | async-start | bytes 5242880 | tf_op jit(solution)/shard_map/all_to_all | solution.py:140
  167.2 2.2 copy-start.2
  169.1 1.9 copy-start.6
  170.8 2.0 copy-start.4
  175.9 6.7 %copy-start.13 = (bf16[16,64,640]{2,1,0:T(8,128)(2,1)S(1)}, bf16[16,64,640]{2,1,0:T(8,128)(2,1)}, u32[]{:S(2)}) copy-start(bf16[16,64,640]{2,1,0:T(8,128)(2,1)} %convolution_convert_fusion.5) | copy-start | bytes 3932164
  202.4 55.4 %all-to-all-start.3 = ((bf16[16,50,2048]{2,1,0:T(8,128)(2,1)}), bf16[16,50,2048]{2,1,0:T(8,128)(2,1)}, u32[]{:S(2)}, u32[]{:S(2)}) async-start(bf16[16,50,2048]{2,1,0:T(8,128)(2,1)} %convolution_convert_fusion), calls=%async_computation.3 | async-start | bytes 7340032 | tf_op jit(solution)/shard_map/all_to_all | solution.py:196
  257.8 6.7 %copy-start.1 = (bf16[640,2048]{1,0:T(8,128)(2,1)S(1)}, bf16[640,2048]{1,0:T(8,128)(2,1)}, u32[]{:S(2)}) copy-start(bf16[640,2048]{1,0:T(8,128)(2,1)} %param.13) | copy-start | bytes 7864324
Sparse Core Ops, SparseCore 0:
  9.7 69.9 all-gather.2
  81.4 36.5 all-gather.4

commit v6 on v5

--- a/solution.py
+++ b/solution.py
@@ -79,25 +79,35 @@
     rank_idx = jnp.sum((jnp.cumsum(onehot, axis=0) - onehot) * onehot, axis=1)
     dest = owner_idx * capacity + rank_idx
     send_match = dest[None, :] == jnp.arange(buffer_rows)[:, None]
-    send_onehot = send_match.astype(jnp.bfloat16).reshape(dp_count, capacity, row_count)
-    send_rows = jnp.einsum(
-        "opk,kd->opd", send_onehot, page_embed, preferred_element_type=jnp.float32
-    ).astype(jnp.bfloat16)
     send_ids = jnp.where(
         jnp.any(send_match, axis=1),
         jnp.sum(jnp.where(send_match, slot_idx[None, :], 0), axis=1),
         row_count,
     ).reshape(dp_count, capacity)
-    recv_rows, recv_ids = (
-        lax.all_to_all(
-            send_rows,
-            "dp",
-            split_axis=0,
-            concat_axis=0,
-            tiled=True,
-        ),
-        lax.all_to_all(send_ids, "dp", split_axis=0, concat_axis=0, tiled=True),
-    )
+    send_onehot = jnp.concatenate(
+        [
+            send_match.astype(jnp.bfloat16).reshape(dp_count, capacity, row_count),
+            jnp.zeros((dp_count, 1, row_count), jnp.bfloat16),
+        ],
+        axis=1,
+    )
+    id_lanes = jnp.zeros((dp_count, feature_width), jnp.float32)
+    id_lanes = id_lanes.at[:, :capacity].set((send_ids // 16).astype(jnp.float32))
+    id_lanes = id_lanes.at[:, 128 : 128 + capacity].set((send_ids % 16).astype(jnp.float32))
+    id_rows = jnp.concatenate(
+        [jnp.zeros((dp_count, capacity, feature_width), jnp.float32), id_lanes[:, None, :]], axis=1
+    )
+    send_rows = (
+        jnp.einsum("opk,kd->opd", send_onehot, page_embed, preferred_element_type=jnp.float32)
+        + id_rows
+    ).astype(jnp.bfloat16)
+    recv_rows = lax.all_to_all(send_rows, "dp", split_axis=0, concat_axis=0, tiled=True)
+    id_row = recv_rows[:, capacity, :].astype(jnp.float32)
+    recv_ids = (
+        id_row[:, :capacity].astype(jnp.int32) * 16
+        + id_row[:, 128 : 128 + capacity].astype(jnp.int32)
+    )
+    recv_ids = jnp.concatenate([recv_ids, jnp.full((dp_count, 1), row_count, jnp.int32)], axis=1)
     recv_onehot = (
         jnp.arange(row_count)[:, None, None] == recv_ids[None, :, :]
     ).astype(jnp.bfloat16)

time: 272 us -> 272 us (level)
  starting transfers between devices: 26.1 us -> 21.3 us
  other arithmetic: 4.57 us -> 8.73 us
    all_to_all x1 -> x0, starting transfers between devices: 7.12 us -> none  [body(): lax.all_to_all(send_ids, 'dp', split_axis=0, concat_axis=0, tiled=True)]
  transfers between devices with their start and end apart: 6 -> 5, of which waited for: 5 -> 4; matrix products, arithmetic and copies ran while one was open for 14% -> 15% of each run, Pallas kernels for 0% -> 0%
where the time goes in v6:
time: 272 us; the launch traced here: 271 us
  waiting for transfers between devices  145 us (53%)
  matrix products  72.3 us (27%)
  starting transfers between devices  21.3 us (8%)
  between operations  15.2 us (6%)
  local copies, waits for them, and re-layouts  8.9 us (3%)
  other arithmetic  8.73 us (3%)
    all_to_all x1, waiting for transfers between devices, body(): lax.all_to_all(send_rows, 'dp', split_axis=0, concat_axis=0, tiled=True)  49.1 us
    all_to_all x1, waiting for transfers between devices, body(): lax.all_to_all(back_rows, 'dp', split_axis=0, concat_axis=0, tiled=True)  48.1 us
    all_to_all x1, waiting for transfers between devices, body(): lax.all_to_all(jnp.broadcast_to(both_emb[None], (dp_count,) + both_emb.sh...  35.6 us
    dot_general x2, matrix products, attend(): jnp.dot(slot_row_block, qkv_mat[1], preferred_element_type=jnp.float32)  13 us
    dot_general x2, matrix products, attend(): jnp.dot(slot_row_block, qkv_mat[2], preferred_element_type=jnp.float32)  12.9 us
    all_gather x1, waiting for transfers between devices, body(): lax.all_gather(out_weight, 'fsdp', axis=1, tiled=True)  11.1 us
    all_to_all x1, starting transfers between devices, body(): lax.all_to_all(send_rows, 'dp', split_axis=0, concat_axis=0, tiled=True)  7.31 us
    all_to_all x1, starting transfers between devices, body(): lax.all_to_all(jnp.broadcast_to(both_emb[None], (dp_count,) + both_emb.sh...  7.03 us
  transfers between devices with their start and end apart: 5, of which 4 were waited for; matrix products, arithmetic and copies ran while one was open for 15% of the time, Pallas kernels for 0%

profile of v6, /device:TPU:0, one launch (start us, length us, event | category | flops | bytes accessed | tf_op | source)
XLA Modules:
  0.0 271.5 jit_solution(3665990168854101643)
XLA Ops:
  16.3 4.5 %add_convert_fusion = bf16[16,51,2048]{2,1,0:T(8,128)(2,1)} fusion(f32[16,1,2048]{2,1,0:T(1,128)S(1)} %scatter.15, bf16[640,2048]{1,0:T(8,128)(2,1)S(1)} %copy-done, pred[16,50,640]{2,1,0:T(8,128)(4,1)S(1)} %broadcast_compare_fusion), kind=kOutput, calls=%fused_computation | convolution fusion | flops 2142437376 | bytes 6606848 | tf_op jit(solution)/shard_map/opk,kd->opd/dot_general | solution.py:101
  20.8 7.3 %all-to-all-start = ((bf16[16,51,2048]{2,1,0:T(8,128)(2,1)}), bf16[16,51,2048]{2,1,0:T(8,128)(2,1)}, u32[]{:S(2)}, u32[]{:S(2)}) async-start(bf16[16,51,2048]{2,1,0:T(8,128)(2,1)} %add_convert_fusion), calls=%async_computation | async-start | bytes 7340032 | tf_op jit(solution)/shard_map/all_to_all | solution.py:104
  29.5 49.1 %all-to-all-done = bf16[16,51,2048]{2,1,0:T(8,128)(2,1)} async-done(((bf16[16,51,2048]{2,1,0:T(8,128)(2,1)}), bf16[16,51,2048]{2,1,0:T(8,128)(2,1)}, u32[]{:S(2)}, u32[]{:S(2)}) %all-to-all-start) | async-done | bytes 3342368 | tf_op jit(solution)/shard_map/all_to_all | solution.py:104
  79.8 5.1 %bitcast_convert_fusion.1 = bf16[640,2048]{1,0:T(8,128)(2,1)S(1)} fusion(bf16[16,51,2048]{2,1,0:T(8,128)(2,1)} %all-to-all-done, s32[16,51]{1,0:T(8,128)S(1)} %concatenate.31), kind=kOutput, calls=%fused_computation.2 | convolution fusion | flops 2140928000 | bytes 5967040 | tf_op jit(solution)/shard_map/sop,opd->sd/dot_general | solution.py:114
  85.5 3.3 %fusion.29 = bf16[32,1024]{1,0:T(8,128)(2,1)S(1)} fusion(bf16[32,2048]{1,0:T(8,128)(2,1)S(1)} %convolution_convert_fusion.2, bf16[3,2048,1024]{2,1,0:T(8,128)(2,1)} %all-gather.3.cloned.1.call-done), kind=kOutput, calls=%fused_computation.56 | convolution fusion | flops 134250496 | bytes 4390912 | tf_op jit(solution)/shard_map/jvp()/dot_general | solution.py:22
  89.0 6.3 %fusion.15 = bf16[640,1024]{1,0:T(8,128)(2,1)} fusion(bf16[640,2048]{1,0:T(8,128)(2,1)S(1)} %bitcast_convert_fusion.1, bf16[3,2048,1024]{2,1,0:T(8,128)(2,1)} %all-gather.3.cloned.1.call-done), kind=kOutput, calls=%fused_computation.33 | convolution fusion | flops 2685009920 | bytes 8126464 | tf_op jit(solution)/shard_map/jvp()/dot_general | solution.py:27
  95.3 1.7 copy.28
  97.0 6.3 %fusion.16 = bf16[640,1024]{1,0:T(8,128)(2,1)S(1)} fusion(bf16[640,2048]{1,0:T(8,128)(2,1)} %copy-done.8, bf16[3,2048,1024]{2,1,0:T(8,128)(2,1)} %all-gather.3.cloned.1.call-done), kind=kOutput, calls=%fused_computation.34 | convolution fusion | flops 2685009920 | bytes 8126464 | tf_op jit(solution)/shard_map/jvp()/dot_general | solution.py:32
  103.4 1.4 copy.27
  106.9 11.1 %all-gather.5.cloned.1.call-done = bf16[1024,2048]{1,0:T(8,128)(2,1)} async-done(((bf16[1024,256]{1,0:T(8,128)(2,1)}), bf16[1024,2048]{1,0:T(8,128)(2,1)}) %all-gather.5.cloned.1.call-update) | async-done | bytes 4194320 | tf_op jit(solution)/shard_map/all_gather | solution.py:119
  118.0 3.0 %convolution_add_fusion = f32[32,2048]{1,0:T(8,128)S(1)} fusion(bf16[32,1024]{1,0:T(8,128)(2,1)S(1)} %reshape.307, bf16[1024,2048]{1,0:T(8,128)(2,1)} %all-gather.5.cloned.1.call-done, bf16[32,2048]{1,0:T(8,128)(2,1)S(1)} %convolution_convert_fusion.2), kind=kOutput, calls=%fused_computation.21 | convolution fusion | flops 134348800 | bytes 4653056 | tf_op jit(solution)/shard_map/jvp()/dot_general | solution.py:45
  121.3 1.8 broadcast_in_dim.99
  123.1 7.0 %all-to-all-start.1 = ((bf16[16,34,2048]{2,1,0:T(8,128)(2,1)}), bf16[16,34,2048]{2,1,0:T(8,128)(2,1)S(1)}, u32[]{:S(2)}, u32[]{:S(2)}) async-start(bf16[16,34,2048]{2,1,0:T(8,128)(2,1)} %broadcast_in_dim.99), calls=%async_computation.1 | async-start | bytes 5242880 | tf_op jit(solution)/shard_map/all_to_all | solution.py:150
  130.8 35.6 %all-to-all-done.1 = bf16[16,34,2048]{2,1,0:T(8,128)(2,1)S(1)} async-done(((bf16[16,34,2048]{2,1,0:T(8,128)(2,1)}), bf16[16,34,2048]{2,1,0:T(8,128)(2,1)S(1)}, u32[]{:S(2)}, u32[]{:S(2)}) %all-to-all-start.1) | async-done | bytes 2228256 | tf_op jit(solution)/shard_map/all_to_all | solution.py:150
  171.0 1.8 fusion.24
  174.1 1.6 convolution_convert_fusion.4
  175.9 6.7 %fusion.6 = bf16[640,2048]{1,0:T(8,128)(2,1)} fusion(bf16[640,1024]{0,1:T(8,128)(2,1)S(1)} %bitcast.129, bf16[3,2048,1024]{2,1,0:T(8,128)(2,1)} %all-gather.3.cloned.1.call-done), kind=kOutput, calls=%fused_computation.15 | convolution fusion | flops 2685665280 | bytes 8126464 | tf_op jit(solution)/shard_map/transpose(jvp())/dot_general | solution.py:27
  182.6 6.6 %fusion.7 = bf16[640,2048]{1,0:T(8,128)(2,1)} fusion(bf16[640,1024]{0,1:T(8,128)(2,1)S(1)} %bitcast.130, bf16[3,2048,1024]{2,1,0:T(8,128)(2,1)} %all-gather.3.cloned.1.call-done), kind=kOutput, calls=%fused_computation.16 | convolution fusion | flops 2685665280 | bytes 8126464 | tf_op jit(solution)/shard_map/transpose(jvp())/dot_general | solution.py:32
  189.3 6.1 %fusion.8 = bf16[640,2048]{1,0:T(8,128)(2,1)S(1)} fusion(bf16[640,2048]{1,0:T(8,128)(2,1)} %fusion.7, bf16[640,2048]{1,0:T(8,128)(2,1)} %fusion.6, bf16[32,1024]{1,0:T(8,128)(2,1)S(1)} %reshape.315, bf16[3,2048,1024]{2,1,0:T(8,128)(2,1)} %all-gather.3.cloned.1.call-done, s32[32]{0:T(128)S(1)} %pad_add_fusion), kind=kOutput, calls=%fused_computation.17 | convolution fusion | flops 227364864 | bytes 12124288 | tf_op jit(solution)/shard_map/transpose(jvp())/dot_general | solution.py:49
  195.3 2.5 fusion.9
  197.8 4.7 %convolution_convert_fusion = bf16[16,51,2048]{2,1,0:T(8,128)(2,1)} fusion(bf16[640,2048,1]{1,0,2:T(8,128)(2,1)S(1)} %fusion.9, s32[16,51]{1,0:T(8,128)S(1)} %concatenate.31), kind=kOutput, calls=%fused_computation.13 | convolution fusion | flops 2141288448 | bytes 5967040 | tf_op jit(solution)/shard_map/sop,sd->opd/dot_general | solution.py:203
  202.4 6.7 %all-to-all-start.2 = ((bf16[16,51,2048]{2,1,0:T(8,128)(2,1)}), bf16[16,51,2048]{2,1,0:T(8,128)(2,1)}, u32[]{:S(2)}, u32[]{:S(2)}) async-start(bf16[16,51,2048]{2,1,0:T(8,128)(2,1)} %convolution_convert_fusion), calls=%async_computation.2 | async-start | bytes 7340032 | tf_op jit(solution)/shard_map/all_to_all | solution.py:206
  209.9 48.1 %all-to-all-done.2 = bf16[16,51,2048]{2,1,0:T(8,128)(2,1)} async-done(((bf16[16,51,2048]{2,1,0:T(8,128)(2,1)}), bf16[16,51,2048]{2,1,0:T(8,128)(2,1)}, u32[]{:S(2)}, u32[]{:S(2)}) %all-to-all-start.2) | async-done | bytes 3342368 | tf_op jit(solution)/shard_map/all_to_all | solution.py:206
  258.0 6.7 %bitcast_convert_fusion = bf16[640,2048]{1,0:T(8,128)(2,1)} fusion(bf16[16,51,2048]{2,1,0:T(8,128)(2,1)} %all-to-all-done.2, pred[16,50,640]{2,1,0:T(8,128)(4,1)S(1)} %copy-done.10), kind=kOutput, calls=%fused_computation.1 | convolution fusion | flops 2140405760 | bytes 6475776 | tf_op jit(solution)/shard_map/opk,opd->kd/dot_general | solution.py:207
  (100 shorter events, 21.3 us)
Async XLA Ops:
  7.2 9.2 %copy-start = (bf16[640,2048]{1,0:T(8,128)(2,1)S(1)}, bf16[640,2048]{1,0:T(8,128)(2,1)}, u32[]{:S(2)}) copy-start(bf16[640,2048]{1,0:T(8,128)(2,1)} %param.17) | copy-start | bytes 7864324
  7.2 78.4 %all-gather.3.cloned.1.call-start = ((), (), s32[]{:S(2)}) async-start(), calls=%async_computation.3 | async-start | bytes 14155776 | tf_op jit(solution)/shard_map/all_gather | solution.py:118
  15.5 0.8 copy-start.9
  20.8 8.1 %copy-start.11 = (s32[1,640]{1,0:T(1,128)S(1)}, s32[1,640]{1,0:T(1,128)}, u32[]{:S(2)}) copy-start(s32[1,640]{1,0:T(1,128)} %param.19) | copy-start | bytes 7684
  20.8 8.1 %copy-start.12 = (f32[16]{0:T(128)S(1)}, f32[16]{0:T(128)}, u32[]{:S(2)}) copy-start(f32[16]{0:T(128)} %param.25) | copy-start | bytes 196
  20.8 8.3 %copy-start.13 = (s32[16]{0:T(128)S(1)}, s32[16]{0:T(128)}, u32[]{:S(2)}) copy-start(s32[16]{0:T(128)} %param.23) | copy-start | bytes 196
  20.8 8.3 %copy-start.14 = (s32[16]{0:T(128)S(1)}, s32[16]{0:T(128)}, u32[]{:S(2)}) copy-start(s32[16]{0:T(128)} %param.22) | copy-start | bytes 196
  20.8 57.8 %all-to-all-start = ((bf16[16,51,2048]{2,1,0:T(8,128)(2,1)}), bf16[16,51,2048]{2,1,0:T(8,128)(2,1)}, u32[]{:S(2)}, u32[]{:S(2)}) async-start(bf16[16,51,2048]{2,1,0:T(8,128)(2,1)} %add_convert_fusion), calls=%async_computation | async-start | bytes 7340032 | tf_op jit(solution)/shard_map/all_to_all | solution.py:104
  28.1 89.9 %all-gather.5.cloned.1.call-start = ((), (), s32[]{:S(2)}) async-start(), calls=%async_computation.4 | async-start | bytes 4718592 | tf_op jit(solution)/shard_map/all_gather | solution.py:119
  84.9 4.1 %copy-start.8 = (bf16[640,2048]{1,0:T(8,128)(2,1)}, bf16[640,2048]{1,0:T(8,128)(2,1)S(1)}, u32[]{:S(2)}) copy-start(bf16[640,2048]{1,0:T(8,128)(2,1)S(1)} %bitcast_convert_fusion.1) | copy-start | bytes 7864324
  97.0 7.8 %copy-start.3 = (bf16[640,1024]{0,1:T(8,128)(2,1)}, bf16[640,1024]{0,1:T(8,128)(2,1)S(1)}, u32[]{:S(2)}) copy-start(bf16[640,1024]{0,1:T(8,128)(2,1)S(1)} %copy.28) | copy-start | bytes 3932164
  104.8 1.3 copy-start.7
  105.3 1.4 copy-start.5
  123.1 43.3 %all-to-all-start.1 = ((bf16[16,34,2048]{2,1,0:T(8,128)(2,1)}), bf16[16,34,2048]{2,1,0:T(8,128)(2,1)S(1)}, u32[]{:S(2)}, u32[]{:S(2)}) async-start(bf16[16,34,2048]{2,1,0:T(8,128)(2,1)} %broadcast_in_dim.99), calls=%async_computation.1 | async-start | bytes 5242880 | tf_op jit(solution)/shard_map/all_to_all | solution.py:150
  167.3 2.2 copy-start.2
  169.1 1.9 copy-start.6
  170.8 2.0 copy-start.4
  175.9 6.7 %copy-start.15 = (bf16[16,64,640]{2,1,0:T(8,128)(2,1)S(1)}, bf16[16,64,640]{2,1,0:T(8,128)(2,1)}, u32[]{:S(2)}) copy-start(bf16[16,64,640]{2,1,0:T(8,128)(2,1)} %convolution_convert_fusion.4) | copy-start | bytes 3932164
  202.4 55.6 %copy-start.10 = (pred[16,50,640]{2,1,0:T(8,128)(4,1)S(1)}, pred[16,50,640]{2,1,0:T(8,128)(4,1)}, u32[]{:S(2)}) copy-start(pred[16,50,640]{2,1,0:T(8,128)(4,1)} %copy-done.9) | copy-start | bytes 1536004
  202.4 55.5 %all-to-all-start.2 = ((bf16[16,51,2048]{2,1,0:T(8,128)(2,1)}), bf16[16,51,2048]{2,1,0:T(8,128)(2,1)}, u32[]{:S(2)}, u32[]{:S(2)}) async-start(bf16[16,51,2048]{2,1,0:T(8,128)(2,1)} %convolution_convert_fusion), calls=%async_computation.2 | async-start | bytes 7340032 | tf_op jit(solution)/shard_map/all_to_all | solution.py:206
  258.0 6.7 %copy-start.1 = (bf16[640,2048]{1,0:T(8,128)(2,1)S(1)}, bf16[640,2048]{1,0:T(8,128)(2,1)}, u32[]{:S(2)}) copy-start(bf16[640,2048]{1,0:T(8,128)(2,1)} %param.17) | copy-start | bytes 7864324
Sparse Core Ops, SparseCore 0:
  9.7 69.9 all-gather.2
  81.4 36.5 all-gather.4

commit v7 on v6

--- a/solution.py
+++ b/solution.py
@@ -15,7 +15,7 @@
     return jnp.log(jnp.sum(jnp.exp(values), axis=axis))
 
 
-def attend(query_rows, slot_row_block, qkv_mat, out_mat, query_doc, doc_row):
+def attend(query_rows, slot_row_block, qkv_mat, out_mat, query_doc, doc_row, block_shift):
     query_count = query_rows.shape[0]
     row_count = slot_row_block.shape[0]
     query_h = (
@@ -42,7 +42,8 @@
     attn_prob = (weights / jnp.sum(weights, axis=2, keepdims=True)).astype(jnp.bfloat16)
     mixed = jnp.einsum("hqk,khd->qhd", attn_prob, value_h, preferred_element_type=jnp.float32)
     mixed = mixed.astype(jnp.bfloat16).reshape(query_count, -1)
-    return jnp.dot(mixed, out_mat, preferred_element_type=jnp.float32)
+    out_cols = jnp.einsum("qe,jec->qjc", mixed, out_mat, preferred_element_type=jnp.float32)
+    return jnp.roll(out_cols, block_shift, axis=1).reshape(query_count, -1)
 
 
 def select_rows(onehot, rows):
@@ -114,10 +115,17 @@
     slot_row_block = jnp.einsum(
         "sop,opd->sd", recv_onehot, recv_rows, preferred_element_type=jnp.float32
     ).astype(jnp.bfloat16)
-    qkv_full, out_full = (
-        lax.all_gather(qkv_weight, "fsdp", axis=1, tiled=True),
-        lax.all_gather(out_weight, "fsdp", axis=1, tiled=True),
-    )
+    fsdp_count = lax.axis_size("fsdp")
+    qkv_full = lax.all_gather(qkv_weight, "fsdp", axis=1, tiled=True)
+    fsdp_index = lax.axis_index("fsdp")
+    out_list = [out_weight]
+    for shift in range(1, fsdp_count):
+        out_list.append(
+            lax.ppermute(
+                out_weight, "fsdp", perm=[(i, (i - shift) % fsdp_count) for i in range(fsdp_count)]
+            )
+        )
+    out_blocks = jnp.stack(out_list, axis=0)
     doc_row = doc_ids[0]
     pair_count = fig_slot.shape[0]
     query_slots = jnp.concatenate([fig_slot, cap_slot], axis=0)
@@ -129,7 +137,7 @@
 
     def branch(inputs):
         picked = select_rows(query_onehot, inputs)
-        return attend(picked, inputs, qkv_full, out_full, query_doc, doc_row)
+        return attend(picked, inputs, qkv_full, out_blocks, query_doc, doc_row, fsdp_index)
 
     attn_out, pullback = jax.vjp(branch, slot_row_block)
     query_rows = select_rows(query_onehot, slot_row_block)

time: 272 us -> 307 us (1.13); the launches traced: 271 us -> 301 us
  waiting for transfers between devices: 145 us -> 161 us
  local copies, waits for them, and re-layouts: 8.9 us -> 16 us
  starting transfers between devices: 21.3 us -> 28.1 us
    ppermute x0 -> x7, waiting for transfers between devices: none -> 76.8 us  [body(): lax.ppermute(out_weight, 'fsdp', perm=[(i, (i - shift) % fsdp_count) for...]
    all_to_all x1, waiting for transfers between devices: 49.1 us -> 0.01 us  [body(): lax.all_to_all(send_rows, 'dp', split_axis=0, concat_axis=0, tiled=True)]
    all_gather x2 -> x1, waiting for transfers between devices: 11.1 us -> 0.02 us  [body(): qkv_full = lax.all_gather(qkv_weight, 'fsdp', axis=1, tiled=True)]
    ppermute x0 -> x7, starting transfers between devices: none -> 7.59 us  [body(): lax.ppermute(out_weight, 'fsdp', perm=[(i, (i - shift) % fsdp_count) for...]
    unnamed x33 -> x42, local copies, waits for them, and re-layouts: 1.97 us -> 8.17 us
  transfers between devices with their start and end apart: 5 -> 11, of which waited for: 4 -> 7; matrix products, arithmetic and copies ran while one was open for 15% -> 9% of each run, Pallas kernels for 0% -> 0%
where the time goes in v7:
time: 307 us; the launch traced here: 301 us
  waiting for transfers between devices  161 us (52%)
  matrix products  72.1 us (23%)
  starting transfers between devices  28.1 us (9%)
  local copies, waits for them, and re-layouts  16 us (5%)
  between operations  15.7 us (5%)
  other arithmetic  8.83 us (3%)
    ppermute x7, waiting for transfers between devices, body(): lax.ppermute(out_weight, 'fsdp', perm=[(i, (i - shift) % fsdp_count) for...  76.8 us
    all_to_all x1, waiting for transfers between devices, body(): lax.all_to_all(back_rows, 'dp', split_axis=0, concat_axis=0, tiled=True)  47.2 us
    all_to_all x1, waiting for transfers between devices, body(): lax.all_to_all(jnp.broadcast_to(both_emb[None], (dp_count,) + both_emb.sh...  35.9 us
    dot_general x2, matrix products, attend(): jnp.dot(slot_row_block, qkv_mat[2], preferred_element_type=jnp.float32)  12.9 us
    dot_general x2, matrix products, attend(): jnp.dot(slot_row_block, qkv_mat[1], preferred_element_type=jnp.float32)  12.8 us
    unnamed x42, local copies, waits for them, and re-layouts  8.17 us
    ppermute x7, starting transfers between devices, body(): lax.ppermute(out_weight, 'fsdp', perm=[(i, (i - shift) % fsdp_count) for...  7.59 us
    all_to_all x1, starting transfers between devices, body(): lax.all_to_all(jnp.broadcast_to(both_emb[None], (dp_count,) + both_emb.sh...  7.35 us
  transfers between devices with their start and end apart: 11, of which 7 were waited for; matrix products, arithmetic and copies ran while one was open for 9% of the time, Pallas kernels for 0%

profile of v7, /device:TPU:0, one launch (start us, length us, event | category | flops | bytes accessed | tf_op | source)
XLA Modules:
  0.0 301.3 jit_solution(7532404522259744521)
XLA Ops:
  16.3 4.5 %add_convert_fusion = bf16[16,51,2048]{2,1,0:T(8,128)(2,1)} fusion(f32[16,1,2048]{2,1,0:T(1,128)S(1)} %scatter.15, bf16[640,2048]{1,0:T(8,128)(2,1)S(1)} %copy-done, pred[16,50,640]{2,1,0:T(8,128)(4,1)S(1)} %broadcast_compare_fusion), kind=kOutput, calls=%fused_computation | convolution fusion | flops 2142437376 | bytes 6606848 | tf_op jit(solution)/shard_map/opk,kd->opd/dot_general | solution.py:102
  20.8 7.3 %all-to-all-start = ((bf16[16,51,2048]{2,1,0:T(8,128)(2,1)}), bf16[16,51,2048]{2,1,0:T(8,128)(2,1)}, u32[]{:S(2)}, u32[]{:S(2)}) async-start(bf16[16,51,2048]{2,1,0:T(8,128)(2,1)} %add_convert_fusion), calls=%async_computation | async-start | bytes 7340032 | tf_op jit(solution)/shard_map/all_to_all | solution.py:105
  28.2 3.2 %collective-permute-start = (bf16[1024,256]{1,0:T(8,128)(2,1)S(1)}, bf16[1024,256]{1,0:T(8,128)(2,1)S(1)}, u32[]{:S(2)}, u32[]{:S(2)}) collective-permute-start(bf16[1024,256]{1,0:T(8,128)(2,1)S(1)} %copy-done.11), channel_id=1, source_target_pairs={{0,7},{1,0},{2,1},{3,2},{4,3},{5,4},{6,5},{7,6},{8,15},{9,8},{10,9... | collective-permute-start | bytes 1572872 | tf_op jit(solution)/shard_map/ppermute | solution.py:124
  32.3 3.3 %collective-permute-start.3 = (bf16[1024,256]{1,0:T(8,128)(2,1)S(1)}, bf16[1024,256]{1,0:T(8,128)(2,1)S(1)}, u32[]{:S(2)}, u32[]{:S(2)}) collective-permute-start(bf16[1024,256]{1,0:T(8,128)(2,1)S(1)} %copy-done.11), channel_id=1, source_target_pairs={{0,4},{1,5},{2,6},{3,7},{4,0},{5,1},{6,2},{7,3},{8,12},{9,13},{10,... | collective-permute-start | bytes 1572872 | tf_op jit(solution)/shard_map/ppermute | solution.py:124
  37.1 17.7 %collective-permute-done = bf16[1024,256]{1,0:T(8,128)(2,1)S(1)} collective-permute-done((bf16[1024,256]{1,0:T(8,128)(2,1)S(1)}, bf16[1024,256]{1,0:T(8,128)(2,1)S(1)}, u32[]{:S(2)}, u32[]{:S(2)}) %collective-permute-start) | collective-permute-done | bytes 524320 | tf_op jit(solution)/shard_map/ppermute | solution.py:124
  55.8 22.0 %collective-permute-done.1 = bf16[1024,256]{1,0:T(8,128)(2,1)S(1)} collective-permute-done((bf16[1024,256]{1,0:T(8,128)(2,1)S(1)}, bf16[1024,256]{1,0:T(8,128)(2,1)S(1)}, u32[]{:S(2)}, u32[]{:S(2)}) %collective-permute-start.1) | collective-permute-done | bytes 524320 | tf_op jit(solution)/shard_map/ppermute | solution.py:124
  79.5 2.5 collective-permute-done.3
  82.9 17.1 %collective-permute-done.4 = bf16[1024,256]{1,0:T(8,128)(2,1)S(1)} collective-permute-done((bf16[1024,256]{1,0:T(8,128)(2,1)S(1)}, bf16[1024,256]{1,0:T(8,128)(2,1)S(1)}, u32[]{:S(2)}, u32[]{:S(2)}) %collective-permute-start.4) | collective-permute-done | bytes 524320 | tf_op jit(solution)/shard_map/ppermute | solution.py:124
  100.8 17.4 %collective-permute-done.5 = bf16[1024,256]{1,0:T(8,128)(2,1)S(1)} collective-permute-done((bf16[1024,256]{1,0:T(8,128)(2,1)S(1)}, bf16[1024,256]{1,0:T(8,128)(2,1)S(1)}, u32[]{:S(2)}, u32[]{:S(2)}) %collective-permute-start.5) | collective-permute-done | bytes 524320 | tf_op jit(solution)/shard_map/ppermute | solution.py:124
  121.2 5.1 %bitcast_convert_fusion.1 = bf16[640,2048]{1,0:T(8,128)(2,1)S(1)} fusion(bf16[16,51,2048]{2,1,0:T(8,128)(2,1)} %all-to-all-done, s32[16,51]{1,0:T(8,128)S(1)} %concatenate.35), kind=kOutput, calls=%fused_computation.2 | convolution fusion | flops 2140928000 | bytes 5967040 | tf_op jit(solution)/shard_map/sop,opd->sd/dot_general | solution.py:115
  126.9 3.3 %fusion.29 = bf16[32,1024]{1,0:T(8,128)(2,1)S(1)} fusion(bf16[32,2048]{1,0:T(8,128)(2,1)S(1)} %convolution_convert_fusion.2, bf16[3,2048,1024]{2,1,0:T(8,128)(2,1)} %all-gather.2.cloned.1.call-done), kind=kOutput, calls=%fused_computation.56 | convolution fusion | flops 134250496 | bytes 4390912 | tf_op jit(solution)/shard_map/jvp()/dot_general | solution.py:22
  130.4 6.1 %fusion.15 = bf16[640,1024]{1,0:T(8,128)(2,1)} fusion(bf16[640,2048]{1,0:T(8,128)(2,1)S(1)} %bitcast_convert_fusion.1, bf16[3,2048,1024]{2,1,0:T(8,128)(2,1)} %all-gather.2.cloned.1.call-done), kind=kOutput, calls=%fused_computation.32 | convolution fusion | flops 2685009920 | bytes 8126464 | tf_op jit(solution)/shard_map/jvp()/dot_general | solution.py:27
  138.2 6.3 %fusion.16 = bf16[640,1024]{1,0:T(8,128)(2,1)S(1)} fusion(bf16[640,2048]{1,0:T(8,128)(2,1)} %copy-done.8, bf16[3,2048,1024]{2,1,0:T(8,128)(2,1)} %all-gather.2.cloned.1.call-done), kind=kOutput, calls=%fused_computation.33 | convolution fusion | flops 2685009920 | bytes 8126464 | tf_op jit(solution)/shard_map/jvp()/dot_general | solution.py:32
  148.1 3.0 fusion.76
  153.3 7.4 %all-to-all-start.1 = ((bf16[16,34,2048]{2,1,0:T(8,128)(2,1)}), bf16[16,34,2048]{2,1,0:T(8,128)(2,1)S(1)}, u32[]{:S(2)}, u32[]{:S(2)}) async-start(bf16[16,34,2048]{2,1,0:T(8,128)(2,1)} %broadcast_in_dim.103), calls=%async_computation.1 | async-start | bytes 5242880 | tf_op jit(solution)/shard_map/all_to_all | solution.py:158
  161.4 35.9 %all-to-all-done.1 = bf16[16,34,2048]{2,1,0:T(8,128)(2,1)S(1)} async-done(((bf16[16,34,2048]{2,1,0:T(8,128)(2,1)}), bf16[16,34,2048]{2,1,0:T(8,128)(2,1)S(1)}, u32[]{:S(2)}, u32[]{:S(2)}) %all-to-all-start.1) | async-done | bytes 2228256 | tf_op jit(solution)/shard_map/all_to_all | solution.py:158
  207.1 6.7 %fusion.6 = bf16[640,2048]{1,0:T(8,128)(2,1)} fusion(bf16[640,1024]{0,1:T(8,128)(2,1)S(1)} %bitcast.157, bf16[3,2048,1024]{2,1,0:T(8,128)(2,1)} %all-gather.2.cloned.1.call-done), kind=kOutput, calls=%fused_computation.15 | convolution fusion | flops 2685665280 | bytes 8126464 | tf_op jit(solution)/shard_map/transpose(jvp())/dot_general | solution.py:27
  213.8 6.6 %fusion.7 = bf16[640,2048]{1,0:T(8,128)(2,1)} fusion(bf16[640,1024]{0,1:T(8,128)(2,1)S(1)} %bitcast.158, bf16[3,2048,1024]{2,1,0:T(8,128)(2,1)} %all-gather.2.cloned.1.call-done), kind=kOutput, calls=%fused_computation.16 | convolution fusion | flops 2685665280 | bytes 8126464 | tf_op jit(solution)/shard_map/transpose(jvp())/dot_general | solution.py:32
  220.4 6.1 %fusion.8 = bf16[640,2048]{1,0:T(8,128)(2,1)S(1)} fusion(bf16[640,2048]{1,0:T(8,128)(2,1)} %fusion.7, bf16[640,2048]{1,0:T(8,128)(2,1)} %fusion.6, bf16[32,1024]{1,0:T(8,128)(2,1)S(1)} %reshape.323, bf16[3,2048,1024]{2,1,0:T(8,128)(2,1)} %all-gather.2.cloned.1.call-done, s32[32]{0:T(128)S(1)} %pad_add_fusion), kind=kOutput, calls=%fused_computation.17 | convolution fusion | flops 227364864 | bytes 12124288 | tf_op jit(solution)/shard_map/transpose(jvp())/dot_general | solution.py:50
  226.5 2.5 fusion.9
  229.0 4.7 %convolution_convert_fusion = bf16[16,51,2048]{2,1,0:T(8,128)(2,1)} fusion(bf16[640,2048,1]{1,0,2:T(8,128)(2,1)S(1)} %fusion.9, s32[16,51]{1,0:T(8,128)S(1)} %concatenate.35), kind=kOutput, calls=%fused_computation.13 | convolution fusion | flops 2141288448 | bytes 5967040 | tf_op jit(solution)/shard_map/sop,sd->opd/dot_general | solution.py:211
  233.7 5.8 %all-to-all-start.2 = ((bf16[16,51,2048]{2,1,0:T(8,128)(2,1)}), bf16[16,51,2048]{2,1,0:T(8,128)(2,1)}, u32[]{:S(2)}, u32[]{:S(2)}) async-start(bf16[16,51,2048]{2,1,0:T(8,128)(2,1)} %convolution_convert_fusion), calls=%async_computation.2 | async-start | bytes 7340032 | tf_op jit(solution)/shard_map/all_to_all | solution.py:214
  240.2 47.2 %all-to-all-done.2 = bf16[16,51,2048]{2,1,0:T(8,128)(2,1)} async-done(((bf16[16,51,2048]{2,1,0:T(8,128)(2,1)}), bf16[16,51,2048]{2,1,0:T(8,128)(2,1)}, u32[]{:S(2)}, u32[]{:S(2)}) %all-to-all-start.2) | async-done | bytes 3342368 | tf_op jit(solution)/shard_map/all_to_all | solution.py:214
  287.4 6.7 %bitcast_convert_fusion = bf16[640,2048]{1,0:T(8,128)(2,1)} fusion(bf16[16,51,2048]{2,1,0:T(8,128)(2,1)} %all-to-all-done.2, pred[16,50,640]{2,1,0:T(8,128)(4,1)S(1)} %copy-done.10), kind=kOutput, calls=%fused_computation.1 | convolution fusion | flops 2140405760 | bytes 6475776 | tf_op jit(solution)/shard_map/opk,opd->kd/dot_general | solution.py:215
  (127 shorter events, 37.3 us)
Async XLA Ops:
  7.2 9.2 %copy-start = (bf16[640,2048]{1,0:T(8,128)(2,1)S(1)}, bf16[640,2048]{1,0:T(8,128)(2,1)}, u32[]{:S(2)}) copy-start(bf16[640,2048]{1,0:T(8,128)(2,1)} %param.17) | copy-start | bytes 7864324
  7.2 119.7 %all-gather.2.cloned.1.call-start = ((), (), s32[]{:S(2)}) async-start(), calls=%async_computation.3 | async-start | bytes 14155776 | tf_op jit(solution)/shard_map/all_gather | solution.py:119
  20.8 7.3 %copy-start.11 = (bf16[1024,256]{1,0:T(8,128)(2,1)S(1)}, bf16[1024,256]{1,0:T(8,128)(2,1)}, u32[]{:S(2)}) copy-start(bf16[1024,256]{1,0:T(8,128)(2,1)} %param.21) | copy-start | bytes 1572868
  20.8 14.8 %copy-start.12 = (s32[1,640]{1,0:T(1,128)S(1)}, s32[1,640]{1,0:T(1,128)}, u32[]{:S(2)}) copy-start(s32[1,640]{1,0:T(1,128)} %param.19) | copy-start | bytes 7684
  20.8 14.8 %copy-start.13 = (s32[16]{0:T(128)S(1)}, s32[16]{0:T(128)}, u32[]{:S(2)}) copy-start(s32[16]{0:T(128)} %param.23) | copy-start | bytes 196
  20.8 14.8 %copy-start.14 = (s32[16]{0:T(128)S(1)}, s32[16]{0:T(128)}, u32[]{:S(2)}) copy-start(s32[16]{0:T(128)} %param.22) | copy-start | bytes 196
  20.8 16.0 %copy-start.15 = (f32[16]{0:T(128)S(1)}, f32[16]{0:T(128)}, u32[]{:S(2)}) copy-start(f32[16]{0:T(128)} %param.25) | copy-start | bytes 196
  20.8 99.1 %all-to-all-start = ((bf16[16,51,2048]{2,1,0:T(8,128)(2,1)}), bf16[16,51,2048]{2,1,0:T(8,128)(2,1)}, u32[]{:S(2)}, u32[]{:S(2)}) async-start(bf16[16,51,2048]{2,1,0:T(8,128)(2,1)} %add_convert_fusion), calls=%async_computation | async-start | bytes 7340032 | tf_op jit(solution)/shard_map/all_to_all | solution.py:105
  28.2 26.6 %collective-permute-start = (bf16[1024,256]{1,0:T(8,128)(2,1)S(1)}, bf16[1024,256]{1,0:T(8,128)(2,1)S(1)}, u32[]{:S(2)}, u32[]{:S(2)}) collective-permute-start(bf16[1024,256]{1,0:T(8,128)(2,1)S(1)} %copy-done.11), channel_id=1, source_target_pairs={{0,7},{1,0},{2,1},{3,2},{4,3},{5,4},{6,5},{7,6},{8,15},{9,8},{10,9... | collective-permute-start | bytes 1572872 | tf_op jit(solution)/shard_map/ppermute | solution.py:124
  31.4 46.5 %collective-permute-start.1 = (bf16[1024,256]{1,0:T(8,128)(2,1)S(1)}, bf16[1024,256]{1,0:T(8,128)(2,1)S(1)}, u32[]{:S(2)}, u32[]{:S(2)}) collective-permute-start(bf16[1024,256]{1,0:T(8,128)(2,1)S(1)} %copy-done.11), channel_id=1, source_target_pairs={{0,6},{1,7},{2,0},{3,1},{4,2},{5,3},{6,4},{7,5},{8,14},{9,15},{10,... | collective-permute-start | bytes 1572872 | tf_op jit(solution)/shard_map/ppermute | solution.py:124
  32.3 46.4 %collective-permute-start.2 = (bf16[1024,256]{1,0:T(8,128)(2,1)S(1)}, bf16[1024,256]{1,0:T(8,128)(2,1)S(1)}, u32[]{:S(2)}, u32[]{:S(2)}) collective-permute-start(bf16[1024,256]{1,0:T(8,128)(2,1)S(1)} %copy-done.11), channel_id=1, source_target_pairs={{0,5},{1,6},{2,7},{3,0},{4,1},{5,2},{6,3},{7,4},{8,13},{9,14},{10,... | collective-permute-start | bytes 1572872 | tf_op jit(solution)/shard_map/ppermute | solution.py:124
  32.3 49.7 %collective-permute-start.3 = (bf16[1024,256]{1,0:T(8,128)(2,1)S(1)}, bf16[1024,256]{1,0:T(8,128)(2,1)S(1)}, u32[]{:S(2)}, u32[]{:S(2)}) collective-permute-start(bf16[1024,256]{1,0:T(8,128)(2,1)S(1)} %copy-done.11), channel_id=1, source_target_pairs={{0,4},{1,5},{2,6},{3,7},{4,0},{5,1},{6,2},{7,3},{8,12},{9,13},{10,... | collective-permute-start | bytes 1572872 | tf_op jit(solution)/shard_map/ppermute | solution.py:124
  35.6 64.4 %collective-permute-start.4 = (bf16[1024,256]{1,0:T(8,128)(2,1)S(1)}, bf16[1024,256]{1,0:T(8,128)(2,1)S(1)}, u32[]{:S(2)}, u32[]{:S(2)}) collective-permute-start(bf16[1024,256]{1,0:T(8,128)(2,1)S(1)} %copy-done.11), channel_id=1, source_target_pairs={{0,3},{1,4},{2,5},{3,6},{4,7},{5,0},{6,1},{7,2},{8,11},{9,12},{10,... | collective-permute-start | bytes 1572872 | tf_op jit(solution)/shard_map/ppermute | solution.py:124
  54.8 63.5 %collective-permute-start.5 = (bf16[1024,256]{1,0:T(8,128)(2,1)S(1)}, bf16[1024,256]{1,0:T(8,128)(2,1)S(1)}, u32[]{:S(2)}, u32[]{:S(2)}) collective-permute-start(bf16[1024,256]{1,0:T(8,128)(2,1)S(1)} %copy-done.11), channel_id=1, source_target_pairs={{0,2},{1,3},{2,4},{3,5},{4,6},{5,7},{6,0},{7,1},{8,10},{9,11},{10,... | collective-permute-start | bytes 1572872 | tf_op jit(solution)/shard_map/ppermute | solution.py:124
  77.9 41.2 %collective-permute-start.6 = (bf16[1024,256]{1,0:T(8,128)(2,1)S(1)}, bf16[1024,256]{1,0:T(8,128)(2,1)S(1)}, u32[]{:S(2)}, u32[]{:S(2)}) collective-permute-start(bf16[1024,256]{1,0:T(8,128)(2,1)S(1)} %copy-done.11), channel_id=1, source_target_pairs={{0,1},{1,2},{2,3},{3,4},{4,5},{5,6},{6,7},{7,0},{8,9},{9,10},{10,1... | collective-permute-start | bytes 1572872 | tf_op jit(solution)/shard_map/ppermute | solution.py:124
  126.3 4.1 %copy-start.8 = (bf16[640,2048]{1,0:T(8,128)(2,1)}, bf16[640,2048]{1,0:T(8,128)(2,1)S(1)}, u32[]{:S(2)}) copy-start(bf16[640,2048]{1,0:T(8,128)(2,1)S(1)} %bitcast_convert_fusion.1) | copy-start | bytes 7864324
  138.2 7.8 %copy-start.3 = (bf16[640,1024]{0,1:T(8,128)(2,1)}, bf16[640,1024]{0,1:T(8,128)(2,1)S(1)}, u32[]{:S(2)}) copy-start(bf16[640,1024]{0,1:T(8,128)(2,1)S(1)} %copy.32) | copy-start | bytes 3932164
  153.3 43.9 %all-to-all-start.1 = ((bf16[16,34,2048]{2,1,0:T(8,128)(2,1)}), bf16[16,34,2048]{2,1,0:T(8,128)(2,1)S(1)}, u32[]{:S(2)}, u32[]{:S(2)}) async-start(bf16[16,34,2048]{2,1,0:T(8,128)(2,1)} %broadcast_in_dim.103), calls=%async_computation.1 | async-start | bytes 5242880 | tf_op jit(solution)/shard_map/all_to_all | solution.py:158
  198.4 2.2 copy-start.2
  200.1 2.0 copy-start.6
  207.1 6.7 %copy-start.16 = (bf16[16,64,640]{2,1,0:T(8,128)(2,1)S(1)}, bf16[16,64,640]{2,1,0:T(8,128)(2,1)}, u32[]{:S(2)}) copy-start(bf16[16,64,640]{2,1,0:T(8,128)(2,1)} %convolution_convert_fusion.4) | copy-start | bytes 3932164
  233.7 53.7 %copy-start.10 = (pred[16,50,640]{2,1,0:T(8,128)(4,1)S(1)}, pred[16,50,640]{2,1,0:T(8,128)(4,1)}, u32[]{:S(2)}) copy-start(pred[16,50,640]{2,1,0:T(8,128)(4,1)} %copy-done.9) | copy-start | bytes 1536004
  233.7 53.7 %all-to-all-start.2 = ((bf16[16,51,2048]{2,1,0:T(8,128)(2,1)}), bf16[16,51,2048]{2,1,0:T(8,128)(2,1)}, u32[]{:S(2)}, u32[]{:S(2)}) async-start(bf16[16,51,2048]{2,1,0:T(8,128)(2,1)} %convolution_convert_fusion), calls=%async_computation.2 | async-start | bytes 7340032 | tf_op jit(solution)/shard_map/all_to_all | solution.py:214
  287.4 6.7 %copy-start.1 = (bf16[640,2048]{1,0:T(8,128)(2,1)S(1)}, bf16[640,2048]{1,0:T(8,128)(2,1)}, u32[]{:S(2)}) copy-start(bf16[640,2048]{1,0:T(8,128)(2,1)} %param.17) | copy-start | bytes 7864324
  (4 other events, 5.6 us)
Sparse Core Ops, SparseCore 0:
  9.7 114.9 all-gather.1

commit v8 on v6

--- a/solution.py
+++ b/solution.py
@@ -15,7 +15,7 @@
     return jnp.log(jnp.sum(jnp.exp(values), axis=axis))
 
 
-def attend(query_rows, slot_row_block, qkv_mat, out_mat, query_doc, doc_row):
+def attend(query_rows, slot_row_block, qkv_mat, kv_mat, out_mat, query_doc, doc_row):
     query_count = query_rows.shape[0]
     row_count = slot_row_block.shape[0]
     query_h = (
@@ -23,16 +23,12 @@
         .astype(jnp.bfloat16)
         .reshape(query_count, -1, HD)
     )
-    key_h = (
-        jnp.dot(slot_row_block, qkv_mat[1], preferred_element_type=jnp.float32)
-        .astype(jnp.bfloat16)
-        .reshape(row_count, -1, HD)
-    )
-    value_h = (
-        jnp.dot(slot_row_block, qkv_mat[2], preferred_element_type=jnp.float32)
-        .astype(jnp.bfloat16)
-        .reshape(row_count, -1, HD)
-    )
+    key_value = jnp.dot(slot_row_block, kv_mat, preferred_element_type=jnp.float32).astype(
+        jnp.bfloat16
+    )
+    head_width = qkv_mat.shape[2]
+    key_h = key_value[:, :head_width].reshape(row_count, -1, HD)
+    value_h = key_value[:, head_width:].reshape(row_count, -1, HD)
     scores = jnp.einsum("qhd,khd->hqk", query_h, key_h, preferred_element_type=jnp.float32) * (
         1.0 / math.sqrt(HD)
     )
@@ -118,6 +114,7 @@
         lax.all_gather(qkv_weight, "fsdp", axis=1, tiled=True),
         lax.all_gather(out_weight, "fsdp", axis=1, tiled=True),
     )
+    kv_full = jnp.concatenate([qkv_full[1], qkv_full[2]], axis=1)
     doc_row = doc_ids[0]
     pair_count = fig_slot.shape[0]
     query_slots = jnp.concatenate([fig_slot, cap_slot], axis=0)
@@ -129,7 +126,7 @@
 
     def branch(inputs):
         picked = select_rows(query_onehot, inputs)
-        return attend(picked, inputs, qkv_full, out_full, query_doc, doc_row)
+        return attend(picked, inputs, qkv_full, kv_full, out_full, query_doc, doc_row)
 
     attn_out, pullback = jax.vjp(branch, slot_row_block)
     query_rows = select_rows(query_onehot, slot_row_block)

time: 272 us -> 268 us (0.985)
  matrix products: 72.3 us -> 60.5 us
  local copies, waits for them, and re-layouts: 8.9 us -> 13.9 us
  waiting for transfers between devices: 145 us -> 148 us
    dot_general x4 -> x2, matrix products: 25.9 us -> 15.6 us  [attend(): jnp.dot(slot_row_block, kv_mat, preferred_element_type=jnp.float32)]
    squeeze x0 -> x1, local copies, waits for them, and re-layouts: none -> 3.94 us  [body(): kv_full = jnp.concatenate([qkv_full[1], qkv_full[2]], axis=1)]
    slice x0 -> x3, local copies, waits for them, and re-layouts: none -> 3.26 us  [the longest x2 1.74 us: attend(): value_h = key_value[:, head_width:].reshape(row_count, -1, HD)]
    convert_element_type x2 -> x0, local copies, waits for them, and re-layouts: 3.14 us -> none  [the longest x1 1.7 us: attend(): key_h = jnp.dot(slot_row_block, qkv_mat[1], preferred_element_type=jnp.fl...]
  transfers between devices with their start and end apart: 5 -> 5, of which waited for: 4 -> 4; matrix products, arithmetic and copies ran while one was open for 15% -> 14% of each run, Pallas kernels for 0% -> 0%
where the time goes in v8:
time: 268 us; the launch traced here: 267 us
  waiting for transfers between devices  148 us (55%)
  matrix products  60.5 us (23%)
  starting transfers between devices  21.1 us (8%)
  between operations  15.2 us (6%)
  local copies, waits for them, and re-layouts  13.9 us (5%)
  other arithmetic  8.73 us (3%)
    all_to_all x1, waiting for transfers between devices, body(): lax.all_to_all(send_rows, 'dp', split_axis=0, concat_axis=0, tiled=True)  49.1 us
    all_to_all x1, waiting for transfers between devices, body(): lax.all_to_all(back_rows, 'dp', split_axis=0, concat_axis=0, tiled=True)  48.1 us
    all_to_all x1, waiting for transfers between devices, body(): lax.all_to_all(jnp.broadcast_to(both_emb[None], (dp_count,) + both_emb.sh...  35.8 us
    dot_general x2, matrix products, attend(): jnp.dot(slot_row_block, kv_mat, preferred_element_type=jnp.float32)  15.6 us
    all_gather x1, waiting for transfers between devices, body(): lax.all_gather(out_weight, 'fsdp', axis=1, tiled=True)  13.7 us
    all_to_all x1, starting transfers between devices, body(): lax.all_to_all(send_rows, 'dp', split_axis=0, concat_axis=0, tiled=True)  7.31 us
    all_to_all x1, starting transfers between devices, body(): lax.all_to_all(jnp.broadcast_to(both_emb[None], (dp_count,) + both_emb.sh...  6.8 us
    all_to_all x1, starting transfers between devices, body(): lax.all_to_all(back_rows, 'dp', split_axis=0, concat_axis=0, tiled=True)  6.7 us
  transfers between devices with their start and end apart: 5, of which 4 were waited for; matrix products, arithmetic and copies ran while one was open for 14% of the time, Pallas kernels for 0%

profile of v8, /device:TPU:0, one launch (start us, length us, event | category | flops | bytes accessed | tf_op | source)
XLA Modules:
  0.0 267.2 jit_solution(11704543807658158003)
XLA Ops:
  8.7 1.4 reduce-window.6
  16.3 4.5 %add_convert_fusion = bf16[16,51,2048]{2,1,0:T(8,128)(2,1)} fusion(f32[16,1,2048]{2,1,0:T(1,128)S(1)} %scatter.15, bf16[640,2048]{1,0:T(8,128)(2,1)S(1)} %copy-done, pred[16,50,640]{2,1,0:T(8,128)(4,1)S(1)} %broadcast_compare_fusion), kind=kOutput, calls=%fused_computation.1 | convolution fusion | flops 2142437376 | bytes 6606848 | tf_op jit(solution)/shard_map/opk,kd->opd/dot_general | solution.py:97
  20.8 7.3 %all-to-all-start = ((bf16[16,51,2048]{2,1,0:T(8,128)(2,1)}), bf16[16,51,2048]{2,1,0:T(8,128)(2,1)}, u32[]{:S(2)}, u32[]{:S(2)}) async-start(bf16[16,51,2048]{2,1,0:T(8,128)(2,1)} %add_convert_fusion), calls=%async_computation | async-start | bytes 7340032 | tf_op jit(solution)/shard_map/all_to_all | solution.py:100
  29.5 49.1 %all-to-all-done = bf16[16,51,2048]{2,1,0:T(8,128)(2,1)} async-done(((bf16[16,51,2048]{2,1,0:T(8,128)(2,1)}), bf16[16,51,2048]{2,1,0:T(8,128)(2,1)}, u32[]{:S(2)}, u32[]{:S(2)}) %all-to-all-start) | async-done | bytes 3342368 | tf_op jit(solution)/shard_map/all_to_all | solution.py:100
  79.8 5.1 %bitcast_convert_fusion.1 = bf16[640,2048]{1,0:T(8,128)(2,1)S(1)} fusion(bf16[16,51,2048]{2,1,0:T(8,128)(2,1)} %all-to-all-done, s32[16,51]{1,0:T(8,128)S(1)} %concatenate.34), kind=kOutput, calls=%fused_computation.5 | convolution fusion | flops 2140928000 | bytes 5967040 | tf_op jit(solution)/shard_map/sop,opd->sd/dot_general | solution.py:110
  85.5 3.9 %slice_bitcast_fusion.2 = (bf16[2048,1024]{1,0:T(8,128)(2,1)S(1)}, bf16[2048,1024]{1,0:T(8,128)(2,1)S(1)}) fusion(bf16[3,2048,1024]{2,1,0:T(8,128)(2,1)} %all-gather.3.cloned.1.call-done), kind=kLoop, calls=%fused_computation.9 | loop fusion | bytes 16777216 | tf_op jit(solution)/shard_map/squeeze | solution.py:117
  89.5 6.1 %fusion.4 = bf16[640,2048]{1,0:T(8,128)(2,1)S(1)} fusion(bf16[640,2048]{1,0:T(8,128)(2,1)S(1)} %bitcast_convert_fusion.1, bf16[2048,1024]{1,0:T(8,128)(2,1)S(1)} %get-tuple-element.58, bf16[2048,1024]{1,0:T(8,128)(2,1)S(1)} %get-tuple-element.57), kind=kOutput, calls=%fused_computation.14 | convolution fusion | flops 5386797056 | bytes 13631488 | tf_op jit(solution)/shard_map/jvp()/dot_general | solution.py:26
  95.9 1.5 copy.28
  97.4 3.1 %fusion.28 = bf16[32,1024]{1,0:T(8,128)(2,1)S(1)} fusion(bf16[32,2048]{1,0:T(8,128)(2,1)S(1)} %convolution_convert_fusion.2, bf16[3,2048,1024]{2,1,0:T(8,128)(2,1)} %all-gather.3.cloned.1.call-done), kind=kOutput, calls=%fused_computation.56 | convolution fusion | flops 134250496 | bytes 4390912 | tf_op jit(solution)/shard_map/jvp()/dot_general | solution.py:22
  100.6 1.5 copy.27
  104.3 13.7 %all-gather.5.cloned.1.call-done = bf16[1024,2048]{1,0:T(8,128)(2,1)} async-done(((bf16[1024,256]{1,0:T(8,128)(2,1)}), bf16[1024,2048]{1,0:T(8,128)(2,1)}) %all-gather.5.cloned.1.call-update) | async-done | bytes 4194320 | tf_op jit(solution)/shard_map/all_gather | solution.py:115
  118.0 3.0 %convolution_add_fusion = f32[32,2048]{1,0:T(8,128)S(1)} fusion(bf16[32,1024]{1,0:T(8,128)(2,1)S(1)} %reshape.307, bf16[1024,2048]{1,0:T(8,128)(2,1)} %all-gather.5.cloned.1.call-done, bf16[32,2048]{1,0:T(8,128)(2,1)S(1)} %convolution_convert_fusion.2), kind=kOutput, calls=%fused_computation.23 | convolution fusion | flops 134348800 | bytes 4653056 | tf_op jit(solution)/shard_map/jvp()/dot_general | solution.py:41
  121.3 1.8 broadcast_in_dim.99
  123.1 6.8 %all-to-all-start.1 = ((bf16[16,34,2048]{2,1,0:T(8,128)(2,1)}), bf16[16,34,2048]{2,1,0:T(8,128)(2,1)S(1)}, u32[]{:S(2)}, u32[]{:S(2)}) async-start(bf16[16,34,2048]{2,1,0:T(8,128)(2,1)} %broadcast_in_dim.99), calls=%async_computation.1 | async-start | bytes 5242880 | tf_op jit(solution)/shard_map/all_to_all | solution.py:147
  130.6 35.8 %all-to-all-done.1 = bf16[16,34,2048]{2,1,0:T(8,128)(2,1)S(1)} async-done(((bf16[16,34,2048]{2,1,0:T(8,128)(2,1)}), bf16[16,34,2048]{2,1,0:T(8,128)(2,1)S(1)}, u32[]{:S(2)}, u32[]{:S(2)}) %all-to-all-start.1) | async-done | bytes 2228256 | tf_op jit(solution)/shard_map/all_to_all | solution.py:147
  170.9 1.6 convolution_convert_fusion.4
  174.5 1.7 convolution_convert_fusion.3
  176.4 9.5 %fusion.5 = bf16[640,2048]{1,0:T(8,128)(2,1)} fusion(bf16[2048,1024]{1,0:T(8,128)(2,1)} %copy-done.10, bf16[2048,1024]{1,0:T(8,128)(2,1)} %copy-done.9, bf16[640,1024]{0,1:T(8,128)(2,1)} %bitcast.115, bf16[640,1024]{0,1:T(8,128)(2,1)S(1)} %bitcast.114), kind=kOutput, calls=%fused_computation.15 | convolution fusion | flops 5392039936 | bytes 13631488 | tf_op jit(solution)/shard_map/transpose(jvp())/dot_general | solution.py:26
  186.0 5.1 %fusion.6 = bf16[640,2048]{1,0:T(8,128)(2,1)S(1)} fusion(bf16[640,2048]{1,0:T(8,128)(2,1)} %fusion.5, bf16[32,1024]{1,0:T(8,128)(2,1)S(1)} %reshape.315, bf16[3,2048,1024]{2,1,0:T(8,128)(2,1)} %all-gather.3.cloned.1.call-done, s32[32]{0:T(128)S(1)} %pad_add_fusion), kind=kOutput, calls=%fused_computation.16 | convolution fusion | flops 224743424 | bytes 9502848 | tf_op jit(solution)/shard_map/transpose(jvp())/dot_general | solution.py:45
  191.0 2.5 fusion.7
  193.5 4.7 %convolution_convert_fusion = bf16[16,51,2048]{2,1,0:T(8,128)(2,1)} fusion(bf16[640,2048,1]{1,0,2:T(8,128)(2,1)S(1)} %fusion.7, s32[16,51]{1,0:T(8,128)S(1)} %concatenate.34), kind=kOutput, calls=%fused_computation.12 | convolution fusion | flops 2141288448 | bytes 5967040 | tf_op jit(solution)/shard_map/sop,sd->opd/dot_general | solution.py:200
  198.2 6.7 %all-to-all-start.2 = ((bf16[16,51,2048]{2,1,0:T(8,128)(2,1)}), bf16[16,51,2048]{2,1,0:T(8,128)(2,1)}, u32[]{:S(2)}, u32[]{:S(2)}) async-start(bf16[16,51,2048]{2,1,0:T(8,128)(2,1)} %convolution_convert_fusion), calls=%async_computation.2 | async-start | bytes 7340032 | tf_op jit(solution)/shard_map/all_to_all | solution.py:203
  205.6 48.1 %all-to-all-done.2 = bf16[16,51,2048]{2,1,0:T(8,128)(2,1)} async-done(((bf16[16,51,2048]{2,1,0:T(8,128)(2,1)}), bf16[16,51,2048]{2,1,0:T(8,128)(2,1)}, u32[]{:S(2)}, u32[]{:S(2)}) %all-to-all-start.2) | async-done | bytes 3342368 | tf_op jit(solution)/shard_map/all_to_all | solution.py:203
  253.7 6.7 %bitcast_convert_fusion = bf16[640,2048]{1,0:T(8,128)(2,1)} fusion(bf16[16,51,2048]{2,1,0:T(8,128)(2,1)} %all-to-all-done.2, pred[16,50,640]{2,1,0:T(8,128)(4,1)S(1)} %copy-done.12), kind=kOutput, calls=%fused_computation.4 | convolution fusion | flops 2140405760 | bytes 6475776 | tf_op jit(solution)/shard_map/opk,opd->kd/dot_general | solution.py:204
  (104 shorter events, 20.9 us)
Async XLA Ops:
  7.2 9.2 %copy-start = (bf16[640,2048]{1,0:T(8,128)(2,1)S(1)}, bf16[640,2048]{1,0:T(8,128)(2,1)}, u32[]{:S(2)}) copy-start(bf16[640,2048]{1,0:T(8,128)(2,1)} %param.17) | copy-start | bytes 7864324
  7.2 78.3 %all-gather.3.cloned.1.call-start = ((), (), s32[]{:S(2)}) async-start(), calls=%async_computation.3 | async-start | bytes 14155776 | tf_op jit(solution)/shard_map/all_gather | solution.py:114
  15.5 0.8 copy-start.11
  20.8 8.1 %copy-start.13 = (s32[1,640]{1,0:T(1,128)S(1)}, s32[1,640]{1,0:T(1,128)}, u32[]{:S(2)}) copy-start(s32[1,640]{1,0:T(1,128)} %param.19) | copy-start | bytes 7684
  20.8 8.1 %copy-start.14 = (f32[16]{0:T(128)S(1)}, f32[16]{0:T(128)}, u32[]{:S(2)}) copy-start(f32[16]{0:T(128)} %param.25) | copy-start | bytes 196
  20.8 8.3 %copy-start.15 = (s32[16]{0:T(128)S(1)}, s32[16]{0:T(128)}, u32[]{:S(2)}) copy-start(s32[16]{0:T(128)} %param.23) | copy-start | bytes 196
  20.8 8.3 %copy-start.16 = (s32[16]{0:T(128)S(1)}, s32[16]{0:T(128)}, u32[]{:S(2)}) copy-start(s32[16]{0:T(128)} %param.22) | copy-start | bytes 196
  20.8 57.8 %all-to-all-start = ((bf16[16,51,2048]{2,1,0:T(8,128)(2,1)}), bf16[16,51,2048]{2,1,0:T(8,128)(2,1)}, u32[]{:S(2)}, u32[]{:S(2)}) async-start(bf16[16,51,2048]{2,1,0:T(8,128)(2,1)} %add_convert_fusion), calls=%async_computation | async-start | bytes 7340032 | tf_op jit(solution)/shard_map/all_to_all | solution.py:100
  28.1 89.9 %all-gather.5.cloned.1.call-start = ((), (), s32[]{:S(2)}) async-start(), calls=%async_computation.4 | async-start | bytes 4718592 | tf_op jit(solution)/shard_map/all_gather | solution.py:115
  89.5 6.1 %copy-start.9 = (bf16[2048,1024]{1,0:T(8,128)(2,1)}, bf16[2048,1024]{1,0:T(8,128)(2,1)S(1)}, u32[]{:S(2)}) copy-start(bf16[2048,1024]{1,0:T(8,128)(2,1)S(1)} %get-tuple-element.57) | copy-start | bytes 12582916
  89.5 6.1 %copy-start.10 = (bf16[2048,1024]{1,0:T(8,128)(2,1)}, bf16[2048,1024]{1,0:T(8,128)(2,1)S(1)}, u32[]{:S(2)}) copy-start(bf16[2048,1024]{1,0:T(8,128)(2,1)S(1)} %get-tuple-element.58) | copy-start | bytes 12582916
  97.4 4.8 %copy-start.3 = (bf16[640,1024]{0,1:T(8,128)(2,1)S(1)}, bf16[640,1024]{0,1:T(8,128)(2,1)}, u32[]{:S(2)}) copy-start(bf16[640,1024]{0,1:T(8,128)(2,1)} %copy.28) | copy-start | bytes 3932164
  102.1 1.3 copy-start.7
  102.6 1.5 copy-start.5
  123.1 43.3 %all-to-all-start.1 = ((bf16[16,34,2048]{2,1,0:T(8,128)(2,1)}), bf16[16,34,2048]{2,1,0:T(8,128)(2,1)S(1)}, u32[]{:S(2)}, u32[]{:S(2)}) async-start(bf16[16,34,2048]{2,1,0:T(8,128)(2,1)} %broadcast_in_dim.99), calls=%async_computation.1 | async-start | bytes 5242880 | tf_op jit(solution)/shard_map/all_to_all | solution.py:147
  167.2 2.2 copy-start.2
  169.1 1.9 copy-start.6
  170.9 1.6 copy-start.8
  172.6 1.3 copy-start.4
  174.5 1.9 copy-start.17
  198.2 55.5 %copy-start.12 = (pred[16,50,640]{2,1,0:T(8,128)(4,1)S(1)}, pred[16,50,640]{2,1,0:T(8,128)(4,1)}, u32[]{:S(2)}) copy-start(pred[16,50,640]{2,1,0:T(8,128)(4,1)} %copy-done.11) | copy-start | bytes 1536004
  198.2 55.5 %all-to-all-start.2 = ((bf16[16,51,2048]{2,1,0:T(8,128)(2,1)}), bf16[16,51,2048]{2,1,0:T(8,128)(2,1)}, u32[]{:S(2)}, u32[]{:S(2)}) async-start(bf16[16,51,2048]{2,1,0:T(8,128)(2,1)} %convolution_convert_fusion), calls=%async_computation.2 | async-start | bytes 7340032 | tf_op jit(solution)/shard_map/all_to_all | solution.py:203
  253.7 6.7 %copy-start.1 = (bf16[640,2048]{1,0:T(8,128)(2,1)S(1)}, bf16[640,2048]{1,0:T(8,128)(2,1)}, u32[]{:S(2)}) copy-start(bf16[640,2048]{1,0:T(8,128)(2,1)} %param.17) | copy-start | bytes 7864324
Sparse Core Ops, SparseCore 0:
  9.7 69.9 all-gather.2
  81.4 36.5 all-gather.4

commit v9 on v8

--- a/solution.py
+++ b/solution.py
@@ -15,7 +15,7 @@
     return jnp.log(jnp.sum(jnp.exp(values), axis=axis))
 
 
-def attend(query_rows, slot_row_block, qkv_mat, kv_mat, out_mat, query_doc, doc_row):
+def attend(query_rows, slot_row_block, qkv_mat, kv_mat, out_mat_t, query_doc, doc_row):
     query_count = query_rows.shape[0]
     row_count = slot_row_block.shape[0]
     query_h = (
@@ -38,7 +38,9 @@
     attn_prob = (weights / jnp.sum(weights, axis=2, keepdims=True)).astype(jnp.bfloat16)
     mixed = jnp.einsum("hqk,khd->qhd", attn_prob, value_h, preferred_element_type=jnp.float32)
     mixed = mixed.astype(jnp.bfloat16).reshape(query_count, -1)
-    return jnp.dot(mixed, out_mat, preferred_element_type=jnp.float32)
+    return lax.dot_general(
+        mixed, out_mat_t, (((1,), (1,)), ((), ())), preferred_element_type=jnp.float32
+    )
 
 
 def select_rows(onehot, rows):
@@ -110,10 +112,10 @@
     slot_row_block = jnp.einsum(
         "sop,opd->sd", recv_onehot, recv_rows, preferred_element_type=jnp.float32
     ).astype(jnp.bfloat16)
-    qkv_full, out_full = (
-        lax.all_gather(qkv_weight, "fsdp", axis=1, tiled=True),
-        lax.all_gather(out_weight, "fsdp", axis=1, tiled=True),
-    )
+    weight_stack = jnp.concatenate([qkv_weight, out_weight.T[None]], axis=0)
+    weight_full = lax.all_gather(weight_stack, "fsdp", axis=1, tiled=True)
+    qkv_full = weight_full[:3]
+    out_full_t = weight_full[3]
     kv_full = jnp.concatenate([qkv_full[1], qkv_full[2]], axis=1)
     doc_row = doc_ids[0]
     pair_count = fig_slot.shape[0]
@@ -126,7 +128,7 @@
 
     def branch(inputs):
         picked = select_rows(query_onehot, inputs)
-        return attend(picked, inputs, qkv_full, kv_full, out_full, query_doc, doc_row)
+        return attend(picked, inputs, qkv_full, kv_full, out_full_t, query_doc, doc_row)
 
     attn_out, pullback = jax.vjp(branch, slot_row_block)
     query_rows = select_rows(query_onehot, slot_row_block)

time: 268 us -> 271 us (1.011)
    concatenate x0 -> x1, other arithmetic: none -> 2.91 us  [body(): weight_stack = jnp.concatenate([qkv_weight, out_weight.T[None]], axis=0)]
    all_gather x2 -> x1, waiting for transfers between devices: 13.7 us -> 12.3 us  [body(): weight_full = lax.all_gather(weight_stack, 'fsdp', axis=1, tiled=True)]
  transfers between devices with their start and end apart: 5 -> 4, of which waited for: 4 -> 4; matrix products, arithmetic and copies ran while one was open for 14% -> 7% of each run, Pallas kernels for 0% -> 0%
where the time goes in v9:
time: 271 us; the launch traced here: 270 us
  waiting for transfers between devices  146 us (54%)
  matrix products  63.2 us (23%)
  starting transfers between devices  20.7 us (8%)
  between operations  15.3 us (6%)
  local copies, waits for them, and re-layouts  14.5 us (5%)
  other arithmetic  10.2 us (4%)
    all_to_all x1, waiting for transfers between devices, body(): lax.all_to_all(send_rows, 'dp', split_axis=0, concat_axis=0, tiled=True)  49.8 us
    all_to_all x1, waiting for transfers between devices, body(): lax.all_to_all(back_rows, 'dp', split_axis=0, concat_axis=0, tiled=True)  48.1 us
    all_to_all x1, waiting for transfers between devices, body(): lax.all_to_all(jnp.broadcast_to(both_emb[None], (dp_count,) + both_emb.sh...  35.8 us
    dot_general x2, matrix products, attend(): jnp.dot(slot_row_block, kv_mat, preferred_element_type=jnp.float32)  15.6 us
    all_gather x1, waiting for transfers between devices, body(): weight_full = lax.all_gather(weight_stack, 'fsdp', axis=1, tiled=True)  12.3 us
    all_to_all x1, starting transfers between devices, body(): lax.all_to_all(send_rows, 'dp', split_axis=0, concat_axis=0, tiled=True)  7.32 us
    all_to_all x1, starting transfers between devices, body(): lax.all_to_all(jnp.broadcast_to(both_emb[None], (dp_count,) + both_emb.sh...  6.82 us
    dot_general x1, matrix products, body(): jnp.einsum('opk,opd->kd', send_onehot, home_rows, preferred_element_type=...  6.67 us
  transfers between devices with their start and end apart: 4, of which 4 were waited for; matrix products, arithmetic and copies ran while one was open for 7% of the time, Pallas kernels for 0%

profile of v9, /device:TPU:0, one launch (start us, length us, event | category | flops | bytes accessed | tf_op | source)
XLA Modules:
  0.0 270.0 jit_solution(5791980668014359407)
XLA Ops:
  8.6 2.9 %pad_maximum_fusion.7 = bf16[4,256,1024]{2,1,0:T(8,128)(2,1)} fusion(bf16[1,256,1024]{2,1,0:T(8,128)(2,1)S(1)} %copy.29, bf16[3,256,1024]{2,1,0:T(8,128)(2,1)} %param.20), kind=kLoop, calls=%fused_computation.31 | loop fusion | flops 1048576 | bytes 4194304 | tf_op jit(solution)/shard_map/concatenate | solution.py:115
  17.8 4.5 %add_convert_fusion = bf16[16,51,2048]{2,1,0:T(8,128)(2,1)} fusion(f32[16,1,2048]{2,1,0:T(1,128)S(1)} %scatter.15, bf16[640,2048]{1,0:T(8,128)(2,1)S(1)} %copy-done, pred[16,50,640]{2,1,0:T(8,128)(4,1)S(1)} %broadcast_compare_fusion), kind=kOutput, calls=%fused_computation.1 | convolution fusion | flops 2142437376 | bytes 6606848 | tf_op jit(solution)/shard_map/opk,kd->opd/dot_general | solution.py:99
  22.3 7.3 %all-to-all-start = ((bf16[16,51,2048]{2,1,0:T(8,128)(2,1)}), bf16[16,51,2048]{2,1,0:T(8,128)(2,1)}, u32[]{:S(2)}, u32[]{:S(2)}) async-start(bf16[16,51,2048]{2,1,0:T(8,128)(2,1)} %add_convert_fusion), calls=%async_computation | async-start | bytes 7340032 | tf_op jit(solution)/shard_map/all_to_all | solution.py:102
  30.3 49.8 %all-to-all-done = bf16[16,51,2048]{2,1,0:T(8,128)(2,1)} async-done(((bf16[16,51,2048]{2,1,0:T(8,128)(2,1)}), bf16[16,51,2048]{2,1,0:T(8,128)(2,1)}, u32[]{:S(2)}, u32[]{:S(2)}) %all-to-all-start) | async-done | bytes 3342368 | tf_op jit(solution)/shard_map/all_to_all | solution.py:102
  81.3 5.1 %bitcast_convert_fusion.1 = bf16[640,2048]{1,0:T(8,128)(2,1)S(1)} fusion(bf16[16,51,2048]{2,1,0:T(8,128)(2,1)} %all-to-all-done, s32[16,51]{1,0:T(8,128)S(1)} %concatenate.37), kind=kOutput, calls=%fused_computation.5 | convolution fusion | flops 2140928000 | bytes 5967040 | tf_op jit(solution)/shard_map/sop,opd->sd/dot_general | solution.py:112
  87.0 12.3 %all-gather.2.cloned.1.call-done = bf16[4,2048,1024]{2,1,0:T(8,128)(2,1)} async-done(((bf16[4,256,1024]{2,1,0:T(8,128)(2,1)}), bf16[4,2048,1024]{2,1,0:T(8,128)(2,1)}) %all-gather.2.cloned.1.call-update) | async-done | bytes 16777232 | tf_op jit(solution)/shard_map/all_gather | solution.py:116
  99.3 3.9 %slice_bitcast_fusion.3 = (bf16[2048,1024]{1,0:T(8,128)(2,1)S(1)}, bf16[2048,1024]{1,0:T(8,128)(2,1)S(1)}) fusion(bf16[4,2048,1024]{2,1,0:T(8,128)(2,1)} %all-gather.2.cloned.1.call-done), kind=kLoop, calls=%fused_computation.10 | loop fusion | bytes 16777216 | tf_op jit(solution)/shard_map/squeeze | solution.py:119
  103.3 6.1 %fusion.6 = bf16[640,2048]{1,0:T(8,128)(2,1)S(1)} fusion(bf16[640,2048]{1,0:T(8,128)(2,1)S(1)} %bitcast_convert_fusion.1, bf16[2048,1024]{1,0:T(8,128)(2,1)S(1)} %get-tuple-element.58, bf16[2048,1024]{1,0:T(8,128)(2,1)S(1)} %get-tuple-element.57), kind=kOutput, calls=%fused_computation.17 | convolution fusion | flops 5386797056 | bytes 13631488 | tf_op jit(solution)/shard_map/jvp()/dot_general | solution.py:26
  109.7 1.5 copy.31
  111.2 3.1 %fusion.32 = bf16[32,1024]{1,0:T(8,128)(2,1)S(1)} fusion(bf16[32,2048]{1,0:T(8,128)(2,1)S(1)} %convolution_convert_fusion.2, bf16[4,2048,1024]{2,1,0:T(8,128)(2,1)} %all-gather.2.cloned.1.call-done), kind=kOutput, calls=%fused_computation.61 | convolution fusion | flops 134250496 | bytes 4390912 | tf_op jit(solution)/shard_map/jvp()/dot_general | solution.py:22
  118.2 3.5 %fusion.14 = f32[32,2048]{1,0:T(8,128)S(1)} fusion(bf16[32,1024]{1,0:T(8,128)(2,1)S(1)} %reshape.307, bf16[4,2048,1024]{2,1,0:T(8,128)(2,1)} %all-gather.2.cloned.1.call-done, bf16[32,2048]{1,0:T(8,128)(2,1)S(1)} %copy-done.11), kind=kOutput, calls=%fused_computation.26 | convolution fusion | flops 134348800 | bytes 4653056 | tf_op jit(solution)/shard_map/jvp()/dot_general | solution.py:41
  122.0 1.8 broadcast_in_dim.103
  123.8 6.8 %all-to-all-start.1 = ((bf16[16,34,2048]{2,1,0:T(8,128)(2,1)}), bf16[16,34,2048]{2,1,0:T(8,128)(2,1)S(1)}, u32[]{:S(2)}, u32[]{:S(2)}) async-start(bf16[16,34,2048]{2,1,0:T(8,128)(2,1)} %broadcast_in_dim.103), calls=%async_computation.1 | async-start | bytes 5242880 | tf_op jit(solution)/shard_map/all_to_all | solution.py:149
  131.3 35.8 %all-to-all-done.1 = bf16[16,34,2048]{2,1,0:T(8,128)(2,1)S(1)} async-done(((bf16[16,34,2048]{2,1,0:T(8,128)(2,1)}), bf16[16,34,2048]{2,1,0:T(8,128)(2,1)S(1)}, u32[]{:S(2)}, u32[]{:S(2)}) %all-to-all-start.1) | async-done | bytes 2228256 | tf_op jit(solution)/shard_map/all_to_all | solution.py:149
  169.9 3.1 %fusion.31 = bf16[32,1024]{1,0:T(8,128)(2,1)S(1)} fusion(bf16[4,2048,1024]{2,1,0:T(8,128)(2,1)} %all-gather.2.cloned.1.call-done, f32[16,2048]{1,0:T(8,128)S(1)} %get-tuple-element.64, f32[16,2048]{1,0:T(8,128)S(1)} %get-tuple-element.63), kind=kOutput, calls=%fused_computation.60 | convolution fusion | flops 134479872 | bytes 4521984 | tf_op jit(solution)/shard_map/transpose(jvp())/dot_general | solution.py:41
  173.2 1.6 convolution_convert_fusion.4
  177.1 1.8 convolution_convert_fusion.3
  179.1 9.5 %fusion.7 = bf16[640,2048]{1,0:T(8,128)(2,1)} fusion(bf16[2048,1024]{1,0:T(8,128)(2,1)} %copy-done.9, bf16[2048,1024]{1,0:T(8,128)(2,1)} %copy-done.8, bf16[640,1024]{0,1:T(8,128)(2,1)} %bitcast.125, bf16[640,1024]{0,1:T(8,128)(2,1)S(1)} %bitcast.124), kind=kOutput, calls=%fused_computation.18 | convolution fusion | flops 5392039936 | bytes 13631488 | tf_op jit(solution)/shard_map/transpose(jvp())/dot_general | solution.py:26
  188.6 5.1 %fusion.8 = bf16[640,2048]{1,0:T(8,128)(2,1)S(1)} fusion(bf16[640,2048]{1,0:T(8,128)(2,1)} %fusion.7, bf16[32,1024]{1,0:T(8,128)(2,1)S(1)} %reshape.315, bf16[4,2048,1024]{2,1,0:T(8,128)(2,1)} %all-gather.2.cloned.1.call-done, s32[32]{0:T(128)S(1)} %pad_add_fusion), kind=kOutput, calls=%fused_computation.19 | convolution fusion | flops 224743424 | bytes 9502848 | tf_op jit(solution)/shard_map/transpose(jvp())/dot_general | solution.py:47
  193.7 2.5 fusion.9
  196.2 4.9 %convolution_convert_fusion = bf16[16,51,2048]{2,1,0:T(8,128)(2,1)} fusion(bf16[640,2048,1]{1,0,2:T(8,128)(2,1)S(1)} %fusion.9, s32[16,51]{1,0:T(8,128)S(1)} %concatenate.37), kind=kOutput, calls=%fused_computation.15 | convolution fusion | flops 2141288448 | bytes 5967040 | tf_op jit(solution)/shard_map/sop,sd->opd/dot_general | solution.py:202
  201.1 6.6 %all-to-all-start.2 = ((bf16[16,51,2048]{2,1,0:T(8,128)(2,1)}), bf16[16,51,2048]{2,1,0:T(8,128)(2,1)}, u32[]{:S(2)}, u32[]{:S(2)}) async-start(bf16[16,51,2048]{2,1,0:T(8,128)(2,1)} %convolution_convert_fusion), calls=%async_computation.2 | async-start | bytes 7340032 | tf_op jit(solution)/shard_map/all_to_all | solution.py:205
  208.4 48.1 %all-to-all-done.2 = bf16[16,51,2048]{2,1,0:T(8,128)(2,1)} async-done(((bf16[16,51,2048]{2,1,0:T(8,128)(2,1)}), bf16[16,51,2048]{2,1,0:T(8,128)(2,1)}, u32[]{:S(2)}, u32[]{:S(2)}) %all-to-all-start.2) | async-done | bytes 3342368 | tf_op jit(solution)/shard_map/all_to_all | solution.py:205
  256.5 6.7 %bitcast_convert_fusion = bf16[640,2048]{1,0:T(8,128)(2,1)} fusion(bf16[16,51,2048]{2,1,0:T(8,128)(2,1)} %all-to-all-done.2, pred[16,50,640]{2,1,0:T(8,128)(4,1)S(1)} %broadcast_compare_fusion), kind=kOutput, calls=%fused_computation.4 | convolution fusion | flops 2140405760 | bytes 6475776 | tf_op jit(solution)/shard_map/opk,opd->kd/dot_general | solution.py:206
  (115 shorter events, 20.3 us)
Async XLA Ops:
  7.2 10.6 %copy-start = (bf16[640,2048]{1,0:T(8,128)(2,1)S(1)}, bf16[640,2048]{1,0:T(8,128)(2,1)}, u32[]{:S(2)}) copy-start(bf16[640,2048]{1,0:T(8,128)(2,1)} %param.17) | copy-start | bytes 7864324
  7.2 92.2 %all-gather.2.cloned.1.call-start = ((), (), s32[]{:S(2)}) async-start(), calls=%async_computation.3 | async-start | bytes 18874368 | tf_op jit(solution)/shard_map/all_gather | solution.py:116
  8.6 3.0 %copy-start.18 = (s32[640]{0:T(1024)S(1)}, s32[640]{0:T(1024)}, u32[]{:S(2)}) copy-start(s32[640]{0:T(1024)} %param.18) | copy-start | bytes 7684
  22.3 7.3 %copy-start.19 = (s32[1,640]{1,0:T(1,128)S(1)}, s32[1,640]{1,0:T(1,128)}, u32[]{:S(2)}) copy-start(s32[1,640]{1,0:T(1,128)} %param.19) | copy-start | bytes 7684
  22.3 7.4 %copy-start.20 = (f32[16]{0:T(128)S(1)}, f32[16]{0:T(128)}, u32[]{:S(2)}) copy-start(f32[16]{0:T(128)} %param.25) | copy-start | bytes 196
  22.3 7.6 %copy-start.21 = (s32[16]{0:T(128)S(1)}, s32[16]{0:T(128)}, u32[]{:S(2)}) copy-start(s32[16]{0:T(128)} %param.23) | copy-start | bytes 196
  22.3 7.6 %copy-start.22 = (s32[16]{0:T(128)S(1)}, s32[16]{0:T(128)}, u32[]{:S(2)}) copy-start(s32[16]{0:T(128)} %param.22) | copy-start | bytes 196
  22.3 57.8 %all-to-all-start = ((bf16[16,51,2048]{2,1,0:T(8,128)(2,1)}), bf16[16,51,2048]{2,1,0:T(8,128)(2,1)}, u32[]{:S(2)}, u32[]{:S(2)}) async-start(bf16[16,51,2048]{2,1,0:T(8,128)(2,1)} %add_convert_fusion), calls=%async_computation | async-start | bytes 7340032 | tf_op jit(solution)/shard_map/all_to_all | solution.py:102
  87.0 24.2 %copy-start.10 = (bf16[32,2048]{1,0:T(8,128)(2,1)}, bf16[32,2048]{1,0:T(8,128)(2,1)S(1)}, u32[]{:S(2)}) copy-start(bf16[32,2048]{1,0:T(8,128)(2,1)S(1)} %convolution_convert_fusion.2) | copy-start | bytes 393220
  103.3 6.1 %copy-start.8 = (bf16[2048,1024]{1,0:T(8,128)(2,1)}, bf16[2048,1024]{1,0:T(8,128)(2,1)S(1)}, u32[]{:S(2)}) copy-start(bf16[2048,1024]{1,0:T(8,128)(2,1)S(1)} %get-tuple-element.57) | copy-start | bytes 12582916
  103.3 6.1 %copy-start.9 = (bf16[2048,1024]{1,0:T(8,128)(2,1)}, bf16[2048,1024]{1,0:T(8,128)(2,1)S(1)}, u32[]{:S(2)}) copy-start(bf16[2048,1024]{1,0:T(8,128)(2,1)S(1)} %get-tuple-element.58) | copy-start | bytes 12582916
  111.2 4.8 %copy-start.2 = (bf16[640,1024]{0,1:T(8,128)(2,1)S(1)}, bf16[640,1024]{0,1:T(8,128)(2,1)}, u32[]{:S(2)}) copy-start(bf16[640,1024]{0,1:T(8,128)(2,1)} %copy.31) | copy-start | bytes 3932164
  114.5 2.0 copy-start.12
  116.5 1.4 copy-start.4
  123.8 43.3 %all-to-all-start.1 = ((bf16[16,34,2048]{2,1,0:T(8,128)(2,1)}), bf16[16,34,2048]{2,1,0:T(8,128)(2,1)S(1)}, u32[]{:S(2)}, u32[]{:S(2)}) async-start(bf16[16,34,2048]{2,1,0:T(8,128)(2,1)} %broadcast_in_dim.103), calls=%async_computation.1 | async-start | bytes 5242880 | tf_op jit(solution)/shard_map/all_to_all | solution.py:149
  169.9 3.3 %copy-start.14 = (f32[16,2048]{1,0:T(8,128)}, f32[16,2048]{1,0:T(8,128)S(1)}, u32[]{:S(2)}) copy-start(f32[16,2048]{1,0:T(8,128)S(1)} %get-tuple-element.63) | copy-start | bytes 393220
  169.9 3.3 %copy-start.16 = (f32[16,2048]{1,0:T(8,128)}, f32[16,2048]{1,0:T(8,128)S(1)}, u32[]{:S(2)}) copy-start(f32[16,2048]{1,0:T(8,128)S(1)} %get-tuple-element.64) | copy-start | bytes 393220
  169.9 3.3 %copy-start.5 = (f32[16,32,640]{2,1,0:T(8,128)S(1)}, f32[16,32,640]{2,1,0:T(8,128)}, u32[]{:S(2)}) copy-start(f32[16,32,640]{2,1,0:T(8,128)} %copy-done.4) | copy-start | bytes 3932164
  173.2 1.7 copy-start.7
  177.1 2.0 copy-start.23
  188.6 5.1 %copy-start.15 = (f32[16,2048]{1,0:T(8,128)S(1)}, f32[16,2048]{1,0:T(8,128)}, u32[]{:S(2)}) copy-start(f32[16,2048]{1,0:T(8,128)} %copy-done.14) | copy-start | bytes 393220
  188.6 5.1 %copy-start.17 = (f32[16,2048]{1,0:T(8,128)S(1)}, f32[16,2048]{1,0:T(8,128)}, u32[]{:S(2)}) copy-start(f32[16,2048]{1,0:T(8,128)} %copy-done.16) | copy-start | bytes 393220
  201.1 55.4 %all-to-all-start.2 = ((bf16[16,51,2048]{2,1,0:T(8,128)(2,1)}), bf16[16,51,2048]{2,1,0:T(8,128)(2,1)}, u32[]{:S(2)}, u32[]{:S(2)}) async-start(bf16[16,51,2048]{2,1,0:T(8,128)(2,1)} %convolution_convert_fusion), calls=%async_computation.2 | async-start | bytes 7340032 | tf_op jit(solution)/shard_map/all_to_all | solution.py:205
  256.5 6.7 %copy-start.1 = (bf16[640,2048]{1,0:T(8,128)(2,1)S(1)}, bf16[640,2048]{1,0:T(8,128)(2,1)}, u32[]{:S(2)}) copy-start(bf16[640,2048]{1,0:T(8,128)(2,1)} %param.17) | copy-start | bytes 7864324
  (4 other events, 4.4 us)
Sparse Core Ops, SparseCore 0:
  11.7 87.5 all-gather.1

commit v10 on v8

--- a/solution.py
+++ b/solution.py
@@ -15,18 +15,11 @@
     return jnp.log(jnp.sum(jnp.exp(values), axis=axis))
 
 
-def attend(query_rows, slot_row_block, qkv_mat, kv_mat, out_mat, query_doc, doc_row):
-    query_count = query_rows.shape[0]
-    row_count = slot_row_block.shape[0]
-    query_h = (
-        jnp.dot(query_rows, qkv_mat[0], preferred_element_type=jnp.float32)
-        .astype(jnp.bfloat16)
-        .reshape(query_count, -1, HD)
-    )
-    key_value = jnp.dot(slot_row_block, kv_mat, preferred_element_type=jnp.float32).astype(
-        jnp.bfloat16
-    )
-    head_width = qkv_mat.shape[2]
+def attend(query_h, key_value, out_mat, query_doc, doc_row):
+    query_count = query_h.shape[0]
+    row_count = key_value.shape[0]
+    head_width = query_h.shape[1]
+    query_h = query_h.reshape(query_count, -1, HD)
     key_h = key_value[:, :head_width].reshape(row_count, -1, HD)
     value_h = key_value[:, head_width:].reshape(row_count, -1, HD)
     scores = jnp.einsum("qhd,khd->hqk", query_h, key_h, preferred_element_type=jnp.float32) * (
@@ -124,12 +117,18 @@
         axis=1,
     )
 
-    def branch(inputs):
-        picked = select_rows(query_onehot, inputs)
-        return attend(picked, inputs, qkv_full, kv_full, out_full, query_doc, doc_row)
-
-    attn_out, pullback = jax.vjp(branch, slot_row_block)
     query_rows = select_rows(query_onehot, slot_row_block)
+    query_h = jnp.dot(query_rows, qkv_full[0], preferred_element_type=jnp.float32).astype(
+        jnp.bfloat16
+    )
+    key_value = jnp.dot(slot_row_block, kv_full, preferred_element_type=jnp.float32).astype(
+        jnp.bfloat16
+    )
+
+    def branch(query_in, key_value_in):
+        return attend(query_in, key_value_in, out_full, query_doc, doc_row)
+
+    attn_out, pullback = jax.vjp(branch, query_h, key_value)
     query_output = query_rows.astype(jnp.float32) + attn_out
     fig_vec = query_output[:pair_count]
     cap_vec = query_output[pair_count:]
@@ -189,21 +188,40 @@
         cap_grad - cap_unit * jnp.sum(cap_unit * cap_grad, axis=1, keepdims=True)
     )
     query_ct = jnp.concatenate([figure_direction, caption_direction], axis=0)
-    slot_ct = lax.dot_general(
-        query_onehot.astype(jnp.float32),
-        query_ct,
-        (((0,), (0,)), ((), ())),
-        precision=lax.Precision.HIGHEST,
-    )
-    branch_ct = pullback(query_ct)[0]
-    slot_gradient = (slot_ct + branch_ct.astype(jnp.float32)).astype(jnp.bfloat16)
-    back_rows = jnp.einsum(
-        "sop,sd->opd", recv_onehot, slot_gradient, preferred_element_type=jnp.float32
-    ).astype(jnp.bfloat16)
-    home_rows = lax.all_to_all(back_rows, "dp", split_axis=0, concat_axis=0, tiled=True)
-    page_grad = jnp.einsum(
-        "opk,opd->kd", send_onehot, home_rows, preferred_element_type=jnp.float32
-    ).astype(jnp.bfloat16)
+    query_ct_rows, key_value_ct = pullback(query_ct)
+    half = feature_width // 2
+    grad_parts = []
+    for part in range(2):
+        cols = slice(part * half, (part + 1) * half)
+        query_part = lax.dot_general(
+            query_ct_rows,
+            qkv_full[0][cols],
+            (((1,), (1,)), ((), ())),
+            preferred_element_type=jnp.float32,
+        )
+        slot_part = lax.dot_general(
+            key_value_ct,
+            kv_full[cols],
+            (((1,), (1,)), ((), ())),
+            preferred_element_type=jnp.float32,
+        )
+        scatter_part = lax.dot_general(
+            query_onehot.astype(jnp.float32),
+            query_part + query_ct[:, cols],
+            (((0,), (0,)), ((), ())),
+            precision=lax.Precision.HIGHEST,
+        )
+        slot_gradient = (slot_part + scatter_part).astype(jnp.bfloat16)
+        back_rows = jnp.einsum(
+            "sop,sd->opd", recv_onehot, slot_gradient, preferred_element_type=jnp.float32
+        ).astype(jnp.bfloat16)
+        home_rows = lax.all_to_all(back_rows, "dp", split_axis=0, concat_axis=0, tiled=True)
+        grad_parts.append(
+            jnp.einsum(
+                "opk,opd->kd", send_onehot, home_rows, preferred_element_type=jnp.float32
+            ).astype(jnp.bfloat16)
+        )
+    page_grad = jnp.concatenate(grad_parts, axis=1)
     return (page_grad, pair_loss)
 
 

time: 268 us -> 266 us (level); the launches traced: 267 us -> 262 us
  waiting for transfers between devices: 148 us -> 131 us
  starting transfers between devices: 21.1 us -> 26 us
  matrix products: 60.5 us -> 64.6 us
    all_to_all x1 -> x2, waiting for transfers between devices: 48.1 us -> 31.8 us  [body(): lax.all_to_all(back_rows, 'dp', split_axis=0, concat_axis=0, tiled=True)]
    dot_general x4 -> x8, matrix products: 21.2 us -> 28.4 us  [the longest x2 11.9 us: body(): lax.dot_general(key_value_ct, kv_full[cols], (((1,), (1,)), ((), ())), pr...]
    dot_general x2 -> x1, matrix products: 5.65 us -> 0.59 us  [select_rows(): picked = jnp.dot(onehot, rows, preferred_element_type=jnp.float32)]
    all_to_all x1 -> x2, starting transfers between devices: 6.7 us -> 11.2 us  [body(): lax.all_to_all(back_rows, 'dp', split_axis=0, concat_axis=0, tiled=True)]
    dot_general x1 -> x2, matrix products: 4.65 us -> 5.83 us  [body(): jnp.einsum('sop,sd->opd', recv_onehot, slot_gradient, preferred_element_t...]
    dot_general x1 -> x2, matrix products: 6.66 us -> 7.48 us  [body(): jnp.einsum('opk,opd->kd', send_onehot, home_rows, preferred_element_type=...]
  transfers between devices with their start and end apart: 5 -> 6, of which waited for: 4 -> 5; matrix products, arithmetic and copies ran while one was open for 14% -> 21% of each run, Pallas kernels for 0% -> 0%
where the time goes in v10:
time: 266 us; the launch traced here: 262 us
  waiting for transfers between devices  131 us (49%)
  matrix products  64.6 us (24%)
  starting transfers between devices  26 us (10%)
  between operations  15.4 us (6%)
  local copies, waits for them, and re-layouts  13.8 us (5%)
  other arithmetic  10.5 us (4%)
    all_to_all x1, waiting for transfers between devices, body(): lax.all_to_all(send_rows, 'dp', split_axis=0, concat_axis=0, tiled=True)  49.1 us
    all_to_all x1, waiting for transfers between devices, body(): lax.all_to_all(jnp.broadcast_to(both_emb[None], (dp_count,) + both_emb.sh...  35.8 us
    all_to_all x2, waiting for transfers between devices, body(): lax.all_to_all(back_rows, 'dp', split_axis=0, concat_axis=0, tiled=True)  31.8 us
    all_gather x1, waiting for transfers between devices, body(): lax.all_gather(out_weight, 'fsdp', axis=1, tiled=True)  13.8 us
    dot_general x2, matrix products, body(): lax.dot_general(key_value_ct, kv_full[cols], (((1,), (1,)), ((), ())), pr...  11.9 us
    all_to_all x2, starting transfers between devices, body(): lax.all_to_all(back_rows, 'dp', split_axis=0, concat_axis=0, tiled=True)  11.2 us
    dot_general x2, matrix products, body(): jnp.einsum('opk,opd->kd', send_onehot, home_rows, preferred_element_type=...  7.48 us
    all_to_all x1, starting transfers between devices, body(): lax.all_to_all(send_rows, 'dp', split_axis=0, concat_axis=0, tiled=True)  7.31 us
  transfers between devices with their start and end apart: 6, of which 5 were waited for; matrix products, arithmetic and copies ran while one was open for 21% of the time, Pallas kernels for 0%

profile of v10, /device:TPU:0, one launch (start us, length us, event | category | flops | bytes accessed | tf_op | source)
XLA Modules:
  0.0 261.7 jit_solution(11759308287036405678)
XLA Ops:
  16.3 4.4 %add_convert_fusion = bf16[16,51,2048]{2,1,0:T(8,128)(2,1)} fusion(f32[16,1,2048]{2,1,0:T(1,128)S(1)} %scatter.15, bf16[640,2048]{1,0:T(8,128)(2,1)S(1)} %copy-done, pred[16,50,640]{2,1,0:T(8,128)(4,1)S(1)} %broadcast_compare_fusion), kind=kOutput, calls=%fused_computation.6 | convolution fusion | flops 2142437376 | bytes 6606848 | tf_op jit(solution)/shard_map/opk,kd->opd/dot_general | solution.py:90
  20.8 7.3 %all-to-all-start = ((bf16[16,51,2048]{2,1,0:T(8,128)(2,1)}), bf16[16,51,2048]{2,1,0:T(8,128)(2,1)}, u32[]{:S(2)}, u32[]{:S(2)}) async-start(bf16[16,51,2048]{2,1,0:T(8,128)(2,1)} %add_convert_fusion), calls=%async_computation | async-start | bytes 7340032 | tf_op jit(solution)/shard_map/all_to_all | solution.py:93
  29.5 49.1 %all-to-all-done = bf16[16,51,2048]{2,1,0:T(8,128)(2,1)} async-done(((bf16[16,51,2048]{2,1,0:T(8,128)(2,1)}), bf16[16,51,2048]{2,1,0:T(8,128)(2,1)}, u32[]{:S(2)}, u32[]{:S(2)}) %all-to-all-start) | async-done | bytes 3342368 | tf_op jit(solution)/shard_map/all_to_all | solution.py:93
  79.8 5.1 %bitcast_convert_fusion = bf16[640,2048]{1,0:T(8,128)(2,1)S(1)} fusion(bf16[16,51,2048]{2,1,0:T(8,128)(2,1)} %all-to-all-done, s32[16,51]{1,0:T(8,128)S(1)} %concatenate.37), kind=kOutput, calls=%fused_computation.7 | convolution fusion | flops 2140928000 | bytes 5967040 | tf_op jit(solution)/shard_map/sop,opd->sd/dot_general | solution.py:103
  85.5 3.9 %slice_bitcast_fusion.2 = (bf16[2048,1024]{1,0:T(8,128)(2,1)S(1)}, bf16[2048,1024]{1,0:T(8,128)(2,1)S(1)}) fusion(bf16[3,2048,1024]{2,1,0:T(8,128)(2,1)} %all-gather.3.cloned.1.call-done), kind=kLoop, calls=%fused_computation.14 | loop fusion | bytes 16777216 | tf_op jit(solution)/shard_map/squeeze | solution.py:110
  89.5 6.1 %fusion.8 = bf16[640,2048]{1,0:T(8,128)(2,1)S(1)} fusion(bf16[640,2048]{1,0:T(8,128)(2,1)S(1)} %bitcast_convert_fusion, bf16[2048,1024]{1,0:T(8,128)(2,1)S(1)} %get-tuple-element.57, bf16[2048,1024]{1,0:T(8,128)(2,1)S(1)} %get-tuple-element.58), kind=kOutput, calls=%fused_computation.16 | convolution fusion | flops 5386797056 | bytes 13631488 | tf_op jit(solution)/shard_map/dot_general | solution.py:124
  97.3 3.1 %fusion.37 = bf16[32,1024]{1,0:T(8,128)(2,1)S(1)} fusion(bf16[32,2048]{1,0:T(8,128)(2,1)S(1)} %convolution_convert_fusion, bf16[3,2048,1024]{2,1,0:T(8,128)(2,1)} %all-gather.3.cloned.1.call-done), kind=kOutput, calls=%fused_computation.71 | convolution fusion | flops 134250496 | bytes 4390912 | tf_op jit(solution)/shard_map/dot_general | solution.py:121
  104.2 13.8 %all-gather.5.cloned.1.call-done = bf16[1024,2048]{1,0:T(8,128)(2,1)} async-done(((bf16[1024,256]{1,0:T(8,128)(2,1)}), bf16[1024,2048]{1,0:T(8,128)(2,1)}) %all-gather.5.cloned.1.call-update) | async-done | bytes 4194320 | tf_op jit(solution)/shard_map/all_gather | solution.py:108
  118.0 3.0 %convolution_add_fusion = f32[32,2048]{1,0:T(8,128)S(1)} fusion(bf16[32,1024]{1,0:T(8,128)(2,1)S(1)} %reshape.309, bf16[1024,2048]{1,0:T(8,128)(2,1)} %all-gather.5.cloned.1.call-done, bf16[32,2048]{1,0:T(8,128)(2,1)S(1)} %convolution_convert_fusion), kind=kOutput, calls=%fused_computation.27 | convolution fusion | flops 134348800 | bytes 4653056 | tf_op jit(solution)/shard_map/jvp()/dot_general | solution.py:34
  121.3 1.8 broadcast_in_dim.99
  123.1 7.0 %all-to-all-start.1 = ((bf16[16,34,2048]{2,1,0:T(8,128)(2,1)}), bf16[16,34,2048]{2,1,0:T(8,128)(2,1)S(1)}, u32[]{:S(2)}, u32[]{:S(2)}) async-start(bf16[16,34,2048]{2,1,0:T(8,128)(2,1)} %broadcast_in_dim.99), calls=%async_computation.1 | async-start | bytes 5242880 | tf_op jit(solution)/shard_map/all_to_all | solution.py:146
  130.8 35.8 %all-to-all-done.1 = bf16[16,34,2048]{2,1,0:T(8,128)(2,1)S(1)} async-done(((bf16[16,34,2048]{2,1,0:T(8,128)(2,1)}), bf16[16,34,2048]{2,1,0:T(8,128)(2,1)S(1)}, u32[]{:S(2)}, u32[]{:S(2)}) %all-to-all-start.1) | async-done | bytes 2228256 | tf_op jit(solution)/shard_map/all_to_all | solution.py:146
  176.6 5.9 %fusion.2 = f32[640,1024]{1,0:T(8,128)S(1)} fusion(bf16[2048,1024]{1,0:T(8,128)(2,1)} %copy-done.10, bf16[2048,1024]{1,0:T(8,128)(2,1)} %copy-done.9, bf16[640,1024]{0,1:T(8,128)(2,1)} %bitcast.130, bf16[640,1024]{0,1:T(8,128)(2,1)} %bitcast.128), kind=kOutput, calls=%fused_computation.9 | convolution fusion | flops 2697986048 | bytes 13631488 | tf_op jit(solution)/shard_map/dot_general | solution.py:202
  182.5 2.3 fusion.35
  186.2 3.0 %fusion.15 = bf16[16,51,1024]{2,1,0:T(8,128)(2,1)} fusion(bf16[640,1024,1]{1,0,2:T(8,128)(2,1)S(1)} %fusion.19, s32[16,51]{1,0:T(8,128)S(1)} %concatenate.37), kind=kOutput, calls=%fused_computation.38 | convolution fusion | flops 1070905344 | bytes 2985152 | tf_op jit(solution)/shard_map/sop,sd->opd/dot_general | solution.py:215
  189.2 6.7 %all-to-all-start.2 = ((bf16[16,51,1024]{2,1,0:T(8,128)(2,1)}), bf16[16,51,1024]{2,1,0:T(8,128)(2,1)}, u32[]{:S(2)}, u32[]{:S(2)}) async-start(bf16[16,51,1024]{2,1,0:T(8,128)(2,1)} %fusion.15), calls=%async_computation.2 | async-start | bytes 3670016 | tf_op jit(solution)/shard_map/all_to_all | solution.py:218
  195.9 2.3 fusion.36
  198.2 6.0 %fusion.5 = f32[640,1024]{1,0:T(8,128)S(1)} fusion(bf16[2048,1024]{1,0:T(8,128)(2,1)} %copy-done.10, bf16[2048,1024]{1,0:T(8,128)(2,1)} %copy-done.9, bf16[640,1024]{0,1:T(8,128)(2,1)} %bitcast.131, bf16[640,1024]{0,1:T(8,128)(2,1)} %bitcast.129), kind=kOutput, calls=%fused_computation.11 | convolution fusion | flops 2697986048 | bytes 13631488 | tf_op jit(solution)/shard_map/dot_general | solution.py:202
  205.5 2.9 %fusion.16 = bf16[16,51,1024]{2,1,0:T(8,128)(2,1)} fusion(bf16[640,1024,1]{1,0,2:T(8,128)(2,1)S(1)} %fusion.20, s32[16,51]{1,0:T(8,128)S(1)} %concatenate.37), kind=kOutput, calls=%fused_computation.39 | convolution fusion | flops 1070905344 | bytes 2985152 | tf_op jit(solution)/shard_map/sop,sd->opd/dot_general | solution.py:215
  208.4 13.6 %all-to-all-done.2 = bf16[16,51,1024]{2,1,0:T(8,128)(2,1)} async-done(((bf16[16,51,1024]{2,1,0:T(8,128)(2,1)}), bf16[16,51,1024]{2,1,0:T(8,128)(2,1)}, u32[]{:S(2)}, u32[]{:S(2)}) %all-to-all-start.2) | async-done | bytes 1671200 | tf_op jit(solution)/shard_map/all_to_all | solution.py:218
  222.0 4.4 %all-to-all-start.3 = ((bf16[16,51,1024]{2,1,0:T(8,128)(2,1)}), bf16[16,51,1024]{2,1,0:T(8,128)(2,1)}, u32[]{:S(2)}, u32[]{:S(2)}) async-start(bf16[16,51,1024]{2,1,0:T(8,128)(2,1)} %fusion.16), calls=%async_computation.3 | async-start | bytes 3670016 | tf_op jit(solution)/shard_map/all_to_all | solution.py:218
  227.1 4.2 %bitcast_convert_fusion.2 = bf16[640,1024]{1,0:T(8,128)(2,1)} fusion(bf16[16,51,1024]{2,1,0:T(8,128)(2,1)} %all-to-all-done.2, pred[16,50,640]{2,1,0:T(8,128)(4,1)S(1)} %copy-done.13), kind=kOutput, calls=%fused_computation.19 | convolution fusion | flops 1070202880 | bytes 3493888 | tf_op jit(solution)/shard_map/opk,opd->kd/dot_general | solution.py:220
  231.3 18.3 %all-to-all-done.3 = bf16[16,51,1024]{2,1,0:T(8,128)(2,1)} async-done(((bf16[16,51,1024]{2,1,0:T(8,128)(2,1)}), bf16[16,51,1024]{2,1,0:T(8,128)(2,1)}, u32[]{:S(2)}, u32[]{:S(2)}) %all-to-all-start.3) | async-done | bytes 1671200 | tf_op jit(solution)/shard_map/all_to_all | solution.py:218
  249.6 3.3 %bitcast_convert_fusion.1 = bf16[640,1024]{1,0:T(8,128)(2,1)S(1)} fusion(bf16[16,51,1024]{2,1,0:T(8,128)(2,1)} %all-to-all-done.3, pred[16,50,640]{2,1,0:T(8,128)(4,1)S(1)} %copy-done.13), kind=kOutput, calls=%fused_computation.18 | convolution fusion | flops 1070202880 | bytes 3493888 | tf_op jit(solution)/shard_map/opk,opd->kd/dot_general | solution.py:220
  (112 shorter events, 33.0 us)
Async XLA Ops:
  7.2 9.2 %copy-start = (bf16[640,2048]{1,0:T(8,128)(2,1)S(1)}, bf16[640,2048]{1,0:T(8,128)(2,1)}, u32[]{:S(2)}) copy-start(bf16[640,2048]{1,0:T(8,128)(2,1)} %param.17) | copy-start | bytes 7864324
  7.2 78.3 %all-gather.3.cloned.1.call-start = ((), (), s32[]{:S(2)}) async-start(), calls=%async_computation.4 | async-start | bytes 14155776 | tf_op jit(solution)/shard_map/all_gather | solution.py:107
  15.5 0.8 copy-start.12
  20.8 8.1 %copy-start.14 = (s32[1,640]{1,0:T(1,128)S(1)}, s32[1,640]{1,0:T(1,128)}, u32[]{:S(2)}) copy-start(s32[1,640]{1,0:T(1,128)} %param.19) | copy-start | bytes 7684
  20.8 8.1 %copy-start.15 = (f32[16]{0:T(128)S(1)}, f32[16]{0:T(128)}, u32[]{:S(2)}) copy-start(f32[16]{0:T(128)} %param.25) | copy-start | bytes 196
  20.8 8.3 %copy-start.16 = (s32[16]{0:T(128)S(1)}, s32[16]{0:T(128)}, u32[]{:S(2)}) copy-start(s32[16]{0:T(128)} %param.23) | copy-start | bytes 196
  20.8 8.3 %copy-start.17 = (s32[16]{0:T(128)S(1)}, s32[16]{0:T(128)}, u32[]{:S(2)}) copy-start(s32[16]{0:T(128)} %param.22) | copy-start | bytes 196
  20.8 57.8 %all-to-all-start = ((bf16[16,51,2048]{2,1,0:T(8,128)(2,1)}), bf16[16,51,2048]{2,1,0:T(8,128)(2,1)}, u32[]{:S(2)}, u32[]{:S(2)}) async-start(bf16[16,51,2048]{2,1,0:T(8,128)(2,1)} %add_convert_fusion), calls=%async_computation | async-start | bytes 7340032 | tf_op jit(solution)/shard_map/all_to_all | solution.py:93
  28.1 89.9 %all-gather.5.cloned.1.call-start = ((), (), s32[]{:S(2)}) async-start(), calls=%async_computation.5 | async-start | bytes 4718592 | tf_op jit(solution)/shard_map/all_gather | solution.py:108
  89.4 6.1 %copy-start.9 = (bf16[2048,1024]{1,0:T(8,128)(2,1)}, bf16[2048,1024]{1,0:T(8,128)(2,1)S(1)}, u32[]{:S(2)}) copy-start(bf16[2048,1024]{1,0:T(8,128)(2,1)S(1)} %get-tuple-element.57) | copy-start | bytes 12582916
  89.4 6.1 %copy-start.10 = (bf16[2048,1024]{1,0:T(8,128)(2,1)}, bf16[2048,1024]{1,0:T(8,128)(2,1)S(1)}, u32[]{:S(2)}) copy-start(bf16[2048,1024]{1,0:T(8,128)(2,1)S(1)} %get-tuple-element.58) | copy-start | bytes 12582916
  97.3 4.7 %copy-start.3 = (bf16[640,1024]{0,1:T(8,128)(2,1)S(1)}, bf16[640,1024]{0,1:T(8,128)(2,1)}, u32[]{:S(2)}) copy-start(bf16[640,1024]{0,1:T(8,128)(2,1)} %copy.28) | copy-start | bytes 3932164
  102.0 1.3 copy-start.7
  102.5 1.5 copy-start.5
  123.1 43.5 %all-to-all-start.1 = ((bf16[16,34,2048]{2,1,0:T(8,128)(2,1)}), bf16[16,34,2048]{2,1,0:T(8,128)(2,1)S(1)}, u32[]{:S(2)}, u32[]{:S(2)}) async-start(bf16[16,34,2048]{2,1,0:T(8,128)(2,1)} %broadcast_in_dim.99), calls=%async_computation.1 | async-start | bytes 5242880 | tf_op jit(solution)/shard_map/all_to_all | solution.py:146
  167.4 2.2 copy-start.2
  169.2 1.9 copy-start.6
  171.1 1.7 copy-start.8
  172.7 1.3 copy-start.4
  189.2 32.8 %all-to-all-start.2 = ((bf16[16,51,1024]{2,1,0:T(8,128)(2,1)}), bf16[16,51,1024]{2,1,0:T(8,128)(2,1)}, u32[]{:S(2)}, u32[]{:S(2)}) async-start(bf16[16,51,1024]{2,1,0:T(8,128)(2,1)} %fusion.15), calls=%async_computation.2 | async-start | bytes 3670016 | tf_op jit(solution)/shard_map/all_to_all | solution.py:218
  208.4 18.7 %copy-start.13 = (pred[16,50,640]{2,1,0:T(8,128)(4,1)S(1)}, pred[16,50,640]{2,1,0:T(8,128)(4,1)}, u32[]{:S(2)}) copy-start(pred[16,50,640]{2,1,0:T(8,128)(4,1)} %copy-done.12) | copy-start | bytes 1536004
  222.0 27.6 %all-to-all-start.3 = ((bf16[16,51,1024]{2,1,0:T(8,128)(2,1)}), bf16[16,51,1024]{2,1,0:T(8,128)(2,1)}, u32[]{:S(2)}, u32[]{:S(2)}) async-start(bf16[16,51,1024]{2,1,0:T(8,128)(2,1)} %fusion.16), calls=%async_computation.3 | async-start | bytes 3670016 | tf_op jit(solution)/shard_map/all_to_all | solution.py:218
  249.6 3.3 %copy-start.11 = (bf16[640,1024]{1,0:T(8,128)(2,1)S(1)}, bf16[640,1024]{1,0:T(8,128)(2,1)}, u32[]{:S(2)}) copy-start(bf16[640,1024]{1,0:T(8,128)(2,1)} %bitcast_convert_fusion.2) | copy-start | bytes 3932164
  249.6 5.0 %copy-start.1 = (bf16[640,2048]{1,0:T(8,128)(2,1)S(1)}, bf16[640,2048]{1,0:T(8,128)(2,1)}, u32[]{:S(2)}) copy-start(bf16[640,2048]{1,0:T(8,128)(2,1)} %param.17) | copy-start | bytes 7864324
Sparse Core Ops, SparseCore 0:
  9.7 69.9 all-gather.2
  81.4 36.5 all-gather.4

commit v11 on v10

--- a/solution.py
+++ b/solution.py
@@ -189,10 +189,9 @@
     )
     query_ct = jnp.concatenate([figure_direction, caption_direction], axis=0)
     query_ct_rows, key_value_ct = pullback(query_ct)
-    half = feature_width // 2
+    first_width = feature_width // 4
     grad_parts = []
-    for part in range(2):
-        cols = slice(part * half, (part + 1) * half)
+    for cols in (slice(0, first_width), slice(first_width, feature_width)):
         query_part = lax.dot_general(
             query_ct_rows,
             qkv_full[0][cols],

time: 266 us -> 269 us (1.011)
  waiting for transfers between devices: 131 us -> 136 us
  matrix products: 64.6 us -> 59.7 us
  local copies, waits for them, and re-layouts: 13.8 us -> 17.2 us
    all_to_all x2, waiting for transfers between devices: 31.8 us -> 36.4 us  [body(): lax.all_to_all(back_rows, 'dp', split_axis=0, concat_axis=0, tiled=True)]
    dot_general x2, matrix products: 11.9 us -> 7.71 us  [body(): lax.dot_general(key_value_ct, kv_full[cols], (((1,), (1,)), ((), ())), pr...]
    unnamed x37 -> x39, local copies, waits for them, and re-layouts: 2.85 us -> 5.94 us
  transfers between devices with their start and end apart: 6 -> 6, of which waited for: 5 -> 5; matrix products, arithmetic and copies ran while one was open for 21% -> 19% of each run, Pallas kernels for 0% -> 0%
where the time goes in v11:
time: 269 us; the launch traced here: 264 us
  waiting for transfers between devices  136 us (51%)
  matrix products  59.7 us (22%)
  starting transfers between devices  25.9 us (10%)
  local copies, waits for them, and re-layouts  17.2 us (6%)
  between operations  15.4 us (6%)
  other arithmetic  10.7 us (4%)
    all_to_all x1, waiting for transfers between devices, body(): lax.all_to_all(send_rows, 'dp', split_axis=0, concat_axis=0, tiled=True)  48.8 us
    all_to_all x2, waiting for transfers between devices, body(): lax.all_to_all(back_rows, 'dp', split_axis=0, concat_axis=0, tiled=True)  36.4 us
    all_to_all x1, waiting for transfers between devices, body(): lax.all_to_all(jnp.broadcast_to(both_emb[None], (dp_count,) + both_emb.sh...  35.7 us
    all_gather x1, waiting for transfers between devices, body(): lax.all_gather(out_weight, 'fsdp', axis=1, tiled=True)  13.9 us
    all_to_all x2, starting transfers between devices, body(): lax.all_to_all(back_rows, 'dp', split_axis=0, concat_axis=0, tiled=True)  11 us
    dot_general x2, matrix products, body(): lax.dot_general(key_value_ct, kv_full[cols], (((1,), (1,)), ((), ())), pr...  7.71 us
    all_to_all x1, starting transfers between devices, body(): lax.all_to_all(send_rows, 'dp', split_axis=0, concat_axis=0, tiled=True)  7.3 us
    all_to_all x1, starting transfers between devices, body(): lax.all_to_all(jnp.broadcast_to(both_emb[None], (dp_count,) + both_emb.sh...  6.98 us
  transfers between devices with their start and end apart: 6, of which 5 were waited for; matrix products, arithmetic and copies ran while one was open for 19% of the time, Pallas kernels for 0%

profile of v11, /device:TPU:0, one launch (start us, length us, event | category | flops | bytes accessed | tf_op | source)
XLA Modules:
  0.0 264.5 jit_solution(16748678377947679276)
XLA Ops:
  16.3 4.4 %add_convert_fusion = bf16[16,51,2048]{2,1,0:T(8,128)(2,1)} fusion(f32[16,1,2048]{2,1,0:T(1,128)S(1)} %scatter.15, bf16[640,2048]{1,0:T(8,128)(2,1)S(1)} %copy-done, pred[16,50,640]{2,1,0:T(8,128)(4,1)S(1)} %broadcast_compare_fusion), kind=kOutput, calls=%fused_computation.4 | convolution fusion | flops 2142437376 | bytes 6606848 | tf_op jit(solution)/shard_map/opk,kd->opd/dot_general | solution.py:90
  20.8 7.3 %all-to-all-start = ((bf16[16,51,2048]{2,1,0:T(8,128)(2,1)}), bf16[16,51,2048]{2,1,0:T(8,128)(2,1)}, u32[]{:S(2)}, u32[]{:S(2)}) async-start(bf16[16,51,2048]{2,1,0:T(8,128)(2,1)} %add_convert_fusion), calls=%async_computation | async-start | bytes 7340032 | tf_op jit(solution)/shard_map/all_to_all | solution.py:93
  29.5 48.8 %all-to-all-done = bf16[16,51,2048]{2,1,0:T(8,128)(2,1)} async-done(((bf16[16,51,2048]{2,1,0:T(8,128)(2,1)}), bf16[16,51,2048]{2,1,0:T(8,128)(2,1)}, u32[]{:S(2)}, u32[]{:S(2)}) %all-to-all-start) | async-done | bytes 3342368 | tf_op jit(solution)/shard_map/all_to_all | solution.py:93
  79.6 5.1 %bitcast_convert_fusion = bf16[640,2048]{1,0:T(8,128)(2,1)S(1)} fusion(bf16[16,51,2048]{2,1,0:T(8,128)(2,1)} %all-to-all-done, s32[16,51]{1,0:T(8,128)S(1)} %concatenate.37), kind=kOutput, calls=%fused_computation.9 | convolution fusion | flops 2140928000 | bytes 5967040 | tf_op jit(solution)/shard_map/sop,opd->sd/dot_general | solution.py:103
  85.3 3.9 %slice_bitcast_fusion.3 = (bf16[2048,1024]{1,0:T(8,128)(2,1)S(1)}, bf16[2048,1024]{1,0:T(8,128)(2,1)S(1)}) fusion(bf16[3,2048,1024]{2,1,0:T(8,128)(2,1)} %all-gather.3.cloned.1.call-done), kind=kLoop, calls=%fused_computation.13 | loop fusion | bytes 16777216 | tf_op jit(solution)/shard_map/squeeze | solution.py:110
  89.3 6.1 %fusion.9 = bf16[640,2048]{1,0:T(8,128)(2,1)S(1)} fusion(bf16[640,2048]{1,0:T(8,128)(2,1)S(1)} %bitcast_convert_fusion, bf16[2048,1024]{1,0:T(8,128)(2,1)S(1)} %get-tuple-element.58, bf16[2048,1024]{1,0:T(8,128)(2,1)S(1)} %get-tuple-element.57), kind=kOutput, calls=%fused_computation.17 | convolution fusion | flops 5386797056 | bytes 13631488 | tf_op jit(solution)/shard_map/dot_general | solution.py:124
  97.2 3.1 %fusion.42 = bf16[32,1024]{1,0:T(8,128)(2,1)S(1)} fusion(bf16[32,2048]{1,0:T(8,128)(2,1)S(1)} %convolution_convert_fusion.1, bf16[3,2048,1024]{2,1,0:T(8,128)(2,1)} %all-gather.3.cloned.1.call-done), kind=kOutput, calls=%fused_computation.71 | convolution fusion | flops 134250496 | bytes 4390912 | tf_op jit(solution)/shard_map/dot_general | solution.py:121
  104.1 13.9 %all-gather.5.cloned.1.call-done = bf16[1024,2048]{1,0:T(8,128)(2,1)} async-done(((bf16[1024,256]{1,0:T(8,128)(2,1)}), bf16[1024,2048]{1,0:T(8,128)(2,1)}) %all-gather.5.cloned.1.call-update) | async-done | bytes 4194320 | tf_op jit(solution)/shard_map/all_gather | solution.py:108
  118.0 3.0 %convolution_add_fusion = f32[32,2048]{1,0:T(8,128)S(1)} fusion(bf16[32,1024]{1,0:T(8,128)(2,1)S(1)} %reshape.309, bf16[1024,2048]{1,0:T(8,128)(2,1)} %all-gather.5.cloned.1.call-done, bf16[32,2048]{1,0:T(8,128)(2,1)S(1)} %convolution_convert_fusion.1), kind=kOutput, calls=%fused_computation.27 | convolution fusion | flops 134348800 | bytes 4653056 | tf_op jit(solution)/shard_map/jvp()/dot_general | solution.py:34
  121.3 1.8 broadcast_in_dim.99
  123.1 7.0 %all-to-all-start.1 = ((bf16[16,34,2048]{2,1,0:T(8,128)(2,1)}), bf16[16,34,2048]{2,1,0:T(8,128)(2,1)S(1)}, u32[]{:S(2)}, u32[]{:S(2)}) async-start(bf16[16,34,2048]{2,1,0:T(8,128)(2,1)} %broadcast_in_dim.99), calls=%async_computation.1 | async-start | bytes 5242880 | tf_op jit(solution)/shard_map/all_to_all | solution.py:146
  130.8 35.7 %all-to-all-done.1 = bf16[16,34,2048]{2,1,0:T(8,128)(2,1)S(1)} async-done(((bf16[16,34,2048]{2,1,0:T(8,128)(2,1)}), bf16[16,34,2048]{2,1,0:T(8,128)(2,1)S(1)}, u32[]{:S(2)}, u32[]{:S(2)}) %all-to-all-start.1) | async-done | bytes 2228256 | tf_op jit(solution)/shard_map/all_to_all | solution.py:146
  178.8 6.1 %fusion.4 = f32[640,1536]{1,0:T(8,128)} fusion(bf16[2048,1024]{1,0:T(8,128)(2,1)S(1)} %copy-done.6, bf16[2048,1024]{1,0:T(8,128)(2,1)S(1)} %copy-done.4, bf16[640,1024]{0,1:T(8,128)(2,1)S(1)} %bitcast.128, bf16[640,1024]{0,1:T(8,128)(2,1)S(1)} %bitcast.126), kind=kOutput, calls=%fused_computation.5 | convolution fusion | flops 4044357632 | bytes 14942208 | tf_op jit(solution)/shard_map/dot_general | solution.py:201
  187.6 2.1 fusion.22
  189.7 6.6 %all-to-all-start.2 = ((bf16[16,51,512]{2,1,0:T(8,128)(2,1)}), bf16[16,51,512]{2,1,0:T(8,128)(2,1)}, u32[]{:S(2)}, u32[]{:S(2)}) async-start(bf16[16,51,512]{2,1,0:T(8,128)(2,1)} %fusion.22), calls=%async_computation.2 | async-start | bytes 1835008 | tf_op jit(solution)/shard_map/all_to_all | solution.py:217
  196.3 2.9 %fusion.16 = f32[32,1536]{1,0:T(8,128)S(1)} fusion(bf16[32,1024]{1,0:T(8,128)(2,1)S(1)} %reshape.317, bf16[3,2048,1024]{2,1,0:T(8,128)(2,1)} %all-gather.3.cloned.1.call-done, f32[16,2048]{1,0:T(8,128)S(1)} %get-tuple-element.64, f32[16,2048]{1,0:T(8,128)S(1)} %get-tuple-element.63), kind=kOutput, calls=%fused_computation.26 | convolution fusion | flops 100761600 | bytes 3670016 | tf_op jit(solution)/shard_map/dot_general | solution.py:195
  199.2 4.0 %fusion.13 = bf16[640,1536,1]{1,0,2:T(8,128)(2,1)S(1)} fusion(f32[640,1536]{1,0:T(8,128)} %fusion.4, f32[32,1536]{1,0:T(8,128)S(1)} %fusion.16, s32[32]{0:T(128)S(1)} %pad_add_fusion.3), kind=kOutput, calls=%fused_computation.20 | convolution fusion | flops 379473920 | bytes 6094976 | tf_op jit(solution)/shard_map/dot_general | solution.py:207
  203.2 3.9 %convolution_convert_fusion = bf16[16,51,1536]{2,1,0:T(8,128)(2,1)} fusion(bf16[640,1536,1]{1,0,2:T(8,128)(2,1)S(1)} %fusion.13, s32[16,51]{1,0:T(8,128)S(1)} %concatenate.37), kind=kOutput, calls=%fused_computation.16 | convolution fusion | flops 1606096896 | bytes 4476096 | tf_op jit(solution)/shard_map/sop,sd->opd/dot_general | solution.py:214
  207.1 4.2 %all-to-all-done.2 = bf16[16,51,512]{2,1,0:T(8,128)(2,1)} async-done(((bf16[16,51,512]{2,1,0:T(8,128)(2,1)}), bf16[16,51,512]{2,1,0:T(8,128)(2,1)}, u32[]{:S(2)}, u32[]{:S(2)}) %all-to-all-start.2) | async-done | bytes 835616 | tf_op jit(solution)/shard_map/all_to_all | solution.py:217
  211.3 4.5 %all-to-all-start.3 = ((bf16[16,51,1536]{2,1,0:T(8,128)(2,1)}), bf16[16,51,1536]{2,1,0:T(8,128)(2,1)}, u32[]{:S(2)}, u32[]{:S(2)}) async-start(bf16[16,51,1536]{2,1,0:T(8,128)(2,1)} %convolution_convert_fusion), calls=%async_computation.3 | async-start | bytes 5505024 | tf_op jit(solution)/shard_map/all_to_all | solution.py:217
  216.5 2.2 fusion.25
  218.9 32.2 %all-to-all-done.3 = bf16[16,51,1536]{2,1,0:T(8,128)(2,1)} async-done(((bf16[16,51,1536]{2,1,0:T(8,128)(2,1)}), bf16[16,51,1536]{2,1,0:T(8,128)(2,1)}, u32[]{:S(2)}, u32[]{:S(2)}) %all-to-all-start.3) | async-done | bytes 2506784 | tf_op jit(solution)/shard_map/all_to_all | solution.py:217
  251.1 4.4 %bitcast_convert_fusion.1 = bf16[640,1536]{1,0:T(8,128)(2,1)S(1)} fusion(bf16[16,51,1536]{2,1,0:T(8,128)(2,1)} %all-to-all-done.3, pred[16,50,640]{2,1,0:T(8,128)(4,1)} %copy-done.13), kind=kOutput, calls=%fused_computation.14 | convolution fusion | flops 1605304320 | bytes 4984832 | tf_op jit(solution)/shard_map/opk,opd->kd/dot_general | solution.py:219
  255.5 1.9 pad_maximum_fusion
  (115 shorter events, 33.9 us)
Async XLA Ops:
  7.2 9.2 %copy-start = (bf16[640,2048]{1,0:T(8,128)(2,1)S(1)}, bf16[640,2048]{1,0:T(8,128)(2,1)}, u32[]{:S(2)}) copy-start(bf16[640,2048]{1,0:T(8,128)(2,1)} %param.17) | copy-start | bytes 7864324
  7.2 78.1 %all-gather.3.cloned.1.call-start = ((), (), s32[]{:S(2)}) async-start(), calls=%async_computation.4 | async-start | bytes 14155776 | tf_op jit(solution)/shard_map/all_gather | solution.py:107
  20.8 8.1 %copy-start.15 = (s32[1,640]{1,0:T(1,128)S(1)}, s32[1,640]{1,0:T(1,128)}, u32[]{:S(2)}) copy-start(s32[1,640]{1,0:T(1,128)} %param.19) | copy-start | bytes 7684
  20.8 8.1 %copy-start.16 = (f32[16]{0:T(128)S(1)}, f32[16]{0:T(128)}, u32[]{:S(2)}) copy-start(f32[16]{0:T(128)} %param.25) | copy-start | bytes 196
  20.8 8.3 %copy-start.17 = (s32[16]{0:T(128)S(1)}, s32[16]{0:T(128)}, u32[]{:S(2)}) copy-start(s32[16]{0:T(128)} %param.23) | copy-start | bytes 196
  20.8 8.3 %copy-start.18 = (s32[16]{0:T(128)S(1)}, s32[16]{0:T(128)}, u32[]{:S(2)}) copy-start(s32[16]{0:T(128)} %param.22) | copy-start | bytes 196
  20.8 57.5 %all-to-all-start = ((bf16[16,51,2048]{2,1,0:T(8,128)(2,1)}), bf16[16,51,2048]{2,1,0:T(8,128)(2,1)}, u32[]{:S(2)}, u32[]{:S(2)}) async-start(bf16[16,51,2048]{2,1,0:T(8,128)(2,1)} %add_convert_fusion), calls=%async_computation | async-start | bytes 7340032 | tf_op jit(solution)/shard_map/all_to_all | solution.py:93
  28.1 89.9 %all-gather.5.cloned.1.call-start = ((), (), s32[]{:S(2)}) async-start(), calls=%async_computation.5 | async-start | bytes 4718592 | tf_op jit(solution)/shard_map/all_gather | solution.py:108
  89.3 6.1 %copy-start.3 = (bf16[2048,1024]{1,0:T(8,128)(2,1)}, bf16[2048,1024]{1,0:T(8,128)(2,1)S(1)}, u32[]{:S(2)}) copy-start(bf16[2048,1024]{1,0:T(8,128)(2,1)S(1)} %get-tuple-element.57) | copy-start | bytes 12582916
  89.3 6.1 %copy-start.5 = (bf16[2048,1024]{1,0:T(8,128)(2,1)}, bf16[2048,1024]{1,0:T(8,128)(2,1)S(1)}, u32[]{:S(2)}) copy-start(bf16[2048,1024]{1,0:T(8,128)(2,1)S(1)} %get-tuple-element.58) | copy-start | bytes 12582916
  97.2 4.8 %copy-start.7 = (bf16[640,1024]{0,1:T(8,128)(2,1)S(1)}, bf16[640,1024]{0,1:T(8,128)(2,1)}, u32[]{:S(2)}) copy-start(bf16[640,1024]{0,1:T(8,128)(2,1)} %copy.30) | copy-start | bytes 3932164
  101.9 1.3 copy-start.11
  102.4 1.5 copy-start.9
  123.1 43.3 %all-to-all-start.1 = ((bf16[16,34,2048]{2,1,0:T(8,128)(2,1)}), bf16[16,34,2048]{2,1,0:T(8,128)(2,1)S(1)}, u32[]{:S(2)}, u32[]{:S(2)}) async-start(bf16[16,34,2048]{2,1,0:T(8,128)(2,1)} %broadcast_in_dim.99), calls=%async_computation.1 | async-start | bytes 5242880 | tf_op jit(solution)/shard_map/all_to_all | solution.py:146
  167.2 2.2 copy-start.2
  169.1 1.9 copy-start.10
  170.9 1.3 copy-start.12
  172.3 1.3 copy-start.8
  173.6 2.2 copy-start.6
  174.2 3.0 %copy-start.4 = (bf16[2048,1024]{1,0:T(8,128)(2,1)S(1)}, bf16[2048,1024]{1,0:T(8,128)(2,1)}, u32[]{:S(2)}) copy-start(bf16[2048,1024]{1,0:T(8,128)(2,1)} %copy-done.3) | copy-start | bytes 12582916
  189.7 21.6 %all-to-all-start.2 = ((bf16[16,51,512]{2,1,0:T(8,128)(2,1)}), bf16[16,51,512]{2,1,0:T(8,128)(2,1)}, u32[]{:S(2)}, u32[]{:S(2)}) async-start(bf16[16,51,512]{2,1,0:T(8,128)(2,1)} %fusion.22), calls=%async_computation.2 | async-start | bytes 1835008 | tf_op jit(solution)/shard_map/all_to_all | solution.py:217
  207.1 9.4 %copy-start.14 = (pred[16,50,640]{2,1,0:T(8,128)(4,1)S(1)}, pred[16,50,640]{2,1,0:T(8,128)(4,1)}, u32[]{:S(2)}) copy-start(pred[16,50,640]{2,1,0:T(8,128)(4,1)} %copy-done.13) | copy-start | bytes 1536004
  211.3 39.8 %all-to-all-start.3 = ((bf16[16,51,1536]{2,1,0:T(8,128)(2,1)}), bf16[16,51,1536]{2,1,0:T(8,128)(2,1)}, u32[]{:S(2)}, u32[]{:S(2)}) async-start(bf16[16,51,1536]{2,1,0:T(8,128)(2,1)} %convolution_convert_fusion), calls=%async_computation.3 | async-start | bytes 5505024 | tf_op jit(solution)/shard_map/all_to_all | solution.py:217
  251.1 6.3 %copy-start.1 = (bf16[640,2048]{1,0:T(8,128)(2,1)S(1)}, bf16[640,2048]{1,0:T(8,128)(2,1)}, u32[]{:S(2)}) copy-start(bf16[640,2048]{1,0:T(8,128)(2,1)} %param.17) | copy-start | bytes 7864324
  (1 other events, 0.8 us)
Sparse Core Ops, SparseCore 0:
  9.7 69.9 all-gather.2
  81.4 36.5 all-gather.4

commit v12 on v10

--- a/solution.py
+++ b/solution.py
@@ -140,9 +140,11 @@
     cap_emb = cap_unit.astype(jnp.bfloat16)
     weight_hi = loss_cotangent.astype(jnp.bfloat16)
     weight_lo = (loss_cotangent - weight_hi.astype(jnp.float32)).astype(jnp.bfloat16)
-    weight_rows = jnp.zeros((2, feature_width), jnp.bfloat16)
-    weight_rows = weight_rows.at[0, :pair_count].set(weight_hi).at[1, :pair_count].set(weight_lo)
-    both_emb = jnp.concatenate([fig_emb, cap_emb, weight_rows], axis=0)
+    weight_lanes = jnp.zeros((2 * pair_count, 128), jnp.bfloat16)
+    weight_lanes = weight_lanes.at[:pair_count, 0].set(weight_hi).at[:pair_count, 1].set(weight_lo)
+    both_emb = jnp.concatenate(
+        [jnp.concatenate([fig_emb, cap_emb], axis=0), weight_lanes], axis=1
+    )
     all_both = lax.all_to_all(
         jnp.broadcast_to(both_emb[None], (dp_count,) + both_emb.shape),
         "dp",
@@ -150,11 +152,11 @@
         concat_axis=0,
         tiled=True,
     )
-    all_fig = all_both[:, :pair_count].reshape(-1, feature_width)
-    all_cap = all_both[:, pair_count : 2 * pair_count].reshape(-1, feature_width)
+    all_fig = all_both[:, :pair_count, :feature_width].reshape(-1, feature_width)
+    all_cap = all_both[:, pair_count:, :feature_width].reshape(-1, feature_width)
     all_weight = (
-        all_both[:, 2 * pair_count, :pair_count].astype(jnp.float32)
-        + all_both[:, 2 * pair_count + 1, :pair_count].astype(jnp.float32)
+        all_both[:, :pair_count, feature_width].astype(jnp.float32)
+        + all_both[:, :pair_count, feature_width + 1].astype(jnp.float32)
     ).reshape(-1)
     logit_mult = logit_scale[0]
     pair_total = all_fig.shape[0]

time: 266 us -> 262 us (0.985)
  waiting for transfers between devices: 131 us -> 125 us
    all_to_all x1, waiting for transfers between devices: 35.8 us -> 30.9 us  [body(): lax.all_to_all(jnp.broadcast_to(both_emb[None], (dp_count,) + both_emb.sh...]
  transfers between devices with their start and end apart: 6 -> 6, of which waited for: 5 -> 5; matrix products, arithmetic and copies ran while one was open for 21% -> 22% of each run, Pallas kernels for 0% -> 0%
where the time goes in v12:
time: 262 us; the launch traced here: 258 us
  waiting for transfers between devices  125 us (48%)
  matrix products  65.5 us (25%)
  starting transfers between devices  24.4 us (9%)
  between operations  15.8 us (6%)
  local copies, waits for them, and re-layouts  15.4 us (6%)
  other arithmetic  11.7 us (4%)
    all_to_all x1, waiting for transfers between devices, body(): lax.all_to_all(send_rows, 'dp', split_axis=0, concat_axis=0, tiled=True)  46.7 us
    all_to_all x2, waiting for transfers between devices, body(): lax.all_to_all(back_rows, 'dp', split_axis=0, concat_axis=0, tiled=True)  32.1 us
    all_to_all x1, waiting for transfers between devices, body(): lax.all_to_all(jnp.broadcast_to(both_emb[None], (dp_count,) + both_emb.sh...  30.9 us
    all_gather x1, waiting for transfers between devices, body(): lax.all_gather(out_weight, 'fsdp', axis=1, tiled=True)  14.3 us
    dot_general x2, matrix products, body(): lax.dot_general(key_value_ct, kv_full[cols], (((1,), (1,)), ((), ())), pr...  11.5 us
    all_to_all x2, starting transfers between devices, body(): lax.all_to_all(back_rows, 'dp', split_axis=0, concat_axis=0, tiled=True)  9.81 us
    dot_general x2, matrix products, body(): jnp.einsum('opk,opd->kd', send_onehot, home_rows, preferred_element_type=...  7.46 us
    all_to_all x1, starting transfers between devices, body(): lax.all_to_all(send_rows, 'dp', split_axis=0, concat_axis=0, tiled=True)  7.31 us
  transfers between devices with their start and end apart: 6, of which 5 were waited for; matrix products, arithmetic and copies ran while one was open for 22% of the time, Pallas kernels for 0%

profile of v12, /device:TPU:0, one launch (start us, length us, event | category | flops | bytes accessed | tf_op | source)
XLA Modules:
  0.0 258.0 jit_solution(14503466422385770425)
XLA Ops:
  15.5 4.5 %add_convert_fusion = bf16[16,51,2048]{2,1,0:T(8,128)(2,1)} fusion(f32[16,1,2048]{2,1,0:T(1,128)S(1)} %scatter.15, bf16[640,2048]{1,0:T(8,128)(2,1)S(1)} %copy-done, pred[16,50,640]{2,1,0:T(8,128)(4,1)S(1)} %broadcast_compare_fusion), kind=kOutput, calls=%fused_computation.6 | convolution fusion | flops 2142437376 | bytes 6606848 | tf_op jit(solution)/shard_map/opk,kd->opd/dot_general | solution.py:90
  20.0 7.3 %all-to-all-start = ((bf16[16,51,2048]{2,1,0:T(8,128)(2,1)}), bf16[16,51,2048]{2,1,0:T(8,128)(2,1)}, u32[]{:S(2)}, u32[]{:S(2)}) async-start(bf16[16,51,2048]{2,1,0:T(8,128)(2,1)} %add_convert_fusion), calls=%async_computation | async-start | bytes 7340032 | tf_op jit(solution)/shard_map/all_to_all | solution.py:93
  31.0 46.7 %all-to-all-done = bf16[16,51,2048]{2,1,0:T(8,128)(2,1)} async-done(((bf16[16,51,2048]{2,1,0:T(8,128)(2,1)}), bf16[16,51,2048]{2,1,0:T(8,128)(2,1)}, u32[]{:S(2)}, u32[]{:S(2)}) %all-to-all-start) | async-done | bytes 3342368 | tf_op jit(solution)/shard_map/all_to_all | solution.py:93
  78.9 5.1 %bitcast_convert_fusion = bf16[640,2048]{1,0:T(8,128)(2,1)S(1)} fusion(bf16[16,51,2048]{2,1,0:T(8,128)(2,1)} %all-to-all-done, s32[16,51]{1,0:T(8,128)S(1)} %concatenate.40), kind=kOutput, calls=%fused_computation.7 | convolution fusion | flops 2140928000 | bytes 5967040 | tf_op jit(solution)/shard_map/sop,opd->sd/dot_general | solution.py:103
  84.6 3.0 %fusion.37 = bf16[32,1024]{1,0:T(8,128)(2,1)S(1)} fusion(bf16[32,2048]{1,0:T(8,128)(2,1)S(1)} %convolution_convert_fusion, bf16[3,2048,1024]{2,1,0:T(8,128)(2,1)} %all-gather.3.cloned.1.call-done), kind=kOutput, calls=%fused_computation.71 | convolution fusion | flops 134250496 | bytes 4390912 | tf_op jit(solution)/shard_map/dot_general | solution.py:121
  87.8 4.2 %slice_bitcast_fusion.2 = (bf16[2048,1024]{1,0:T(8,128)(2,1)S(1)}, bf16[2048,1024]{1,0:T(8,128)(2,1)S(1)}) fusion(bf16[3,2048,1024]{2,1,0:T(8,128)(2,1)} %all-gather.3.cloned.1.call-done), kind=kLoop, calls=%fused_computation.14 | loop fusion | bytes 16777216 | tf_op jit(solution)/shard_map/squeeze | solution.py:110
  92.0 6.1 %fusion.8 = bf16[640,2048]{1,0:T(8,128)(2,1)S(1)} fusion(bf16[640,2048]{1,0:T(8,128)(2,1)S(1)} %bitcast_convert_fusion, bf16[2048,1024]{1,0:T(8,128)(2,1)S(1)} %get-tuple-element.57, bf16[2048,1024]{1,0:T(8,128)(2,1)S(1)} %get-tuple-element.58), kind=kOutput, calls=%fused_computation.16 | convolution fusion | flops 5386797056 | bytes 13631488 | tf_op jit(solution)/shard_map/dot_general | solution.py:124
  101.1 1.8 copy-done.7
  103.7 14.3 %all-gather.5.cloned.1.call-done = bf16[1024,2048]{1,0:T(8,128)(2,1)} async-done(((bf16[1024,256]{1,0:T(8,128)(2,1)}), bf16[1024,2048]{1,0:T(8,128)(2,1)}) %all-gather.5.cloned.1.call-update) | async-done | bytes 4194320 | tf_op jit(solution)/shard_map/all_gather | solution.py:108
  118.0 3.0 %convolution_add_fusion = f32[32,2048]{1,0:T(8,128)S(1)} fusion(bf16[32,1024]{1,0:T(8,128)(2,1)S(1)} %reshape.309, bf16[1024,2048]{1,0:T(8,128)(2,1)} %all-gather.5.cloned.1.call-done, bf16[32,2048]{1,0:T(8,128)(2,1)S(1)} %convolution_convert_fusion), kind=kOutput, calls=%fused_computation.27 | convolution fusion | flops 134348800 | bytes 4653056 | tf_op jit(solution)/shard_map/jvp()/dot_general | solution.py:34
  122.8 7.0 %all-to-all-start.1 = ((bf16[16,32,2176]{2,1,0:T(8,128)(2,1)}), bf16[16,32,2176]{2,1,0:T(8,128)(2,1)S(1)}, u32[]{:S(2)}, u32[]{:S(2)}) async-start(bf16[16,32,2176]{2,1,0:T(8,128)(2,1)} %broadcast_in_dim.99), calls=%async_computation.1 | async-start | bytes 4456448 | tf_op jit(solution)/shard_map/all_to_all | solution.py:148
  131.1 30.9 %all-to-all-done.1 = bf16[16,32,2176]{2,1,0:T(8,128)(2,1)S(1)} async-done(((bf16[16,32,2176]{2,1,0:T(8,128)(2,1)}), bf16[16,32,2176]{2,1,0:T(8,128)(2,1)S(1)}, u32[]{:S(2)}, u32[]{:S(2)}) %all-to-all-start.1) | async-done | bytes 2228256 | tf_op jit(solution)/shard_map/all_to_all | solution.py:148
  174.1 5.9 %fusion.5 = f32[640,1024]{1,0:T(8,128)S(1)} fusion(bf16[2048,1024]{1,0:T(8,128)(2,1)} %copy-done.9, bf16[2048,1024]{1,0:T(8,128)(2,1)} %copy-done.8, bf16[640,1024]{0,1:T(8,128)(2,1)} %bitcast.130, bf16[640,1024]{0,1:T(8,128)(2,1)} %bitcast.132), kind=kOutput, calls=%fused_computation.11 | convolution fusion | flops 2697986048 | bytes 13631488 | tf_op jit(solution)/shard_map/dot_general | solution.py:204
  180.0 2.3 fusion.36
  183.7 2.9 %fusion.16 = bf16[16,51,1024]{2,1,0:T(8,128)(2,1)} fusion(bf16[640,1024,1]{1,0,2:T(8,128)(2,1)S(1)} %fusion.20, s32[16,51]{1,0:T(8,128)S(1)} %copy-done.17), kind=kOutput, calls=%fused_computation.39 | convolution fusion | flops 1070905344 | bytes 2985152 | tf_op jit(solution)/shard_map/sop,sd->opd/dot_general | solution.py:217
  186.6 5.4 %all-to-all-start.3 = ((bf16[16,51,1024]{2,1,0:T(8,128)(2,1)}), bf16[16,51,1024]{2,1,0:T(8,128)(2,1)}, u32[]{:S(2)}, u32[]{:S(2)}) async-start(bf16[16,51,1024]{2,1,0:T(8,128)(2,1)} %fusion.16), calls=%async_computation.3 | async-start | bytes 3670016 | tf_op jit(solution)/shard_map/all_to_all | solution.py:220
  192.0 2.4 fusion.35
  194.4 5.6 %fusion.2 = f32[640,1024]{1,0:T(8,128)S(1)} fusion(bf16[2048,1024]{1,0:T(8,128)(2,1)} %copy-done.9, bf16[2048,1024]{1,0:T(8,128)(2,1)} %copy-done.8, bf16[640,1024]{0,1:T(8,128)(2,1)S(1)} %bitcast.131, bf16[640,1024]{0,1:T(8,128)(2,1)} %bitcast.133), kind=kOutput, calls=%fused_computation.9 | convolution fusion | flops 2697986048 | bytes 13631488 | tf_op jit(solution)/shard_map/dot_general | solution.py:204
  201.4 2.9 %fusion.15 = bf16[16,51,1024]{2,1,0:T(8,128)(2,1)} fusion(bf16[640,1024,1]{1,0,2:T(8,128)(2,1)S(1)} %fusion.19, s32[16,51]{1,0:T(8,128)S(1)} %copy-done.17), kind=kOutput, calls=%fused_computation.38 | convolution fusion | flops 1070905344 | bytes 2985152 | tf_op jit(solution)/shard_map/sop,sd->opd/dot_general | solution.py:217
  204.2 13.9 %all-to-all-done.3 = bf16[16,51,1024]{2,1,0:T(8,128)(2,1)} async-done(((bf16[16,51,1024]{2,1,0:T(8,128)(2,1)}), bf16[16,51,1024]{2,1,0:T(8,128)(2,1)}, u32[]{:S(2)}, u32[]{:S(2)}) %all-to-all-start.3) | async-done | bytes 1671200 | tf_op jit(solution)/shard_map/all_to_all | solution.py:220
  218.1 4.4 %all-to-all-start.2 = ((bf16[16,51,1024]{2,1,0:T(8,128)(2,1)}), bf16[16,51,1024]{2,1,0:T(8,128)(2,1)}, u32[]{:S(2)}, u32[]{:S(2)}) async-start(bf16[16,51,1024]{2,1,0:T(8,128)(2,1)} %fusion.15), calls=%async_computation.2 | async-start | bytes 3670016 | tf_op jit(solution)/shard_map/all_to_all | solution.py:220
  223.2 4.2 %bitcast_convert_fusion.1 = bf16[640,1024]{1,0:T(8,128)(2,1)} fusion(bf16[16,51,1024]{2,1,0:T(8,128)(2,1)} %all-to-all-done.3, pred[16,50,640]{2,1,0:T(8,128)(4,1)S(1)} %broadcast_compare_fusion), kind=kOutput, calls=%fused_computation.18 | convolution fusion | flops 1070202880 | bytes 3493888 | tf_op jit(solution)/shard_map/opk,opd->kd/dot_general | solution.py:222
  227.4 18.3 %all-to-all-done.2 = bf16[16,51,1024]{2,1,0:T(8,128)(2,1)} async-done(((bf16[16,51,1024]{2,1,0:T(8,128)(2,1)}), bf16[16,51,1024]{2,1,0:T(8,128)(2,1)}, u32[]{:S(2)}, u32[]{:S(2)}) %all-to-all-start.2) | async-done | bytes 1671200 | tf_op jit(solution)/shard_map/all_to_all | solution.py:220
  245.7 3.3 %bitcast_convert_fusion.2 = bf16[640,1024]{1,0:T(8,128)(2,1)S(1)} fusion(bf16[16,51,1024]{2,1,0:T(8,128)(2,1)} %all-to-all-done.2, pred[16,50,640]{2,1,0:T(8,128)(4,1)S(1)} %broadcast_compare_fusion), kind=kOutput, calls=%fused_computation.19 | convolution fusion | flops 1070202880 | bytes 3493888 | tf_op jit(solution)/shard_map/opk,opd->kd/dot_general | solution.py:222
  (132 shorter events, 37.0 us)
Async XLA Ops:
  7.2 8.4 %copy-start = (bf16[640,2048]{1,0:T(8,128)(2,1)S(1)}, bf16[640,2048]{1,0:T(8,128)(2,1)}, u32[]{:S(2)}) copy-start(bf16[640,2048]{1,0:T(8,128)(2,1)} %param.17) | copy-start | bytes 7864324
  7.2 77.4 %all-gather.3.cloned.1.call-start = ((), (), s32[]{:S(2)}) async-start(), calls=%async_computation.4 | async-start | bytes 14155776 | tf_op jit(solution)/shard_map/all_gather | solution.py:107
  20.0 8.1 %copy-start.22 = (f32[16]{0:T(128)S(1)}, f32[16]{0:T(128)}, u32[]{:S(2)}) copy-start(f32[16]{0:T(128)} %param.25) | copy-start | bytes 196
  20.0 8.2 %copy-start.18 = (s32[1,640]{1,0:T(1,128)S(1)}, s32[1,640]{1,0:T(1,128)}, u32[]{:S(2)}) copy-start(s32[1,640]{1,0:T(1,128)} %param.19) | copy-start | bytes 7684
  20.0 10.6 %copy-start.23 = (s32[16]{0:T(128)S(1)}, s32[16]{0:T(128)}, u32[]{:S(2)}) copy-start(s32[16]{0:T(128)} %param.23) | copy-start | bytes 196
  20.0 10.6 %copy-start.24 = (s32[16]{0:T(128)S(1)}, s32[16]{0:T(128)}, u32[]{:S(2)}) copy-start(s32[16]{0:T(128)} %param.22) | copy-start | bytes 196
  20.0 57.6 %all-to-all-start = ((bf16[16,51,2048]{2,1,0:T(8,128)(2,1)}), bf16[16,51,2048]{2,1,0:T(8,128)(2,1)}, u32[]{:S(2)}, u32[]{:S(2)}) async-start(bf16[16,51,2048]{2,1,0:T(8,128)(2,1)} %add_convert_fusion), calls=%async_computation | async-start | bytes 7340032 | tf_op jit(solution)/shard_map/all_to_all | solution.py:93
  27.3 90.7 %all-gather.5.cloned.1.call-start = ((), (), s32[]{:S(2)}) async-start(), calls=%async_computation.5 | async-start | bytes 4718592 | tf_op jit(solution)/shard_map/all_gather | solution.py:108
  30.6 48.3 %copy-start.14 = (bf16[32,128]{1,0:T(8,128)(2,1)}, bf16[32,128]{1,0:T(8,128)(2,1)S(1)}, u32[]{:S(2)}) copy-start(bf16[32,128]{1,0:T(8,128)(2,1)S(1)} %scatter.19) | copy-start | bytes 24580
  78.9 5.1 %copy-start.16 = (s32[16,51]{1,0:T(8,128)}, s32[16,51]{1,0:T(8,128)S(1)}, u32[]{:S(2)}) copy-start(s32[16,51]{1,0:T(8,128)S(1)} %concatenate.40) | copy-start | bytes 9796
  87.8 12.8 %copy-start.11 = (bf16[32,16,64]{2,1,0:T(8,128)(2,1)}, bf16[32,16,64]{2,1,0:T(8,128)(2,1)S(1)}, u32[]{:S(2)}) copy-start(bf16[32,16,64]{2,1,0:T(8,128)(2,1)S(1)} %reshape.307) | copy-start | bytes 196612
  92.0 6.1 %copy-start.8 = (bf16[2048,1024]{1,0:T(8,128)(2,1)}, bf16[2048,1024]{1,0:T(8,128)(2,1)S(1)}, u32[]{:S(2)}) copy-start(bf16[2048,1024]{1,0:T(8,128)(2,1)S(1)} %get-tuple-element.57) | copy-start | bytes 12582916
  92.0 6.1 %copy-start.9 = (bf16[2048,1024]{1,0:T(8,128)(2,1)}, bf16[2048,1024]{1,0:T(8,128)(2,1)S(1)}, u32[]{:S(2)}) copy-start(bf16[2048,1024]{1,0:T(8,128)(2,1)S(1)} %get-tuple-element.58) | copy-start | bytes 12582916
  100.6 2.9 %copy-start.5 = (bf16[640,1024]{0,1:T(8,128)(2,1)}, bf16[640,1024]{0,1:T(8,128)(2,1)S(1)}, u32[]{:S(2)}) copy-start(bf16[640,1024]{0,1:T(8,128)(2,1)S(1)} %copy.43) | copy-start | bytes 3932164
  103.7 17.6 %copy-start.15 = (bf16[32,128]{1,0:T(8,128)(2,1)S(1)}, bf16[32,128]{1,0:T(8,128)(2,1)}, u32[]{:S(2)}) copy-start(bf16[32,128]{1,0:T(8,128)(2,1)} %copy-done.14) | copy-start | bytes 24580
  122.8 39.2 %all-to-all-start.1 = ((bf16[16,32,2176]{2,1,0:T(8,128)(2,1)}), bf16[16,32,2176]{2,1,0:T(8,128)(2,1)S(1)}, u32[]{:S(2)}, u32[]{:S(2)}) async-start(bf16[16,32,2176]{2,1,0:T(8,128)(2,1)} %broadcast_in_dim.99), calls=%async_computation.1 | async-start | bytes 4456448 | tf_op jit(solution)/shard_map/all_to_all | solution.py:148
  130.5 33.5 %copy-start.19 = (s32[16]{0:T(128)}, s32[16]{0:T(128)S(1)}, u32[]{:S(2)}) copy-start(s32[16]{0:T(128)S(1)} %iota_add_fusion) | copy-start | bytes 196
  167.0 2.6 %copy-start.6 = (bf16[640,1024]{0,1:T(8,128)(2,1)S(1)}, bf16[640,1024]{0,1:T(8,128)(2,1)}, u32[]{:S(2)}) copy-start(bf16[640,1024]{0,1:T(8,128)(2,1)} %copy-done.5) | copy-start | bytes 3932164
  186.6 31.5 %all-to-all-start.3 = ((bf16[16,51,1024]{2,1,0:T(8,128)(2,1)}), bf16[16,51,1024]{2,1,0:T(8,128)(2,1)}, u32[]{:S(2)}, u32[]{:S(2)}) async-start(bf16[16,51,1024]{2,1,0:T(8,128)(2,1)} %fusion.16), calls=%async_computation.3 | async-start | bytes 3670016 | tf_op jit(solution)/shard_map/all_to_all | solution.py:220
  204.2 18.3 %copy-start.20 = (s32[16]{0:T(128)S(1)}, s32[16]{0:T(128)}, u32[]{:S(2)}) copy-start(s32[16]{0:T(128)} %copy-done.19) | copy-start | bytes 196
  204.2 18.3 %copy-start.21 = (f32[256]{0:T(256)S(1)}, f32[256]{0:T(256)}, u32[]{:S(2)}) copy-start(f32[256]{0:T(256)} %get-tuple-element.71) | copy-start | bytes 3076
  218.1 27.6 %all-to-all-start.2 = ((bf16[16,51,1024]{2,1,0:T(8,128)(2,1)}), bf16[16,51,1024]{2,1,0:T(8,128)(2,1)}, u32[]{:S(2)}, u32[]{:S(2)}) async-start(bf16[16,51,1024]{2,1,0:T(8,128)(2,1)} %fusion.15), calls=%async_computation.2 | async-start | bytes 3670016 | tf_op jit(solution)/shard_map/all_to_all | solution.py:220
  245.7 3.3 %copy-start.10 = (bf16[640,1024]{1,0:T(8,128)(2,1)S(1)}, bf16[640,1024]{1,0:T(8,128)(2,1)}, u32[]{:S(2)}) copy-start(bf16[640,1024]{1,0:T(8,128)(2,1)} %bitcast_convert_fusion.1) | copy-start | bytes 3932164
  245.7 5.0 %copy-start.1 = (bf16[640,2048]{1,0:T(8,128)(2,1)S(1)}, bf16[640,2048]{1,0:T(8,128)(2,1)}, u32[]{:S(2)}) copy-start(bf16[640,2048]{1,0:T(8,128)(2,1)} %param.17) | copy-start | bytes 7864324
  (8 other events, 15.8 us)
Sparse Core Ops, SparseCore 0:
  9.7 69.9 all-gather.2
  81.4 36.5 all-gather.4

commit v13 on v12

--- a/solution.py
+++ b/solution.py
@@ -192,6 +192,7 @@
     query_ct = jnp.concatenate([figure_direction, caption_direction], axis=0)
     query_ct_rows, key_value_ct = pullback(query_ct)
     half = feature_width // 2
+    onehot_three = jnp.concatenate([query_onehot] * 3, axis=0)
     grad_parts = []
     for part in range(2):
         cols = slice(part * half, (part + 1) * half)
@@ -207,11 +208,17 @@
             (((1,), (1,)), ((), ())),
             preferred_element_type=jnp.float32,
         )
+        scatter_src = query_part + query_ct[:, cols]
+        piece_hi = lax.reduce_precision(scatter_src, exponent_bits=8, mantissa_bits=7)
+        rest = scatter_src - piece_hi
+        piece_mid = lax.reduce_precision(rest, exponent_bits=8, mantissa_bits=7)
+        piece_lo = rest - piece_mid
+        pieces = jnp.concatenate([piece_hi, piece_mid, piece_lo], axis=0).astype(jnp.bfloat16)
         scatter_part = lax.dot_general(
-            query_onehot.astype(jnp.float32),
-            query_part + query_ct[:, cols],
+            onehot_three,
+            pieces,
             (((0,), (0,)), ((), ())),
-            precision=lax.Precision.HIGHEST,
+            preferred_element_type=jnp.float32,
         )
         slot_gradient = (slot_part + scatter_part).astype(jnp.bfloat16)
         back_rows = jnp.einsum(

time: 262 us -> 260 us (level); the launches traced: 258 us -> 259 us
  matrix products: 65.5 us -> 68.3 us
    dot_general x2, matrix products: 5.74 us -> 10 us  [body(): jnp.einsum('sop,sd->opd', recv_onehot, slot_gradient, preferred_element_t...]
    dot_general x2 -> x0, matrix products: 2.67 us -> none  [body(): lax.dot_general(query_onehot.astype(jnp.float32), query_part + query_ct[:...]
where the time goes in v13:
time: 260 us; the launch traced here: 259 us
  waiting for transfers between devices  124 us (48%)
  matrix products  68.3 us (26%)
  starting transfers between devices  23.9 us (9%)
  local copies, waits for them, and re-layouts  15.7 us (6%)
  between operations  15.3 us (6%)
  other arithmetic  11.9 us (5%)
    all_to_all x1, waiting for transfers between devices, body(): lax.all_to_all(send_rows, 'dp', split_axis=0, concat_axis=0, tiled=True)  46.8 us
    all_to_all x2, waiting for transfers between devices, body(): lax.all_to_all(back_rows, 'dp', split_axis=0, concat_axis=0, tiled=True)  31.6 us
    all_to_all x1, waiting for transfers between devices, body(): lax.all_to_all(jnp.broadcast_to(both_emb[None], (dp_count,) + both_emb.sh...  30.2 us
    dot_general x2, matrix products, body(): lax.dot_general(key_value_ct, kv_full[cols], (((1,), (1,)), ((), ())), pr...  14.1 us
    all_gather x1, waiting for transfers between devices, body(): lax.all_gather(out_weight, 'fsdp', axis=1, tiled=True)  14.1 us
    dot_general x2, matrix products, body(): jnp.einsum('sop,sd->opd', recv_onehot, slot_gradient, preferred_element_t...  10 us
    all_to_all x2, starting transfers between devices, body(): lax.all_to_all(back_rows, 'dp', split_axis=0, concat_axis=0, tiled=True)  9.51 us
    all_to_all x1, starting transfers between devices, body(): lax.all_to_all(send_rows, 'dp', split_axis=0, concat_axis=0, tiled=True)  7.3 us
  transfers between devices with their start and end apart: 6, of which 5 were waited for; matrix products, arithmetic and copies ran while one was open for 22% of the time, Pallas kernels for 0%

profile of v13, /device:TPU:0, one launch (start us, length us, event | category | flops | bytes accessed | tf_op | source)
XLA Modules:
  0.0 259.1 jit_solution(14258695298128781325)
XLA Ops:
  15.5 4.5 %add_convert_fusion = bf16[16,51,2048]{2,1,0:T(8,128)(2,1)} fusion(f32[16,1,2048]{2,1,0:T(1,128)S(1)} %scatter.15, bf16[640,2048]{1,0:T(8,128)(2,1)S(1)} %copy-done, pred[16,50,640]{2,1,0:T(8,128)(4,1)S(1)} %broadcast_compare_fusion), kind=kOutput, calls=%fused_computation.6 | convolution fusion | flops 2142437376 | bytes 6606848 | tf_op jit(solution)/shard_map/opk,kd->opd/dot_general | solution.py:90
  20.0 7.3 %all-to-all-start = ((bf16[16,51,2048]{2,1,0:T(8,128)(2,1)}), bf16[16,51,2048]{2,1,0:T(8,128)(2,1)}, u32[]{:S(2)}, u32[]{:S(2)}) async-start(bf16[16,51,2048]{2,1,0:T(8,128)(2,1)} %add_convert_fusion), calls=%async_computation | async-start | bytes 7340032 | tf_op jit(solution)/shard_map/all_to_all | solution.py:93
  31.0 46.8 %all-to-all-done = bf16[16,51,2048]{2,1,0:T(8,128)(2,1)} async-done(((bf16[16,51,2048]{2,1,0:T(8,128)(2,1)}), bf16[16,51,2048]{2,1,0:T(8,128)(2,1)}, u32[]{:S(2)}, u32[]{:S(2)}) %all-to-all-start) | async-done | bytes 3342368 | tf_op jit(solution)/shard_map/all_to_all | solution.py:93
  79.0 5.1 %bitcast_convert_fusion = bf16[640,2048]{1,0:T(8,128)(2,1)S(1)} fusion(bf16[16,51,2048]{2,1,0:T(8,128)(2,1)} %all-to-all-done, s32[16,51]{1,0:T(8,128)S(1)} %concatenate.54), kind=kOutput, calls=%fused_computation.7 | convolution fusion | flops 2140928000 | bytes 5967040 | tf_op jit(solution)/shard_map/sop,opd->sd/dot_general | solution.py:103
  84.8 3.0 %fusion.37 = bf16[32,1024]{1,0:T(8,128)(2,1)S(1)} fusion(bf16[32,2048]{1,0:T(8,128)(2,1)S(1)} %convolution_convert_fusion, bf16[3,2048,1024]{2,1,0:T(8,128)(2,1)} %all-gather.3.cloned.1.call-done), kind=kOutput, calls=%fused_computation.71 | convolution fusion | flops 134250496 | bytes 4390912 | tf_op jit(solution)/shard_map/dot_general | solution.py:121
  87.9 4.2 %slice_bitcast_fusion.2 = (bf16[2048,1024]{1,0:T(8,128)(2,1)S(1)}, bf16[2048,1024]{1,0:T(8,128)(2,1)S(1)}) fusion(bf16[3,2048,1024]{2,1,0:T(8,128)(2,1)} %all-gather.3.cloned.1.call-done), kind=kLoop, calls=%fused_computation.14 | loop fusion | bytes 16777216 | tf_op jit(solution)/shard_map/squeeze | solution.py:110
  92.2 6.1 %fusion.8 = bf16[640,2048]{1,0:T(8,128)(2,1)S(1)} fusion(bf16[640,2048]{1,0:T(8,128)(2,1)S(1)} %bitcast_convert_fusion, bf16[2048,1024]{1,0:T(8,128)(2,1)S(1)} %get-tuple-element.57, bf16[2048,1024]{1,0:T(8,128)(2,1)S(1)} %get-tuple-element.58), kind=kOutput, calls=%fused_computation.16 | convolution fusion | flops 5386797056 | bytes 13631488 | tf_op jit(solution)/shard_map/dot_general | solution.py:124
  101.3 1.8 copy-done.7
  103.9 14.1 %all-gather.5.cloned.1.call-done = bf16[1024,2048]{1,0:T(8,128)(2,1)} async-done(((bf16[1024,256]{1,0:T(8,128)(2,1)}), bf16[1024,2048]{1,0:T(8,128)(2,1)}) %all-gather.5.cloned.1.call-update) | async-done | bytes 4194320 | tf_op jit(solution)/shard_map/all_gather | solution.py:108
  118.0 3.0 %convolution_add_fusion = f32[32,2048]{1,0:T(8,128)S(1)} fusion(bf16[32,1024]{1,0:T(8,128)(2,1)S(1)} %reshape.309, bf16[1024,2048]{1,0:T(8,128)(2,1)} %all-gather.5.cloned.1.call-done, bf16[32,2048]{1,0:T(8,128)(2,1)S(1)} %convolution_convert_fusion), kind=kOutput, calls=%fused_computation.27 | convolution fusion | flops 134348800 | bytes 4653056 | tf_op jit(solution)/shard_map/jvp()/dot_general | solution.py:34
  122.8 6.8 %all-to-all-start.1 = ((bf16[16,32,2176]{2,1,0:T(8,128)(2,1)}), bf16[16,32,2176]{2,1,0:T(8,128)(2,1)S(1)}, u32[]{:S(2)}, u32[]{:S(2)}) async-start(bf16[16,32,2176]{2,1,0:T(8,128)(2,1)} %broadcast_in_dim.99), calls=%async_computation.1 | async-start | bytes 4456448 | tf_op jit(solution)/shard_map/all_to_all | solution.py:148
  131.6 30.2 %all-to-all-done.1 = bf16[16,32,2176]{2,1,0:T(8,128)(2,1)S(1)} async-done(((bf16[16,32,2176]{2,1,0:T(8,128)(2,1)}), bf16[16,32,2176]{2,1,0:T(8,128)(2,1)S(1)}, u32[]{:S(2)}, u32[]{:S(2)}) %all-to-all-start.1) | async-done | bytes 2228256 | tf_op jit(solution)/shard_map/all_to_all | solution.py:148
  173.6 7.4 %fusion.5 = f32[640,1024]{1,0:T(8,128)} fusion(bf16[2048,1024]{1,0:T(8,128)(2,1)} %copy-done.9, bf16[2048,1024]{1,0:T(8,128)(2,1)} %copy-done.8, bf16[640,1024]{0,1:T(8,128)(2,1)} %bitcast.134, bf16[640,1024]{0,1:T(8,128)(2,1)} %bitcast.136), kind=kOutput, calls=%fused_computation.11 | convolution fusion | flops 2697986048 | bytes 13631488 | tf_op jit(solution)/shard_map/dot_general | solution.py:205
  181.1 2.3 reduce-precision_convert_fusion.1
  183.4 5.0 %fusion.16 = bf16[16,51,1024]{2,1,0:T(8,128)(2,1)} fusion(s32[16,51]{1,0:T(8,128)S(1)} %copy-done.18, f32[640,1024]{1,0:T(8,128)} %fusion.5, bf16[32,1024]{1,0:T(8,128)(2,1)S(1)} %get-tuple-element.71, bf16[32,1024]{1,0:T(8,128)(2,1)S(1)} %get-tuple-element.72, bf16[32,1024]{1,0:T(8,128)(2,1)S(1)} %get-tuple-element.70, pred[32,640]{1,0:T(32,128)(4,1)S(1)} %copy-done.16), kind=kOutput, calls=%fused_computation.39 | convolution fusion | flops 1198757888 | bytes 4512960 | tf_op jit(solution)/shard_map/sop,sd->opd/dot_general | solution.py:224
  188.5 5.1 %all-to-all-start.3 = ((bf16[16,51,1024]{2,1,0:T(8,128)(2,1)}), bf16[16,51,1024]{2,1,0:T(8,128)(2,1)S(1)}, u32[]{:S(2)}, u32[]{:S(2)}) async-start(bf16[16,51,1024]{2,1,0:T(8,128)(2,1)} %fusion.16), calls=%async_computation.3 | async-start | bytes 3670016 | tf_op jit(solution)/shard_map/all_to_all | solution.py:227
  193.6 2.5 reduce-precision_convert_fusion.3
  196.1 6.7 %fusion.2 = f32[640,1024]{1,0:T(8,128)} fusion(bf16[2048,1024]{1,0:T(8,128)(2,1)} %copy-done.9, bf16[2048,1024]{1,0:T(8,128)(2,1)} %copy-done.8, bf16[640,1024]{0,1:T(8,128)(2,1)S(1)} %bitcast.135, bf16[640,1024]{0,1:T(8,128)(2,1)S(1)} %bitcast.137), kind=kOutput, calls=%fused_computation.9 | convolution fusion | flops 2697986048 | bytes 13631488 | tf_op jit(solution)/shard_map/dot_general | solution.py:205
  202.8 5.0 %fusion.15 = bf16[16,51,1024]{2,1,0:T(8,128)(2,1)} fusion(s32[16,51]{1,0:T(8,128)S(1)} %copy-done.18, f32[640,1024]{1,0:T(8,128)} %fusion.2, bf16[32,1024]{1,0:T(8,128)(2,1)S(1)} %get-tuple-element.68, bf16[32,1024]{1,0:T(8,128)(2,1)S(1)} %get-tuple-element.69, bf16[32,1024]{1,0:T(8,128)(2,1)S(1)} %get-tuple-element.67, pred[32,640]{1,0:T(32,128)(4,1)S(1)} %copy-done.16), kind=kOutput, calls=%fused_computation.38 | convolution fusion | flops 1198757888 | bytes 4512960 | tf_op jit(solution)/shard_map/sop,sd->opd/dot_general | solution.py:224
  207.8 11.8 %all-to-all-done.3 = bf16[16,51,1024]{2,1,0:T(8,128)(2,1)S(1)} async-done(((bf16[16,51,1024]{2,1,0:T(8,128)(2,1)}), bf16[16,51,1024]{2,1,0:T(8,128)(2,1)S(1)}, u32[]{:S(2)}, u32[]{:S(2)}) %all-to-all-start.3) | async-done | bytes 1671200 | tf_op jit(solution)/shard_map/all_to_all | solution.py:227
  219.6 4.4 %all-to-all-start.2 = ((bf16[16,51,1024]{2,1,0:T(8,128)(2,1)}), bf16[16,51,1024]{2,1,0:T(8,128)(2,1)}, u32[]{:S(2)}, u32[]{:S(2)}) async-start(bf16[16,51,1024]{2,1,0:T(8,128)(2,1)} %fusion.15), calls=%async_computation.2 | async-start | bytes 3670016 | tf_op jit(solution)/shard_map/all_to_all | solution.py:227
  224.7 2.7 %bitcast_convert_fusion.1 = bf16[640,1024]{1,0:T(8,128)(2,1)} fusion(bf16[16,51,1024]{2,1,0:T(8,128)(2,1)S(1)} %all-to-all-done.3, pred[16,50,640]{2,1,0:T(8,128)(4,1)S(1)} %broadcast_compare_fusion), kind=kOutput, calls=%fused_computation.18 | convolution fusion | flops 1070202880 | bytes 3493888 | tf_op jit(solution)/shard_map/opk,opd->kd/dot_general | solution.py:229
  227.4 19.8 %all-to-all-done.2 = bf16[16,51,1024]{2,1,0:T(8,128)(2,1)} async-done(((bf16[16,51,1024]{2,1,0:T(8,128)(2,1)}), bf16[16,51,1024]{2,1,0:T(8,128)(2,1)}, u32[]{:S(2)}, u32[]{:S(2)}) %all-to-all-start.2) | async-done | bytes 1671200 | tf_op jit(solution)/shard_map/all_to_all | solution.py:227
  247.2 3.3 %bitcast_convert_fusion.2 = bf16[640,1024]{1,0:T(8,128)(2,1)S(1)} fusion(bf16[16,51,1024]{2,1,0:T(8,128)(2,1)} %all-to-all-done.2, pred[16,50,640]{2,1,0:T(8,128)(4,1)S(1)} %broadcast_compare_fusion), kind=kOutput, calls=%fused_computation.19 | convolution fusion | flops 1070202880 | bytes 3493888 | tf_op jit(solution)/shard_map/opk,opd->kd/dot_general | solution.py:229
  (133 shorter events, 34.8 us)
Async XLA Ops:
  7.2 8.4 %copy-start = (bf16[640,2048]{1,0:T(8,128)(2,1)S(1)}, bf16[640,2048]{1,0:T(8,128)(2,1)}, u32[]{:S(2)}) copy-start(bf16[640,2048]{1,0:T(8,128)(2,1)} %param.17) | copy-start | bytes 7864324
  7.2 77.6 %all-gather.3.cloned.1.call-start = ((), (), s32[]{:S(2)}) async-start(), calls=%async_computation.4 | async-start | bytes 14155776 | tf_op jit(solution)/shard_map/all_gather | solution.py:107
  20.0 8.1 %copy-start.22 = (f32[16]{0:T(128)S(1)}, f32[16]{0:T(128)}, u32[]{:S(2)}) copy-start(f32[16]{0:T(128)} %param.25) | copy-start | bytes 196
  20.0 8.2 %copy-start.19 = (s32[1,640]{1,0:T(1,128)S(1)}, s32[1,640]{1,0:T(1,128)}, u32[]{:S(2)}) copy-start(s32[1,640]{1,0:T(1,128)} %param.19) | copy-start | bytes 7684
  20.0 10.6 %copy-start.23 = (s32[16]{0:T(128)S(1)}, s32[16]{0:T(128)}, u32[]{:S(2)}) copy-start(s32[16]{0:T(128)} %param.23) | copy-start | bytes 196
  20.0 10.6 %copy-start.24 = (s32[16]{0:T(128)S(1)}, s32[16]{0:T(128)}, u32[]{:S(2)}) copy-start(s32[16]{0:T(128)} %param.22) | copy-start | bytes 196
  20.0 57.8 %all-to-all-start = ((bf16[16,51,2048]{2,1,0:T(8,128)(2,1)}), bf16[16,51,2048]{2,1,0:T(8,128)(2,1)}, u32[]{:S(2)}, u32[]{:S(2)}) async-start(bf16[16,51,2048]{2,1,0:T(8,128)(2,1)} %add_convert_fusion), calls=%async_computation | async-start | bytes 7340032 | tf_op jit(solution)/shard_map/all_to_all | solution.py:93
  27.3 90.7 %all-gather.5.cloned.1.call-start = ((), (), s32[]{:S(2)}) async-start(), calls=%async_computation.5 | async-start | bytes 4718592 | tf_op jit(solution)/shard_map/all_gather | solution.py:108
  30.6 48.4 %copy-start.14 = (bf16[32,128]{1,0:T(8,128)(2,1)}, bf16[32,128]{1,0:T(8,128)(2,1)S(1)}, u32[]{:S(2)}) copy-start(bf16[32,128]{1,0:T(8,128)(2,1)S(1)} %scatter.19) | copy-start | bytes 24580
  79.0 5.1 %copy-start.17 = (s32[16,51]{1,0:T(8,128)}, s32[16,51]{1,0:T(8,128)S(1)}, u32[]{:S(2)}) copy-start(s32[16,51]{1,0:T(8,128)S(1)} %concatenate.54) | copy-start | bytes 9796
  87.9 12.8 %copy-start.11 = (bf16[32,16,64]{2,1,0:T(8,128)(2,1)}, bf16[32,16,64]{2,1,0:T(8,128)(2,1)S(1)}, u32[]{:S(2)}) copy-start(bf16[32,16,64]{2,1,0:T(8,128)(2,1)S(1)} %reshape.307) | copy-start | bytes 196612
  92.1 6.1 %copy-start.8 = (bf16[2048,1024]{1,0:T(8,128)(2,1)}, bf16[2048,1024]{1,0:T(8,128)(2,1)S(1)}, u32[]{:S(2)}) copy-start(bf16[2048,1024]{1,0:T(8,128)(2,1)S(1)} %get-tuple-element.57) | copy-start | bytes 12582916
  92.1 6.1 %copy-start.9 = (bf16[2048,1024]{1,0:T(8,128)(2,1)}, bf16[2048,1024]{1,0:T(8,128)(2,1)S(1)}, u32[]{:S(2)}) copy-start(bf16[2048,1024]{1,0:T(8,128)(2,1)S(1)} %get-tuple-element.58) | copy-start | bytes 12582916
  100.7 2.9 %copy-start.5 = (bf16[640,1024]{0,1:T(8,128)(2,1)}, bf16[640,1024]{0,1:T(8,128)(2,1)S(1)}, u32[]{:S(2)}) copy-start(bf16[640,1024]{0,1:T(8,128)(2,1)S(1)} %copy.43) | copy-start | bytes 3932164
  103.9 17.4 %copy-start.15 = (bf16[32,128]{1,0:T(8,128)(2,1)S(1)}, bf16[32,128]{1,0:T(8,128)(2,1)}, u32[]{:S(2)}) copy-start(bf16[32,128]{1,0:T(8,128)(2,1)} %copy-done.14) | copy-start | bytes 24580
  122.8 39.0 %all-to-all-start.1 = ((bf16[16,32,2176]{2,1,0:T(8,128)(2,1)}), bf16[16,32,2176]{2,1,0:T(8,128)(2,1)S(1)}, u32[]{:S(2)}, u32[]{:S(2)}) async-start(bf16[16,32,2176]{2,1,0:T(8,128)(2,1)} %broadcast_in_dim.99), calls=%async_computation.1 | async-start | bytes 4456448 | tf_op jit(solution)/shard_map/all_to_all | solution.py:148
  130.3 33.0 %copy-start.20 = (s32[16]{0:T(128)}, s32[16]{0:T(128)S(1)}, u32[]{:S(2)}) copy-start(s32[16]{0:T(128)S(1)} %iota_add_fusion) | copy-start | bytes 196
  164.8 2.5 copy-start.4
  166.5 2.6 %copy-start.6 = (bf16[640,1024]{0,1:T(8,128)(2,1)S(1)}, bf16[640,1024]{0,1:T(8,128)(2,1)}, u32[]{:S(2)}) copy-start(bf16[640,1024]{0,1:T(8,128)(2,1)} %copy-done.5) | copy-start | bytes 3932164
  188.5 31.1 %all-to-all-start.3 = ((bf16[16,51,1024]{2,1,0:T(8,128)(2,1)}), bf16[16,51,1024]{2,1,0:T(8,128)(2,1)S(1)}, u32[]{:S(2)}, u32[]{:S(2)}) async-start(bf16[16,51,1024]{2,1,0:T(8,128)(2,1)} %fusion.16), calls=%async_computation.3 | async-start | bytes 3670016 | tf_op jit(solution)/shard_map/all_to_all | solution.py:227
  207.8 16.2 %copy-start.21 = (s32[16]{0:T(128)S(1)}, s32[16]{0:T(128)}, u32[]{:S(2)}) copy-start(s32[16]{0:T(128)} %copy-done.20) | copy-start | bytes 196
  219.6 27.6 %all-to-all-start.2 = ((bf16[16,51,1024]{2,1,0:T(8,128)(2,1)}), bf16[16,51,1024]{2,1,0:T(8,128)(2,1)}, u32[]{:S(2)}, u32[]{:S(2)}) async-start(bf16[16,51,1024]{2,1,0:T(8,128)(2,1)} %fusion.15), calls=%async_computation.2 | async-start | bytes 3670016 | tf_op jit(solution)/shard_map/all_to_all | solution.py:227
  247.2 3.3 %copy-start.10 = (bf16[640,1024]{1,0:T(8,128)(2,1)S(1)}, bf16[640,1024]{1,0:T(8,128)(2,1)}, u32[]{:S(2)}) copy-start(bf16[640,1024]{1,0:T(8,128)(2,1)} %bitcast_convert_fusion.1) | copy-start | bytes 3932164
  247.2 5.0 %copy-start.1 = (bf16[640,2048]{1,0:T(8,128)(2,1)S(1)}, bf16[640,2048]{1,0:T(8,128)(2,1)}, u32[]{:S(2)}) copy-start(bf16[640,2048]{1,0:T(8,128)(2,1)} %param.17) | copy-start | bytes 7864324
  (9 other events, 19.3 us)
Sparse Core Ops, SparseCore 0:
  9.7 69.9 all-gather.2
  81.4 36.5 all-gather.4

commit v14 on v13

--- a/solution.py
+++ b/solution.py
@@ -169,20 +169,26 @@
     own_rows = first_pair + jnp.arange(pair_count)
     own_mask = (jnp.arange(pair_total)[None, :] == own_rows[:, None]).astype(jnp.float32)
     loss_all = 0.5 * (row_lse - diag_logit) + 0.5 * (col_lse - diag_logit)
-    pair_loss = jnp.dot(own_mask, loss_all, precision=lax.Precision.HIGHEST)
+    pair_loss = lax.dynamic_slice(loss_all, (first_pair,), (pair_count,))
     prob_rows = jnp.exp(logits - row_lse[:, None])
     prob_cols = jnp.exp(logits - col_lse[None, :])
     coef = 0.5 * all_weight[:, None] * (prob_rows - eye_mat) + 0.5 * (
         prob_cols - eye_mat
     ) * all_weight[None, :]
-    coef_rows = jnp.dot(own_mask, coef, precision=lax.Precision.HIGHEST)
-    coef_cols = jnp.dot(own_mask, coef.T, precision=lax.Precision.HIGHEST)
-    fig_grad = logit_mult * jnp.dot(
-        coef_rows, all_cap.astype(jnp.float32), precision=lax.Precision.HIGHEST
-    )
-    cap_grad = logit_mult * jnp.dot(
-        coef_cols, all_fig.astype(jnp.float32), precision=lax.Precision.HIGHEST
-    )
+    coef_rows = lax.dynamic_slice(coef, (first_pair, 0), (pair_count, pair_total))
+    coef_cols = lax.dynamic_slice(coef, (0, first_pair), (pair_total, pair_count)).T
+
+    def exact_product(coef_part, emb):
+        piece_hi = lax.reduce_precision(coef_part, exponent_bits=8, mantissa_bits=7)
+        rest = coef_part - piece_hi
+        piece_mid = lax.reduce_precision(rest, exponent_bits=8, mantissa_bits=7)
+        piece_lo = rest - piece_mid
+        pieces = jnp.concatenate([piece_hi, piece_mid, piece_lo], axis=1).astype(jnp.bfloat16)
+        emb_three = jnp.concatenate([emb, emb, emb], axis=0)
+        return jnp.dot(pieces, emb_three, preferred_element_type=jnp.float32)
+
+    fig_grad = logit_mult * exact_product(coef_rows, all_cap)
+    cap_grad = logit_mult * exact_product(coef_cols, all_fig)
     figure_direction = fig_inv * (
         fig_grad - fig_unit * jnp.sum(fig_unit * fig_grad, axis=1, keepdims=True)
     )

time: 260 us -> 264 us (1.015)
  no operation moved by 1% of the time
where the time goes in v14:
time: 264 us; the launch traced here: 263 us
  waiting for transfers between devices  124 us (47%)
  matrix products  69.3 us (26%)
  starting transfers between devices  23.9 us (9%)
  local copies, waits for them, and re-layouts  18.3 us (7%)
  between operations  15.4 us (6%)
  other arithmetic  12.1 us (5%)
    all_to_all x1, waiting for transfers between devices, body(): lax.all_to_all(send_rows, 'dp', split_axis=0, concat_axis=0, tiled=True)  46.8 us
    all_to_all x2, waiting for transfers between devices, body(): lax.all_to_all(back_rows, 'dp', split_axis=0, concat_axis=0, tiled=True)  31.7 us
    all_to_all x1, waiting for transfers between devices, body(): lax.all_to_all(jnp.broadcast_to(both_emb[None], (dp_count,) + both_emb.sh...  30.2 us
    all_gather x1, waiting for transfers between devices, body(): lax.all_gather(out_weight, 'fsdp', axis=1, tiled=True)  14.1 us
    dot_general x2, matrix products, body(): lax.dot_general(key_value_ct, kv_full[cols], (((1,), (1,)), ((), ())), pr...  14.1 us
    dot_general x2, matrix products, body(): jnp.einsum('sop,sd->opd', recv_onehot, slot_gradient, preferred_element_t...  10 us
    all_to_all x2, starting transfers between devices, body(): lax.all_to_all(back_rows, 'dp', split_axis=0, concat_axis=0, tiled=True)  9.51 us
    all_to_all x1, starting transfers between devices, body(): lax.all_to_all(send_rows, 'dp', split_axis=0, concat_axis=0, tiled=True)  7.3 us
  transfers between devices with their start and end apart: 6, of which 5 were waited for; matrix products, arithmetic and copies ran while one was open for 22% of the time, Pallas kernels for 0%

profile of v14, /device:TPU:0, one launch (start us, length us, event | category | flops | bytes accessed | tf_op | source)
XLA Modules:
  0.0 263.1 jit_solution(17651575859086107045)
XLA Ops:
  15.5 4.5 %add_convert_fusion = bf16[16,51,2048]{2,1,0:T(8,128)(2,1)} fusion(f32[16,1,2048]{2,1,0:T(1,128)S(1)} %scatter.15, bf16[640,2048]{1,0:T(8,128)(2,1)S(1)} %copy-done, pred[16,50,640]{2,1,0:T(8,128)(4,1)S(1)} %broadcast_compare_fusion), kind=kOutput, calls=%fused_computation.6 | convolution fusion | flops 2142437376 | bytes 6606848 | tf_op jit(solution)/shard_map/opk,kd->opd/dot_general | solution.py:90
  20.0 7.3 %all-to-all-start = ((bf16[16,51,2048]{2,1,0:T(8,128)(2,1)}), bf16[16,51,2048]{2,1,0:T(8,128)(2,1)}, u32[]{:S(2)}, u32[]{:S(2)}) async-start(bf16[16,51,2048]{2,1,0:T(8,128)(2,1)} %add_convert_fusion), calls=%async_computation | async-start | bytes 7340032 | tf_op jit(solution)/shard_map/all_to_all | solution.py:93
  31.0 46.8 %all-to-all-done = bf16[16,51,2048]{2,1,0:T(8,128)(2,1)} async-done(((bf16[16,51,2048]{2,1,0:T(8,128)(2,1)}), bf16[16,51,2048]{2,1,0:T(8,128)(2,1)}, u32[]{:S(2)}, u32[]{:S(2)}) %all-to-all-start) | async-done | bytes 3342368 | tf_op jit(solution)/shard_map/all_to_all | solution.py:93
  79.0 5.1 %bitcast_convert_fusion = bf16[640,2048]{1,0:T(8,128)(2,1)S(1)} fusion(bf16[16,51,2048]{2,1,0:T(8,128)(2,1)} %all-to-all-done, s32[16,51]{1,0:T(8,128)S(1)} %concatenate.68), kind=kOutput, calls=%fused_computation.7 | convolution fusion | flops 2140928000 | bytes 5967040 | tf_op jit(solution)/shard_map/sop,opd->sd/dot_general | solution.py:103
  84.7 3.0 %fusion.55 = bf16[32,1024]{1,0:T(8,128)(2,1)S(1)} fusion(bf16[32,2048]{1,0:T(8,128)(2,1)S(1)} %convolution_convert_fusion, bf16[3,2048,1024]{2,1,0:T(8,128)(2,1)} %all-gather.3.cloned.1.call-done), kind=kOutput, calls=%fused_computation.83 | convolution fusion | flops 134250496 | bytes 4390912 | tf_op jit(solution)/shard_map/dot_general | solution.py:121
  87.9 4.2 %slice_bitcast_fusion.2 = (bf16[2048,1024]{1,0:T(8,128)(2,1)S(1)}, bf16[2048,1024]{1,0:T(8,128)(2,1)S(1)}) fusion(bf16[3,2048,1024]{2,1,0:T(8,128)(2,1)} %all-gather.3.cloned.1.call-done), kind=kLoop, calls=%fused_computation.14 | loop fusion | bytes 16777216 | tf_op jit(solution)/shard_map/squeeze | solution.py:110
  92.1 6.1 %fusion.8 = bf16[640,2048]{1,0:T(8,128)(2,1)S(1)} fusion(bf16[640,2048]{1,0:T(8,128)(2,1)S(1)} %bitcast_convert_fusion, bf16[2048,1024]{1,0:T(8,128)(2,1)S(1)} %get-tuple-element.57, bf16[2048,1024]{1,0:T(8,128)(2,1)S(1)} %get-tuple-element.58), kind=kOutput, calls=%fused_computation.16 | convolution fusion | flops 5386797056 | bytes 13631488 | tf_op jit(solution)/shard_map/dot_general | solution.py:124
  103.9 14.1 %all-gather.5.cloned.1.call-done = bf16[1024,2048]{1,0:T(8,128)(2,1)} async-done(((bf16[1024,256]{1,0:T(8,128)(2,1)}), bf16[1024,2048]{1,0:T(8,128)(2,1)}) %all-gather.5.cloned.1.call-update) | async-done | bytes 4194320 | tf_op jit(solution)/shard_map/all_gather | solution.py:108
  118.0 3.0 %convolution_add_fusion = f32[32,2048]{1,0:T(8,128)S(1)} fusion(bf16[32,1024]{1,0:T(8,128)(2,1)S(1)} %reshape.305, bf16[1024,2048]{1,0:T(8,128)(2,1)} %all-gather.5.cloned.1.call-done, bf16[32,2048]{1,0:T(8,128)(2,1)S(1)} %convolution_convert_fusion), kind=kOutput, calls=%fused_computation.39 | convolution fusion | flops 134348800 | bytes 4653056 | tf_op jit(solution)/shard_map/jvp()/dot_general | solution.py:34
  122.8 6.8 %all-to-all-start.1 = ((bf16[16,32,2176]{2,1,0:T(8,128)(2,1)}), bf16[16,32,2176]{2,1,0:T(8,128)(2,1)S(1)}, u32[]{:S(2)}, u32[]{:S(2)}) async-start(bf16[16,32,2176]{2,1,0:T(8,128)(2,1)} %broadcast_in_dim.97), calls=%async_computation.1 | async-start | bytes 4456448 | tf_op jit(solution)/shard_map/all_to_all | solution.py:148
  131.6 30.2 %all-to-all-done.1 = bf16[16,32,2176]{2,1,0:T(8,128)(2,1)S(1)} async-done(((bf16[16,32,2176]{2,1,0:T(8,128)(2,1)}), bf16[16,32,2176]{2,1,0:T(8,128)(2,1)S(1)}, u32[]{:S(2)}, u32[]{:S(2)}) %all-to-all-start.1) | async-done | bytes 2228256 | tf_op jit(solution)/shard_map/all_to_all | solution.py:148
  164.3 2.6 fusion.24
  177.6 7.4 %fusion.5 = f32[640,1024]{1,0:T(8,128)} fusion(bf16[2048,1024]{1,0:T(8,128)(2,1)} %copy-done.9, bf16[2048,1024]{1,0:T(8,128)(2,1)} %copy-done.8, bf16[640,1024]{0,1:T(8,128)(2,1)} %bitcast.130, bf16[640,1024]{0,1:T(8,128)(2,1)} %bitcast.132), kind=kOutput, calls=%fused_computation.11 | convolution fusion | flops 2697986048 | bytes 13631488 | tf_op jit(solution)/shard_map/dot_general | solution.py:211
  185.1 2.3 reduce-precision_convert_fusion.1
  187.4 5.0 %fusion.34 = bf16[16,51,1024]{2,1,0:T(8,128)(2,1)} fusion(s32[16,51]{1,0:T(8,128)S(1)} %copy-done.21, f32[640,1024]{1,0:T(8,128)} %fusion.5, bf16[32,1024]{1,0:T(8,128)(2,1)S(1)} %get-tuple-element.76, bf16[32,1024]{1,0:T(8,128)(2,1)S(1)} %get-tuple-element.77, bf16[32,1024]{1,0:T(8,128)(2,1)S(1)} %get-tuple-element.75, pred[32,640]{1,0:T(32,128)(4,1)S(1)} %copy-done.19), kind=kOutput, calls=%fused_computation.51 | convolution fusion | flops 1198757888 | bytes 4512960 | tf_op jit(solution)/shard_map/sop,sd->opd/dot_general | solution.py:230
  192.5 5.1 %all-to-all-start.3 = ((bf16[16,51,1024]{2,1,0:T(8,128)(2,1)}), bf16[16,51,1024]{2,1,0:T(8,128)(2,1)S(1)}, u32[]{:S(2)}, u32[]{:S(2)}) async-start(bf16[16,51,1024]{2,1,0:T(8,128)(2,1)} %fusion.34), calls=%async_computation.3 | async-start | bytes 3670016 | tf_op jit(solution)/shard_map/all_to_all | solution.py:233
  197.6 2.5 reduce-precision_convert_fusion.3
  200.1 6.7 %fusion.2 = f32[640,1024]{1,0:T(8,128)} fusion(bf16[2048,1024]{1,0:T(8,128)(2,1)} %copy-done.9, bf16[2048,1024]{1,0:T(8,128)(2,1)} %copy-done.8, bf16[640,1024]{0,1:T(8,128)(2,1)S(1)} %bitcast.131, bf16[640,1024]{0,1:T(8,128)(2,1)S(1)} %bitcast.133), kind=kOutput, calls=%fused_computation.9 | convolution fusion | flops 2697986048 | bytes 13631488 | tf_op jit(solution)/shard_map/dot_general | solution.py:211
  206.8 5.0 %fusion.33 = bf16[16,51,1024]{2,1,0:T(8,128)(2,1)} fusion(s32[16,51]{1,0:T(8,128)S(1)} %copy-done.21, f32[640,1024]{1,0:T(8,128)} %fusion.2, bf16[32,1024]{1,0:T(8,128)(2,1)S(1)} %get-tuple-element.73, bf16[32,1024]{1,0:T(8,128)(2,1)S(1)} %get-tuple-element.74, bf16[32,1024]{1,0:T(8,128)(2,1)S(1)} %get-tuple-element.72, pred[32,640]{1,0:T(32,128)(4,1)S(1)} %copy-done.19), kind=kOutput, calls=%fused_computation.50 | convolution fusion | flops 1198757888 | bytes 4512960 | tf_op jit(solution)/shard_map/sop,sd->opd/dot_general | solution.py:230
  211.8 11.8 %all-to-all-done.3 = bf16[16,51,1024]{2,1,0:T(8,128)(2,1)S(1)} async-done(((bf16[16,51,1024]{2,1,0:T(8,128)(2,1)}), bf16[16,51,1024]{2,1,0:T(8,128)(2,1)S(1)}, u32[]{:S(2)}, u32[]{:S(2)}) %all-to-all-start.3) | async-done | bytes 1671200 | tf_op jit(solution)/shard_map/all_to_all | solution.py:233
  223.6 4.4 %all-to-all-start.2 = ((bf16[16,51,1024]{2,1,0:T(8,128)(2,1)}), bf16[16,51,1024]{2,1,0:T(8,128)(2,1)}, u32[]{:S(2)}, u32[]{:S(2)}) async-start(bf16[16,51,1024]{2,1,0:T(8,128)(2,1)} %fusion.33), calls=%async_computation.2 | async-start | bytes 3670016 | tf_op jit(solution)/shard_map/all_to_all | solution.py:233
  228.6 2.7 %bitcast_convert_fusion.1 = bf16[640,1024]{1,0:T(8,128)(2,1)} fusion(bf16[16,51,1024]{2,1,0:T(8,128)(2,1)S(1)} %all-to-all-done.3, pred[16,50,640]{2,1,0:T(8,128)(4,1)S(1)} %broadcast_compare_fusion), kind=kOutput, calls=%fused_computation.30 | convolution fusion | flops 1070202880 | bytes 3493888 | tf_op jit(solution)/shard_map/opk,opd->kd/dot_general | solution.py:235
  231.3 19.9 %all-to-all-done.2 = bf16[16,51,1024]{2,1,0:T(8,128)(2,1)} async-done(((bf16[16,51,1024]{2,1,0:T(8,128)(2,1)}), bf16[16,51,1024]{2,1,0:T(8,128)(2,1)}, u32[]{:S(2)}, u32[]{:S(2)}) %all-to-all-start.2) | async-done | bytes 1671200 | tf_op jit(solution)/shard_map/all_to_all | solution.py:233
  251.2 3.3 %bitcast_convert_fusion.2 = bf16[640,1024]{1,0:T(8,128)(2,1)S(1)} fusion(bf16[16,51,1024]{2,1,0:T(8,128)(2,1)} %all-to-all-done.2, pred[16,50,640]{2,1,0:T(8,128)(4,1)S(1)} %broadcast_compare_fusion), kind=kOutput, calls=%fused_computation.31 | convolution fusion | flops 1070202880 | bytes 3493888 | tf_op jit(solution)/shard_map/opk,opd->kd/dot_general | solution.py:235
  (138 shorter events, 37.8 us)
Async XLA Ops:
  7.2 8.4 %copy-start = (bf16[640,2048]{1,0:T(8,128)(2,1)S(1)}, bf16[640,2048]{1,0:T(8,128)(2,1)}, u32[]{:S(2)}) copy-start(bf16[640,2048]{1,0:T(8,128)(2,1)} %param.17) | copy-start | bytes 7864324
  7.2 77.6 %all-gather.3.cloned.1.call-start = ((), (), s32[]{:S(2)}) async-start(), calls=%async_computation.4 | async-start | bytes 14155776 | tf_op jit(solution)/shard_map/all_gather | solution.py:107
  20.0 8.1 %copy-start.23 = (f32[16]{0:T(128)S(1)}, f32[16]{0:T(128)}, u32[]{:S(2)}) copy-start(f32[16]{0:T(128)} %param.25) | copy-start | bytes 196
  20.0 8.2 %copy-start.22 = (s32[1,640]{1,0:T(1,128)S(1)}, s32[1,640]{1,0:T(1,128)}, u32[]{:S(2)}) copy-start(s32[1,640]{1,0:T(1,128)} %param.19) | copy-start | bytes 7684
  20.0 10.6 %copy-start.24 = (s32[16]{0:T(128)S(1)}, s32[16]{0:T(128)}, u32[]{:S(2)}) copy-start(s32[16]{0:T(128)} %param.23) | copy-start | bytes 196
  20.0 10.6 %copy-start.25 = (s32[16]{0:T(128)S(1)}, s32[16]{0:T(128)}, u32[]{:S(2)}) copy-start(s32[16]{0:T(128)} %param.22) | copy-start | bytes 196
  20.0 57.8 %all-to-all-start = ((bf16[16,51,2048]{2,1,0:T(8,128)(2,1)}), bf16[16,51,2048]{2,1,0:T(8,128)(2,1)}, u32[]{:S(2)}, u32[]{:S(2)}) async-start(bf16[16,51,2048]{2,1,0:T(8,128)(2,1)} %add_convert_fusion), calls=%async_computation | async-start | bytes 7340032 | tf_op jit(solution)/shard_map/all_to_all | solution.py:93
  27.3 90.7 %all-gather.5.cloned.1.call-start = ((), (), s32[]{:S(2)}) async-start(), calls=%async_computation.5 | async-start | bytes 4718592 | tf_op jit(solution)/shard_map/all_gather | solution.py:108
  30.6 48.4 %copy-start.17 = (bf16[32,128]{1,0:T(8,128)(2,1)}, bf16[32,128]{1,0:T(8,128)(2,1)S(1)}, u32[]{:S(2)}) copy-start(bf16[32,128]{1,0:T(8,128)(2,1)S(1)} %scatter.19) | copy-start | bytes 24580
  79.0 5.1 %copy-start.20 = (s32[16,51]{1,0:T(8,128)}, s32[16,51]{1,0:T(8,128)S(1)}, u32[]{:S(2)}) copy-start(s32[16,51]{1,0:T(8,128)S(1)} %concatenate.68) | copy-start | bytes 9796
  87.9 12.8 %copy-start.14 = (bf16[32,16,64]{2,1,0:T(8,128)(2,1)}, bf16[32,16,64]{2,1,0:T(8,128)(2,1)S(1)}, u32[]{:S(2)}) copy-start(bf16[32,16,64]{2,1,0:T(8,128)(2,1)S(1)} %reshape.303) | copy-start | bytes 196612
  92.1 6.1 %copy-start.8 = (bf16[2048,1024]{1,0:T(8,128)(2,1)}, bf16[2048,1024]{1,0:T(8,128)(2,1)S(1)}, u32[]{:S(2)}) copy-start(bf16[2048,1024]{1,0:T(8,128)(2,1)S(1)} %get-tuple-element.57) | copy-start | bytes 12582916
  92.1 6.1 %copy-start.9 = (bf16[2048,1024]{1,0:T(8,128)(2,1)}, bf16[2048,1024]{1,0:T(8,128)(2,1)S(1)}, u32[]{:S(2)}) copy-start(bf16[2048,1024]{1,0:T(8,128)(2,1)S(1)} %get-tuple-element.58) | copy-start | bytes 12582916
  100.7 2.9 %copy-start.5 = (bf16[640,1024]{0,1:T(8,128)(2,1)}, bf16[640,1024]{0,1:T(8,128)(2,1)S(1)}, u32[]{:S(2)}) copy-start(bf16[640,1024]{0,1:T(8,128)(2,1)S(1)} %copy.80) | copy-start | bytes 3932164
  103.9 17.4 %copy-start.18 = (bf16[32,128]{1,0:T(8,128)(2,1)S(1)}, bf16[32,128]{1,0:T(8,128)(2,1)}, u32[]{:S(2)}) copy-start(bf16[32,128]{1,0:T(8,128)(2,1)} %copy-done.17) | copy-start | bytes 24580
  122.8 39.0 %all-to-all-start.1 = ((bf16[16,32,2176]{2,1,0:T(8,128)(2,1)}), bf16[16,32,2176]{2,1,0:T(8,128)(2,1)S(1)}, u32[]{:S(2)}, u32[]{:S(2)}) async-start(bf16[16,32,2176]{2,1,0:T(8,128)(2,1)} %broadcast_in_dim.97), calls=%async_computation.1 | async-start | bytes 4456448 | tf_op jit(solution)/shard_map/all_to_all | solution.py:148
  164.3 2.6 copy-start.12
  167.6 3.7 %copy-start.4 = (f32[16,32,640]{2,1,0:T(8,128)S(1)}, f32[16,32,640]{2,1,0:T(8,128)}, u32[]{:S(2)}) copy-start(f32[16,32,640]{2,1,0:T(8,128)} %copy-done.3) | copy-start | bytes 3932164
  170.5 2.6 copy-start.6
  192.5 31.1 %all-to-all-start.3 = ((bf16[16,51,1024]{2,1,0:T(8,128)(2,1)}), bf16[16,51,1024]{2,1,0:T(8,128)(2,1)S(1)}, u32[]{:S(2)}, u32[]{:S(2)}) async-start(bf16[16,51,1024]{2,1,0:T(8,128)(2,1)} %fusion.34), calls=%async_computation.3 | async-start | bytes 3670016 | tf_op jit(solution)/shard_map/all_to_all | solution.py:233
  197.6 2.5 copy-start.26
  223.6 27.6 %all-to-all-start.2 = ((bf16[16,51,1024]{2,1,0:T(8,128)(2,1)}), bf16[16,51,1024]{2,1,0:T(8,128)(2,1)}, u32[]{:S(2)}, u32[]{:S(2)}) async-start(bf16[16,51,1024]{2,1,0:T(8,128)(2,1)} %fusion.33), calls=%async_computation.2 | async-start | bytes 3670016 | tf_op jit(solution)/shard_map/all_to_all | solution.py:233
  251.2 3.3 %copy-start.10 = (bf16[640,1024]{1,0:T(8,128)(2,1)S(1)}, bf16[640,1024]{1,0:T(8,128)(2,1)}, u32[]{:S(2)}) copy-start(bf16[640,1024]{1,0:T(8,128)(2,1)} %bitcast_convert_fusion.1) | copy-start | bytes 3932164
  251.2 5.0 %copy-start.1 = (bf16[640,2048]{1,0:T(8,128)(2,1)S(1)}, bf16[640,2048]{1,0:T(8,128)(2,1)}, u32[]{:S(2)}) copy-start(bf16[640,2048]{1,0:T(8,128)(2,1)} %param.17) | copy-start | bytes 7864324
  (10 other events, 19.1 us)
Sparse Core Ops, SparseCore 0:
  9.7 69.9 all-gather.2
  81.4 36.5 all-gather.4

commit v15 on v14

--- a/solution.py
+++ b/solution.py
@@ -169,15 +169,14 @@
     own_rows = first_pair + jnp.arange(pair_count)
     own_mask = (jnp.arange(pair_total)[None, :] == own_rows[:, None]).astype(jnp.float32)
     loss_all = 0.5 * (row_lse - diag_logit) + 0.5 * (col_lse - diag_logit)
-    pair_loss = lax.dynamic_slice(loss_all, (first_pair,), (pair_count,))
+    pair_loss = jnp.dot(own_mask, loss_all, precision=lax.Precision.HIGHEST)
     prob_rows = jnp.exp(logits - row_lse[:, None])
     prob_cols = jnp.exp(logits - col_lse[None, :])
     coef = 0.5 * all_weight[:, None] * (prob_rows - eye_mat) + 0.5 * (
         prob_cols - eye_mat
     ) * all_weight[None, :]
-    coef_rows = lax.dynamic_slice(coef, (first_pair, 0), (pair_count, pair_total))
-    coef_cols = lax.dynamic_slice(coef, (0, first_pair), (pair_total, pair_count)).T
-
+    coef_rows = jnp.dot(own_mask, coef, precision=lax.Precision.HIGHEST)
+    coef_cols = jnp.dot(own_mask, coef.T, precision=lax.Precision.HIGHEST)
     def exact_product(coef_part, emb):
         piece_hi = lax.reduce_precision(coef_part, exponent_bits=8, mantissa_bits=7)
         rest = coef_part - piece_hi

time: 264 us -> 261 us (0.989)
  no operation moved by 1% of the time
where the time goes in v15:
time: 261 us; the launch traced here: 260 us
  waiting for transfers between devices  124 us (48%)
  matrix products  68.4 us (26%)
  starting transfers between devices  23.9 us (9%)
  local copies, waits for them, and re-layouts  16.8 us (6%)
  between operations  15.3 us (6%)
  other arithmetic  11.9 us (5%)
    all_to_all x1, waiting for transfers between devices, body(): lax.all_to_all(send_rows, 'dp', split_axis=0, concat_axis=0, tiled=True)  46.8 us
    all_to_all x2, waiting for transfers between devices, body(): lax.all_to_all(back_rows, 'dp', split_axis=0, concat_axis=0, tiled=True)  31.6 us
    all_to_all x1, waiting for transfers between devices, body(): lax.all_to_all(jnp.broadcast_to(both_emb[None], (dp_count,) + both_emb.sh...  30.2 us
    all_gather x1, waiting for transfers between devices, body(): lax.all_gather(out_weight, 'fsdp', axis=1, tiled=True)  14.1 us
    dot_general x2, matrix products, body(): lax.dot_general(key_value_ct, kv_full[cols], (((1,), (1,)), ((), ())), pr...  14.1 us
    dot_general x2, matrix products, body(): jnp.einsum('sop,sd->opd', recv_onehot, slot_gradient, preferred_element_t...  10 us
    all_to_all x2, starting transfers between devices, body(): lax.all_to_all(back_rows, 'dp', split_axis=0, concat_axis=0, tiled=True)  9.51 us
    all_to_all x1, starting transfers between devices, body(): lax.all_to_all(send_rows, 'dp', split_axis=0, concat_axis=0, tiled=True)  7.3 us
  transfers between devices with their start and end apart: 6, of which 5 were waited for; matrix products, arithmetic and copies ran while one was open for 22% of the time, Pallas kernels for 0%

profile of v15, /device:TPU:0, one launch (start us, length us, event | category | flops | bytes accessed | tf_op | source)
XLA Modules:
  0.0 260.3 jit_solution(5574978318901065691)
XLA Ops:
  15.5 4.5 %add_convert_fusion = bf16[16,51,2048]{2,1,0:T(8,128)(2,1)} fusion(f32[16,1,2048]{2,1,0:T(1,128)S(1)} %scatter.15, bf16[640,2048]{1,0:T(8,128)(2,1)S(1)} %copy-done, pred[16,50,640]{2,1,0:T(8,128)(4,1)S(1)} %broadcast_compare_fusion), kind=kOutput, calls=%fused_computation.6 | convolution fusion | flops 2142437376 | bytes 6606848 | tf_op jit(solution)/shard_map/opk,kd->opd/dot_general | solution.py:90
  20.0 7.3 %all-to-all-start = ((bf16[16,51,2048]{2,1,0:T(8,128)(2,1)}), bf16[16,51,2048]{2,1,0:T(8,128)(2,1)}, u32[]{:S(2)}, u32[]{:S(2)}) async-start(bf16[16,51,2048]{2,1,0:T(8,128)(2,1)} %add_convert_fusion), calls=%async_computation | async-start | bytes 7340032 | tf_op jit(solution)/shard_map/all_to_all | solution.py:93
  31.0 46.8 %all-to-all-done = bf16[16,51,2048]{2,1,0:T(8,128)(2,1)} async-done(((bf16[16,51,2048]{2,1,0:T(8,128)(2,1)}), bf16[16,51,2048]{2,1,0:T(8,128)(2,1)}, u32[]{:S(2)}, u32[]{:S(2)}) %all-to-all-start) | async-done | bytes 3342368 | tf_op jit(solution)/shard_map/all_to_all | solution.py:93
  79.0 5.1 %bitcast_convert_fusion = bf16[640,2048]{1,0:T(8,128)(2,1)S(1)} fusion(bf16[16,51,2048]{2,1,0:T(8,128)(2,1)} %all-to-all-done, s32[16,51]{1,0:T(8,128)S(1)} %concatenate.68), kind=kOutput, calls=%fused_computation.7 | convolution fusion | flops 2140928000 | bytes 5967040 | tf_op jit(solution)/shard_map/sop,opd->sd/dot_general | solution.py:103
  84.7 3.0 %fusion.55 = bf16[32,1024]{1,0:T(8,128)(2,1)S(1)} fusion(bf16[32,2048]{1,0:T(8,128)(2,1)S(1)} %convolution_convert_fusion, bf16[3,2048,1024]{2,1,0:T(8,128)(2,1)} %all-gather.3.cloned.1.call-done), kind=kOutput, calls=%fused_computation.83 | convolution fusion | flops 134250496 | bytes 4390912 | tf_op jit(solution)/shard_map/dot_general | solution.py:121
  87.9 4.2 %slice_bitcast_fusion.2 = (bf16[2048,1024]{1,0:T(8,128)(2,1)S(1)}, bf16[2048,1024]{1,0:T(8,128)(2,1)S(1)}) fusion(bf16[3,2048,1024]{2,1,0:T(8,128)(2,1)} %all-gather.3.cloned.1.call-done), kind=kLoop, calls=%fused_computation.14 | loop fusion | bytes 16777216 | tf_op jit(solution)/shard_map/squeeze | solution.py:110
  92.1 6.1 %fusion.8 = bf16[640,2048]{1,0:T(8,128)(2,1)S(1)} fusion(bf16[640,2048]{1,0:T(8,128)(2,1)S(1)} %bitcast_convert_fusion, bf16[2048,1024]{1,0:T(8,128)(2,1)S(1)} %get-tuple-element.57, bf16[2048,1024]{1,0:T(8,128)(2,1)S(1)} %get-tuple-element.58), kind=kOutput, calls=%fused_computation.16 | convolution fusion | flops 5386797056 | bytes 13631488 | tf_op jit(solution)/shard_map/dot_general | solution.py:124
  101.2 1.8 copy-done.7
  103.9 14.1 %all-gather.5.cloned.1.call-done = bf16[1024,2048]{1,0:T(8,128)(2,1)} async-done(((bf16[1024,256]{1,0:T(8,128)(2,1)}), bf16[1024,2048]{1,0:T(8,128)(2,1)}) %all-gather.5.cloned.1.call-update) | async-done | bytes 4194320 | tf_op jit(solution)/shard_map/all_gather | solution.py:108
  118.0 3.0 %convolution_add_fusion = f32[32,2048]{1,0:T(8,128)S(1)} fusion(bf16[32,1024]{1,0:T(8,128)(2,1)S(1)} %reshape.309, bf16[1024,2048]{1,0:T(8,128)(2,1)} %all-gather.5.cloned.1.call-done, bf16[32,2048]{1,0:T(8,128)(2,1)S(1)} %convolution_convert_fusion), kind=kOutput, calls=%fused_computation.39 | convolution fusion | flops 134348800 | bytes 4653056 | tf_op jit(solution)/shard_map/jvp()/dot_general | solution.py:34
  122.8 6.8 %all-to-all-start.1 = ((bf16[16,32,2176]{2,1,0:T(8,128)(2,1)}), bf16[16,32,2176]{2,1,0:T(8,128)(2,1)S(1)}, u32[]{:S(2)}, u32[]{:S(2)}) async-start(bf16[16,32,2176]{2,1,0:T(8,128)(2,1)} %broadcast_in_dim.99), calls=%async_computation.1 | async-start | bytes 4456448 | tf_op jit(solution)/shard_map/all_to_all | solution.py:148
  131.6 30.2 %all-to-all-done.1 = bf16[16,32,2176]{2,1,0:T(8,128)(2,1)S(1)} async-done(((bf16[16,32,2176]{2,1,0:T(8,128)(2,1)}), bf16[16,32,2176]{2,1,0:T(8,128)(2,1)S(1)}, u32[]{:S(2)}, u32[]{:S(2)}) %all-to-all-start.1) | async-done | bytes 2228256 | tf_op jit(solution)/shard_map/all_to_all | solution.py:148
  174.8 7.4 %fusion.5 = f32[640,1024]{1,0:T(8,128)} fusion(bf16[2048,1024]{1,0:T(8,128)(2,1)} %copy-done.9, bf16[2048,1024]{1,0:T(8,128)(2,1)} %copy-done.8, bf16[640,1024]{0,1:T(8,128)(2,1)} %bitcast.130, bf16[640,1024]{0,1:T(8,128)(2,1)} %bitcast.132), kind=kOutput, calls=%fused_computation.11 | convolution fusion | flops 2697986048 | bytes 13631488 | tf_op jit(solution)/shard_map/dot_general | solution.py:210
  182.3 2.3 reduce-precision_convert_fusion.1
  184.6 5.0 %fusion.34 = bf16[16,51,1024]{2,1,0:T(8,128)(2,1)} fusion(s32[16,51]{1,0:T(8,128)S(1)} %copy-done.18, f32[640,1024]{1,0:T(8,128)} %fusion.5, bf16[32,1024]{1,0:T(8,128)(2,1)S(1)} %get-tuple-element.71, bf16[32,1024]{1,0:T(8,128)(2,1)S(1)} %get-tuple-element.72, bf16[32,1024]{1,0:T(8,128)(2,1)S(1)} %get-tuple-element.70, pred[32,640]{1,0:T(32,128)(4,1)S(1)} %copy-done.16), kind=kOutput, calls=%fused_computation.51 | convolution fusion | flops 1198757888 | bytes 4512960 | tf_op jit(solution)/shard_map/sop,sd->opd/dot_general | solution.py:229
  189.7 5.1 %all-to-all-start.3 = ((bf16[16,51,1024]{2,1,0:T(8,128)(2,1)}), bf16[16,51,1024]{2,1,0:T(8,128)(2,1)S(1)}, u32[]{:S(2)}, u32[]{:S(2)}) async-start(bf16[16,51,1024]{2,1,0:T(8,128)(2,1)} %fusion.34), calls=%async_computation.3 | async-start | bytes 3670016 | tf_op jit(solution)/shard_map/all_to_all | solution.py:232
  194.8 2.5 reduce-precision_convert_fusion.3
  197.3 6.7 %fusion.2 = f32[640,1024]{1,0:T(8,128)} fusion(bf16[2048,1024]{1,0:T(8,128)(2,1)} %copy-done.9, bf16[2048,1024]{1,0:T(8,128)(2,1)} %copy-done.8, bf16[640,1024]{0,1:T(8,128)(2,1)S(1)} %bitcast.131, bf16[640,1024]{0,1:T(8,128)(2,1)S(1)} %bitcast.133), kind=kOutput, calls=%fused_computation.9 | convolution fusion | flops 2697986048 | bytes 13631488 | tf_op jit(solution)/shard_map/dot_general | solution.py:210
  204.0 5.0 %fusion.33 = bf16[16,51,1024]{2,1,0:T(8,128)(2,1)} fusion(s32[16,51]{1,0:T(8,128)S(1)} %copy-done.18, f32[640,1024]{1,0:T(8,128)} %fusion.2, bf16[32,1024]{1,0:T(8,128)(2,1)S(1)} %get-tuple-element.68, bf16[32,1024]{1,0:T(8,128)(2,1)S(1)} %get-tuple-element.69, bf16[32,1024]{1,0:T(8,128)(2,1)S(1)} %get-tuple-element.67, pred[32,640]{1,0:T(32,128)(4,1)S(1)} %copy-done.16), kind=kOutput, calls=%fused_computation.50 | convolution fusion | flops 1198757888 | bytes 4512960 | tf_op jit(solution)/shard_map/sop,sd->opd/dot_general | solution.py:229
  209.0 11.8 %all-to-all-done.3 = bf16[16,51,1024]{2,1,0:T(8,128)(2,1)S(1)} async-done(((bf16[16,51,1024]{2,1,0:T(8,128)(2,1)}), bf16[16,51,1024]{2,1,0:T(8,128)(2,1)S(1)}, u32[]{:S(2)}, u32[]{:S(2)}) %all-to-all-start.3) | async-done | bytes 1671200 | tf_op jit(solution)/shard_map/all_to_all | solution.py:232
  220.8 4.4 %all-to-all-start.2 = ((bf16[16,51,1024]{2,1,0:T(8,128)(2,1)}), bf16[16,51,1024]{2,1,0:T(8,128)(2,1)}, u32[]{:S(2)}, u32[]{:S(2)}) async-start(bf16[16,51,1024]{2,1,0:T(8,128)(2,1)} %fusion.33), calls=%async_computation.2 | async-start | bytes 3670016 | tf_op jit(solution)/shard_map/all_to_all | solution.py:232
  225.9 2.7 %bitcast_convert_fusion.1 = bf16[640,1024]{1,0:T(8,128)(2,1)} fusion(bf16[16,51,1024]{2,1,0:T(8,128)(2,1)S(1)} %all-to-all-done.3, pred[16,50,640]{2,1,0:T(8,128)(4,1)S(1)} %broadcast_compare_fusion), kind=kOutput, calls=%fused_computation.30 | convolution fusion | flops 1070202880 | bytes 3493888 | tf_op jit(solution)/shard_map/opk,opd->kd/dot_general | solution.py:234
  228.6 19.8 %all-to-all-done.2 = bf16[16,51,1024]{2,1,0:T(8,128)(2,1)} async-done(((bf16[16,51,1024]{2,1,0:T(8,128)(2,1)}), bf16[16,51,1024]{2,1,0:T(8,128)(2,1)}, u32[]{:S(2)}, u32[]{:S(2)}) %all-to-all-start.2) | async-done | bytes 1671200 | tf_op jit(solution)/shard_map/all_to_all | solution.py:232
  248.4 3.3 %bitcast_convert_fusion.2 = bf16[640,1024]{1,0:T(8,128)(2,1)S(1)} fusion(bf16[16,51,1024]{2,1,0:T(8,128)(2,1)} %all-to-all-done.2, pred[16,50,640]{2,1,0:T(8,128)(4,1)S(1)} %broadcast_compare_fusion), kind=kOutput, calls=%fused_computation.31 | convolution fusion | flops 1070202880 | bytes 3493888 | tf_op jit(solution)/shard_map/opk,opd->kd/dot_general | solution.py:234
  (133 shorter events, 36.0 us)
Async XLA Ops:
  7.2 8.4 %copy-start = (bf16[640,2048]{1,0:T(8,128)(2,1)S(1)}, bf16[640,2048]{1,0:T(8,128)(2,1)}, u32[]{:S(2)}) copy-start(bf16[640,2048]{1,0:T(8,128)(2,1)} %param.17) | copy-start | bytes 7864324
  7.2 77.6 %all-gather.3.cloned.1.call-start = ((), (), s32[]{:S(2)}) async-start(), calls=%async_computation.4 | async-start | bytes 14155776 | tf_op jit(solution)/shard_map/all_gather | solution.py:107
  20.0 8.1 %copy-start.22 = (f32[16]{0:T(128)S(1)}, f32[16]{0:T(128)}, u32[]{:S(2)}) copy-start(f32[16]{0:T(128)} %param.25) | copy-start | bytes 196
  20.0 8.2 %copy-start.19 = (s32[1,640]{1,0:T(1,128)S(1)}, s32[1,640]{1,0:T(1,128)}, u32[]{:S(2)}) copy-start(s32[1,640]{1,0:T(1,128)} %param.19) | copy-start | bytes 7684
  20.0 10.6 %copy-start.23 = (s32[16]{0:T(128)S(1)}, s32[16]{0:T(128)}, u32[]{:S(2)}) copy-start(s32[16]{0:T(128)} %param.23) | copy-start | bytes 196
  20.0 10.6 %copy-start.24 = (s32[16]{0:T(128)S(1)}, s32[16]{0:T(128)}, u32[]{:S(2)}) copy-start(s32[16]{0:T(128)} %param.22) | copy-start | bytes 196
  20.0 57.8 %all-to-all-start = ((bf16[16,51,2048]{2,1,0:T(8,128)(2,1)}), bf16[16,51,2048]{2,1,0:T(8,128)(2,1)}, u32[]{:S(2)}, u32[]{:S(2)}) async-start(bf16[16,51,2048]{2,1,0:T(8,128)(2,1)} %add_convert_fusion), calls=%async_computation | async-start | bytes 7340032 | tf_op jit(solution)/shard_map/all_to_all | solution.py:93
  27.3 90.7 %all-gather.5.cloned.1.call-start = ((), (), s32[]{:S(2)}) async-start(), calls=%async_computation.5 | async-start | bytes 4718592 | tf_op jit(solution)/shard_map/all_gather | solution.py:108
  30.6 48.4 %copy-start.14 = (bf16[32,128]{1,0:T(8,128)(2,1)}, bf16[32,128]{1,0:T(8,128)(2,1)S(1)}, u32[]{:S(2)}) copy-start(bf16[32,128]{1,0:T(8,128)(2,1)S(1)} %scatter.19) | copy-start | bytes 24580
  79.0 5.1 %copy-start.17 = (s32[16,51]{1,0:T(8,128)}, s32[16,51]{1,0:T(8,128)S(1)}, u32[]{:S(2)}) copy-start(s32[16,51]{1,0:T(8,128)S(1)} %concatenate.68) | copy-start | bytes 9796
  87.9 12.8 %copy-start.11 = (bf16[32,16,64]{2,1,0:T(8,128)(2,1)}, bf16[32,16,64]{2,1,0:T(8,128)(2,1)S(1)}, u32[]{:S(2)}) copy-start(bf16[32,16,64]{2,1,0:T(8,128)(2,1)S(1)} %reshape.307) | copy-start | bytes 196612
  92.1 6.1 %copy-start.8 = (bf16[2048,1024]{1,0:T(8,128)(2,1)}, bf16[2048,1024]{1,0:T(8,128)(2,1)S(1)}, u32[]{:S(2)}) copy-start(bf16[2048,1024]{1,0:T(8,128)(2,1)S(1)} %get-tuple-element.57) | copy-start | bytes 12582916
  92.1 6.1 %copy-start.9 = (bf16[2048,1024]{1,0:T(8,128)(2,1)}, bf16[2048,1024]{1,0:T(8,128)(2,1)S(1)}, u32[]{:S(2)}) copy-start(bf16[2048,1024]{1,0:T(8,128)(2,1)S(1)} %get-tuple-element.58) | copy-start | bytes 12582916
  100.7 2.9 %copy-start.5 = (bf16[640,1024]{0,1:T(8,128)(2,1)}, bf16[640,1024]{0,1:T(8,128)(2,1)S(1)}, u32[]{:S(2)}) copy-start(bf16[640,1024]{0,1:T(8,128)(2,1)S(1)} %copy.43) | copy-start | bytes 3932164
  103.9 17.4 %copy-start.15 = (bf16[32,128]{1,0:T(8,128)(2,1)S(1)}, bf16[32,128]{1,0:T(8,128)(2,1)}, u32[]{:S(2)}) copy-start(bf16[32,128]{1,0:T(8,128)(2,1)} %copy-done.14) | copy-start | bytes 24580
  122.8 39.0 %all-to-all-start.1 = ((bf16[16,32,2176]{2,1,0:T(8,128)(2,1)}), bf16[16,32,2176]{2,1,0:T(8,128)(2,1)S(1)}, u32[]{:S(2)}, u32[]{:S(2)}) async-start(bf16[16,32,2176]{2,1,0:T(8,128)(2,1)} %broadcast_in_dim.99), calls=%async_computation.1 | async-start | bytes 4456448 | tf_op jit(solution)/shard_map/all_to_all | solution.py:148
  130.3 33.1 %copy-start.20 = (s32[16]{0:T(128)}, s32[16]{0:T(128)S(1)}, u32[]{:S(2)}) copy-start(s32[16]{0:T(128)S(1)} %iota_add_fusion) | copy-start | bytes 196
  164.8 3.7 %copy-start.4 = (f32[16,32,640]{2,1,0:T(8,128)S(1)}, f32[16,32,640]{2,1,0:T(8,128)}, u32[]{:S(2)}) copy-start(f32[16,32,640]{2,1,0:T(8,128)} %copy-done.3) | copy-start | bytes 3932164
  167.7 2.6 copy-start.6
  189.7 31.1 %all-to-all-start.3 = ((bf16[16,51,1024]{2,1,0:T(8,128)(2,1)}), bf16[16,51,1024]{2,1,0:T(8,128)(2,1)S(1)}, u32[]{:S(2)}, u32[]{:S(2)}) async-start(bf16[16,51,1024]{2,1,0:T(8,128)(2,1)} %fusion.34), calls=%async_computation.3 | async-start | bytes 3670016 | tf_op jit(solution)/shard_map/all_to_all | solution.py:232
  209.0 16.2 %copy-start.21 = (s32[16]{0:T(128)S(1)}, s32[16]{0:T(128)}, u32[]{:S(2)}) copy-start(s32[16]{0:T(128)} %copy-done.20) | copy-start | bytes 196
  220.8 27.6 %all-to-all-start.2 = ((bf16[16,51,1024]{2,1,0:T(8,128)(2,1)}), bf16[16,51,1024]{2,1,0:T(8,128)(2,1)}, u32[]{:S(2)}, u32[]{:S(2)}) async-start(bf16[16,51,1024]{2,1,0:T(8,128)(2,1)} %fusion.33), calls=%async_computation.2 | async-start | bytes 3670016 | tf_op jit(solution)/shard_map/all_to_all | solution.py:232
  248.4 3.3 %copy-start.10 = (bf16[640,1024]{1,0:T(8,128)(2,1)S(1)}, bf16[640,1024]{1,0:T(8,128)(2,1)}, u32[]{:S(2)}) copy-start(bf16[640,1024]{1,0:T(8,128)(2,1)} %bitcast_convert_fusion.1) | copy-start | bytes 3932164
  248.4 5.0 %copy-start.1 = (bf16[640,2048]{1,0:T(8,128)(2,1)S(1)}, bf16[640,2048]{1,0:T(8,128)(2,1)}, u32[]{:S(2)}) copy-start(bf16[640,2048]{1,0:T(8,128)(2,1)} %param.17) | copy-start | bytes 7864324
  (9 other events, 19.3 us)
Sparse Core Ops, SparseCore 0:
  9.7 69.9 all-gather.2
  81.4 36.5 all-gather.4
